TPU v7x, 32 devices: a whole 2x2x4 slice. The times are simulated.
32 devices in a mesh: groups: 2 (over x), seq: 16 (over z, y, core).
Axes of the slice: x: 2, y: 2, z: 4, core: 2. Of those that a mesh axis runs over, the one named last changes fastest.
Arguments:
- query_feats: bfloat16 [16384, 2560], P(('groups', 'seq')), parts along dimension 0, may hold values from -10 to 10
- key_feats: bfloat16 [16384, 2560], P(('groups', 'seq')), parts along dimension 0, may hold values from -10 to 10
- value_feats: bfloat16 [16384, 2560], P(('groups', 'seq')), parts along dimension 0, may hold values from -6 to 6
- owner_map: int32 [256], P('groups'), parts along dimension 0, may hold values from 0 to 15, as said below
- pattern: int32 [256, 23], P('groups'), parts along dimension 0, may hold values from 0 to 127, as said below
Outputs:
- attended: bfloat16 [16384, 2560], P(('groups', 'seq')), parts along dimension 0
- log_sums: float32 [32, 8, 1280], P(('groups', 'seq')), parts along dimension 0
There are 2 independent parts, one for each index of `groups`. A program takes and returns all parts, laid end to end along the dimension named above; each array names one. Nothing has to cross between parts.
Inputs may be any that keep to these rules, and one draw needn't show every extreme that they name: `owner_map`: each device owns exactly 8 tiles. In every block of 32 consecutive tile numbers each device owns at least one tile and at most 2, and some device owns exactly 2. `pattern`: row t holds 23 different tiles: all 8 tiles owned by the owner of tile t, and 15 tiles owned by other devices. Over all query tiles owned by one device, the listed tiles of other devices are exactly one tile of each other device; at most 4 of them lie in one block of 32 consecutive tile numbers, and exactly 4 in every such block but one.
All inputs are finite; a program needn't handle non-finite values.
Results may differ from a plain program's by a relative error of at most 0.005.
Values may be sent and summed in bfloat16 or wider, within the bound.
No kernel may reach another device: no remote copies, remote signals or barrier semaphores. Data moves between devices by JAX's collectives and lax.ppermute only.
A program may use at most 192 MiB of HBM per device.

v0:
```python
import jax
import jax.numpy as jnp
from jax import lax
from jax.sharding import PartitionSpec as P

HEADS = 20
HEAD_DIM = 128
WIDTH = 64
FRAMES = 16


masked_score = -1e30


def frame_pieces(rows_in, strips):
    channels = rows_in.shape[1]
    shaped = rows_in.reshape(strips, 4, WIDTH // 4, 4, channels)
    return shaped.transpose(0, 2, 1, 3, 4).reshape(strips * (WIDTH // 4), 16, channels)


def frame_rows(pieces, strips):
    channels = pieces.shape[2]
    shaped = pieces.reshape(strips, WIDTH // 4, 4, 4, channels)
    return shaped.transpose(0, 2, 1, 3, 4).reshape(strips * 4 * WIDTH, channels)


def owner_tables(owner_map, group_size, piece_count):
    tile_count = owner_map.shape[0]
    devices = jnp.arange(group_size, dtype=jnp.int32)
    onehot = (owner_map[:, None] == devices[None, :]).astype(jnp.int32)
    running = jnp.cumsum(onehot, axis=0)
    own_rank = jnp.sum(onehot * running, axis=1) - 1
    by_class = owner_map.reshape(tile_count // piece_count, piece_count)
    local_iota = jnp.arange(piece_count, dtype=jnp.int32)
    earlier = (by_class[:, :, None] == by_class[:, None, :]) & (
        local_iota[None, None, :] < local_iota[None, :, None]
    )
    class_rank = jnp.sum(earlier.astype(jnp.int32), axis=2).reshape(tile_count)
    return (own_rank, class_rank)


def owned_tiles(owner_map, own_rank, device, own_count):
    tile_iota = jnp.arange(owner_map.shape[0], dtype=jnp.int32)
    slot_iota = jnp.arange(own_count, dtype=jnp.int32)
    match_rows = (owner_map[None, :] == device) & (own_rank[None, :] == slot_iota[:, None])
    return jnp.sum(jnp.where(match_rows, tile_iota[None, :], 0), axis=1)


def request_table(owner_map, pattern, group_size):
    devices = jnp.arange(group_size, dtype=jnp.int32)
    entry_owner = jnp.take(owner_map, pattern)
    foreign = entry_owner != owner_map[:, None]
    entry_hit = (entry_owner[:, :, None] == devices[None, None, :]) & foreign[:, :, None]
    per_tile = jnp.max(jnp.where(entry_hit, pattern[:, :, None], -1), axis=1)
    per_user = owner_map[None, :] == devices[:, None]
    return jnp.max(jnp.where(per_user[:, :, None], per_tile[None, :, :], -1), axis=1)


def supplier_of(tile_class, frame_slice, frame_devs):
    return (4 * (tile_class // frame_devs) + frame_slice) * frame_devs + tile_class % frame_devs


def expand_mask(block_mask):
    query_tiles = block_mask.shape[0]
    key_tiles = block_mask.shape[1]
    wide = jnp.broadcast_to(block_mask[:, None, :, None], (query_tiles, 64, key_tiles, 64))
    return wide.reshape(query_tiles * 64, key_tiles * 64)


def head_part(matrix, offset):
    return lax.dynamic_slice_in_dim(matrix, offset, HEAD_DIM, 1)


def head_scores(query_head, key_rows, offset, mask):
    key_head = head_part(key_rows, offset)
    scores = lax.dot_general(
        query_head, key_head, (((1,), (1,)), ((), ())), preferred_element_type=jnp.float32
    ) * HEAD_DIM ** (-0.5)
    return jnp.where(mask, scores, masked_score)


def attend_pooled(own_query, pool_key, pool_value, mask):

    def one_head(head_index):
        offset = head_index * HEAD_DIM
        scores = head_scores(head_part(own_query, offset), pool_key, offset, mask)
        row_max = jnp.max(scores, axis=1, keepdims=True)
        log_total = row_max + jnp.log(jnp.sum(jnp.exp(scores - row_max), axis=1, keepdims=True))
        weights = jnp.exp(scores - log_total).astype(jnp.bfloat16)
        mixed_rows = jnp.dot(
            weights, head_part(pool_value, offset), preferred_element_type=jnp.float32
        )
        return (mixed_rows.astype(jnp.bfloat16), log_total[:, 0])

    return lax.map(one_head, jnp.arange(HEADS, dtype=jnp.int32))


def shards(query_feats, key_feats, value_feats, owner_map, pattern):
    group_size = lax.axis_size("seq")
    device = lax.axis_index("seq")
    channels = query_feats.shape[1]
    strips = query_feats.shape[0] // (4 * WIDTH)
    piece_count = strips * (WIDTH // 4)
    tile_count = owner_map.shape[0]
    own_count = tile_count // group_size
    capacity = (piece_count + group_size - 1) // group_size
    frame_devs = group_size // FRAMES
    devices = jnp.arange(group_size, dtype=jnp.int32)
    local_iota = jnp.arange(piece_count, dtype=jnp.int32)
    cap_iota = jnp.arange(capacity, dtype=jnp.int32)
    slice_iota = jnp.arange(4, dtype=jnp.int32)
    own_rank, class_rank = owner_tables(owner_map, group_size, piece_count)
    my_frame = device // frame_devs
    my_class = my_frame // 4 * frame_devs + device % frame_devs
    my_tiles = my_class * piece_count + local_iota
    my_owner = jnp.take(owner_map, my_tiles)
    my_slot = jnp.take(class_rank, my_tiles)
    send_hit = (my_owner[None, None, :] == devices[:, None, None]) & (
        my_slot[None, None, :] == cap_iota[None, :, None]
    )
    send_index = jnp.sum(jnp.where(send_hit, local_iota[None, None, :], 0), axis=2).reshape(-1)
    query_pieces = frame_pieces(query_feats, strips)
    key_pieces = frame_pieces(key_feats, strips)
    value_pieces = frame_pieces(value_feats, strips)
    sent_query = jnp.take(query_pieces, send_index, axis=0).reshape(
        group_size, capacity, 16, channels
    )
    sent_key = jnp.take(key_pieces, send_index, axis=0).reshape(group_size, capacity, 16, channels)
    sent_value = jnp.take(value_pieces, send_index, axis=0).reshape(
        group_size, capacity, 16, channels
    )
    got_query, got_key, got_value = (
        lax.all_to_all(sent_query, "seq", split_axis=0, concat_axis=0, tiled=True),
        lax.all_to_all(sent_key, "seq", split_axis=0, concat_axis=0, tiled=True),
        lax.all_to_all(sent_value, "seq", split_axis=0, concat_axis=0, tiled=True),
    )
    own_ids = owned_tiles(owner_map, own_rank, device, own_count)
    own_class = own_ids // piece_count
    own_slot = jnp.take(class_rank, own_ids)
    gather_rows = (
        supplier_of(own_class[:, None], slice_iota[None, :], frame_devs) * capacity
        + own_slot[:, None]
    ).reshape(-1)
    own_query = jnp.take(
        got_query.reshape(group_size * capacity, 16, channels), gather_rows, axis=0
    ).reshape(own_count * 64, channels)
    own_key = jnp.take(
        got_key.reshape(group_size * capacity, 16, channels), gather_rows, axis=0
    ).reshape(own_count * 64, channels)
    own_value = jnp.take(
        got_value.reshape(group_size * capacity, 16, channels), gather_rows, axis=0
    ).reshape(own_count * 64, channels)
    requests = request_table(owner_map, pattern, group_size)
    far_ids = jnp.take(requests, device, axis=0)
    asked_tiles = jnp.take(requests, device, axis=1)
    serve_index = jnp.take(own_rank, jnp.maximum(asked_tiles, 0))
    out_key = jnp.take(own_key.reshape(own_count, 64, channels), serve_index, axis=0)
    out_value = jnp.take(own_value.reshape(own_count, 64, channels), serve_index, axis=0)
    far_key, far_value = (
        lax.all_to_all(out_key, "seq", split_axis=0, concat_axis=0, tiled=True),
        lax.all_to_all(out_value, "seq", split_axis=0, concat_axis=0, tiled=True),
    )
    listed = jnp.take(pattern, own_ids, axis=0)
    near_mask = expand_mask(jnp.any(listed[:, :, None] == own_ids[None, None, :], axis=1))
    far_mask = expand_mask(jnp.any(listed[:, :, None] == far_ids[None, None, :], axis=1))
    far_key_rows = far_key.reshape(group_size * 64, channels)
    far_value_rows = far_value.reshape(group_size * 64, channels)
    pool_key = jnp.concatenate([own_key, far_key_rows], axis=0)
    pool_value = jnp.concatenate([own_value, far_value_rows], axis=0)
    pool_mask = jnp.concatenate([near_mask, far_mask], axis=1)
    head_out, head_logs = attend_pooled(own_query, pool_key, pool_value, pool_mask)
    mixed_rows = head_out.transpose(1, 0, 2).reshape(own_count * 64, channels)
    log_sums = (
        head_logs.reshape(HEADS, own_count, 64).transpose(1, 0, 2).reshape(1, own_count, HEADS * 64)
    )
    out_pieces = mixed_rows.reshape(own_count * 4, 16, channels)
    dest_frame = devices // frame_devs
    dest_class = dest_frame // 4 * frame_devs + devices % frame_devs
    dest_slice = dest_frame % 4
    own_iota = jnp.arange(own_count, dtype=jnp.int32)
    back_hit = (own_class[None, None, :] == dest_class[:, None, None]) & (
        own_slot[None, None, :] == cap_iota[None, :, None]
    )
    back_index = jnp.sum(
        jnp.where(back_hit, own_iota[None, None, :] * 4 + dest_slice[:, None, None], 0), axis=2
    ).reshape(-1)
    back_sent = jnp.take(out_pieces, back_index, axis=0).reshape(group_size, capacity, 16, channels)
    returned = lax.all_to_all(back_sent, "seq", split_axis=0, concat_axis=0, tiled=True)
    place_rows = my_owner * capacity + my_slot
    placed = jnp.take(returned.reshape(group_size * capacity, 16, channels), place_rows, axis=0)
    attended = frame_rows(placed, strips)
    return (attended, log_sums)


def solution(mesh):
    placed = (
        P(("groups", "seq"), None),
        P(("groups", "seq"), None),
        P(("groups", "seq"), None),
        P("groups"),
        P("groups", None),
    )
    return jax.shard_map(
        shards,
        mesh=mesh,
        in_specs=placed,
        out_specs=(P(("groups", "seq"), None), P(("groups", "seq"), None, None)),
        check_vma=False,
    )
```

profile of v0, /device:TPU:13, one launch (start us, length us, event | category | flops | bytes accessed | tf_op | source)
XLA Modules:
  0.0 715.2 jit_solution(2850382932839869369)
XLA Ops:
  7.9 4.3 reshape.491
  14.2 5.5 reshape.498
  19.8 2.3 copy.56
  22.0 2.9 copy.57
  25.0 2.2 gather_fusion.6
  27.2 4.0 gather_fusion.8
  31.2 4.3 reshape.506
  37.5 2.2 gather_fusion.11
  39.7 5.6 broadcast_select_fusion.7
  45.3 65.0 %all_to_all.30 = bf16[16,2,16,2560]{3,2,1,0:T(8,128)(2,1)} all-to-all(bf16[16,2,16,2560]{3,2,1,0:T(8,128)(2,1)S(1)} %bitcast.69), channel_id=1, replica_groups=mesh['groups'=2,'seq'=16] {'seq'}, dimensions={0} | all-to-all | bytes 5242880 | tf_op jit(solution)/shard_map/all_to_all | solution.py:133
  110.2 63.6 %all_to_all.31 = bf16[16,2,16,2560]{3,2,1,0:T(8,128)(2,1)} all-to-all(bf16[16,2,16,2560]{3,2,1,0:T(8,128)(2,1)S(1)} %bitcast.68), channel_id=1, replica_groups=mesh['groups'=2,'seq'=16] {'seq'}, dimensions={0} | all-to-all | bytes 5242880 | tf_op jit(solution)/shard_map/all_to_all | solution.py:134
  173.8 5.3 all-to-all-start.3
  179.6 16.9 %gather_fusion.1 = s32[2944]{0:T(1024)S(1)} fusion(s32[128]{0:T(128)S(1)} %copy-done, s32[3072]{0:T(1024)S(1)} %pad_clamp_fusion), kind=kCustom, calls=%fused_computation.13 | custom fusion | bytes 35328 | tf_op jit(solution)/shard_map/jit(_take)/gather | solution.py:51
  198.4 3.9 gather_fusion.7
  202.3 3.9 gather_fusion.9
  206.2 31.6 %all-to-all-done.3 = bf16[16,2,16,2560]{3,2,1,0:T(8,128)(2,1)S(1)} async-done(((bf16[16,2,16,2560]{3,2,1,0:T(8,128)(2,1)}), bf16[16,2,16,2560]{3,2,1,0:T(8,128)(2,1)S(1)}, u32[]{:S(2)}, u32[]{:S(2)}) %all-to-all-start.3) | async-done | bytes 2621472 | tf_op jit(solution)/shard_map/all_to_all | solution.py:135
  237.8 2.2 gather_fusion.12
  240.0 6.3 broadcast_select_fusion.4
  246.3 3.2 gather_fusion.10
  249.5 4.9 gather_fusion.13
  254.5 9.1 %broadcast_select_fusion = (bf16[16,64,2560]{2,1,0:T(8,128)(2,1)}, bf16[16,64,2560]{2,1,0:T(8,128)(2,1)}) fusion(bf16[16,64,2560]{2,1,0:T(8,128)(2,1)} %gather_fusion.13, pred[16]{0:T(512)(128)(4,1)S(1)} %get-tuple-element.92, bf16[16,64,2560]{2,1,0:T(8,128)(2,1)} %gather_fusion.10), kind=kLoop, calls=%fused_computation.33 | loop fusion | flops 5242880 | bytes 20971536 | tf_op jit(solution)/shard_map/jit(_take)/select_n | solution.py:158
  263.5 119.7 %all_to_all.32 = bf16[16,64,2560]{2,1,0:T(8,128)(2,1)} all-to-all(bf16[16,64,2560]{2,1,0:T(8,128)(2,1)} %get-tuple-element.102), channel_id=1, replica_groups=mesh['groups'=2,'seq'=16] {'seq'}, dimensions={0} | all-to-all | bytes 10485760 | tf_op jit(solution)/shard_map/all_to_all | solution.py:161
  383.3 5.4 all-to-all-start.2
  391.1 4.1 reshape.505
  398.5 6.9 pad_maximum_fusion.1
  405.4 98.2 %all-to-all-done.2 = bf16[16,64,2560]{2,1,0:T(8,128)(2,1)} async-done(((bf16[16,64,2560]{2,1,0:T(8,128)(2,1)}), bf16[16,64,2560]{2,1,0:T(8,128)(2,1)}, u32[]{:S(2)}, u32[]{:S(2)}) %all-to-all-start.2) | async-done | bytes 5242912 | tf_op jit(solution)/shard_map/all_to_all | solution.py:160
  503.6 6.2 pad_maximum_fusion
  509.8 121.4 %while.14 = (s32[]{:T(128)}, bf16[20,512,128]{2,1,0:T(8,128)(2,1)}, f32[20,512]{1,0:T(8,128)S(1)}, s32[20]{0:T(128)S(1)}, bf16[512,2560]{1,0:T(8,128)(2,1)}, /*i...) while((s32[]{:T(128)}, bf16[20,512,128]{2,1,0:T(8,128)(2,1)}, ...), condition=%wide.region_12.16_spmd, body=%wide.region_9.15_spmd.sunk | while | flops 408223232 | bytes 11292343 | solution.py:95
  511.0 1.9 fusion.22
  513.5 2.3 fusion.23
  519.5 2.3 fusion.23
  523.2 1.9 fusion.22
  525.6 2.3 fusion.23
  531.7 2.3 fusion.23
  535.3 1.9 fusion.22
  537.7 2.3 fusion.23
  543.8 2.3 fusion.23
  547.4 1.9 fusion.22
  549.9 2.3 fusion.23
  555.9 2.3 fusion.23
  559.6 1.9 fusion.22
  562.0 2.3 fusion.23
  568.1 2.3 fusion.23
  571.7 1.9 fusion.22
  574.1 2.3 fusion.23
  580.2 2.3 fusion.23
  586.3 2.3 fusion.23
  592.3 2.3 fusion.23
  598.4 2.3 fusion.23
  604.5 2.3 fusion.23
  610.6 2.3 fusion.23
  616.6 2.3 fusion.23
  620.3 1.9 fusion.22
  622.7 2.3 fusion.23
  628.8 2.3 fusion.23
  631.1 3.5 copy.63
  634.6 2.8 reshape_reshape.11
  637.5 2.5 gather_fusion.14
  641.7 4.9 all-to-all-start.5
  647.5 57.8 %all-to-all-done.5 = bf16[16,2,16,2560]{3,2,1,0:T(8,128)(2,1)S(1)} async-done(((bf16[16,2,16,2560]{3,2,1,0:T(8,128)(2,1)}), bf16[16,2,16,2560]{3,2,1,0:T(8,128)(2,1)S(1)}, u32[]{:S(2)}, u32[]{:S(2)}) %all-to-all-start.5) | async-done | bytes 2621472 | tf_op jit(solution)/shard_map/all_to_all | solution.py:188
  705.3 2.2 gather_fusion.15
  707.5 2.0 broadcast_select_fusion.2
  711.0 2.0 copy.65
  713.0 2.2 reshape.516
  (178 shorter events, 71.8 us)
Async XLA Ops:
  173.8 5.5 copy-start.1
  173.8 5.8 copy-start
  173.8 63.9 %all-to-all-start.3 = ((bf16[16,2,16,2560]{3,2,1,0:T(8,128)(2,1)}), bf16[16,2,16,2560]{3,2,1,0:T(8,128)(2,1)S(1)}, u32[]{:S(2)}, u32[]{:S(2)}) async-start(bf16[16,2,16,2560]{3,2,1,0:T(8,128)(2,1)} %bitcast.67), calls=%async_computation.3 | async-start | bytes 5242880 | tf_op jit(solution)/shard_map/all_to_all | solution.py:135
  383.3 120.3 %all-to-all-start.2 = ((bf16[16,64,2560]{2,1,0:T(8,128)(2,1)}), bf16[16,64,2560]{2,1,0:T(8,128)(2,1)}, u32[]{:S(2)}, u32[]{:S(2)}) async-start(bf16[16,64,2560]{2,1,0:T(8,128)(2,1)} %get-tuple-element.103), calls=%async_computation.2 | async-start | bytes 10485760 | tf_op jit(solution)/shard_map/all_to_all | solution.py:160
  641.7 63.6 %all-to-all-start.5 = ((bf16[16,2,16,2560]{3,2,1,0:T(8,128)(2,1)}), bf16[16,2,16,2560]{3,2,1,0:T(8,128)(2,1)S(1)}, u32[]{:S(2)}, u32[]{:S(2)}) async-start(bf16[16,2,16,2560]{3,2,1,0:T(8,128)(2,1)} %bitcast.59), calls=%async_computation.5 | async-start | bytes 5242880 | tf_op jit(solution)/shard_map/all_to_all | solution.py:188
where the time goes:
time: 718 us; the launch traced here: 715 us
  blocking collectives  248 us (35%)
  waiting for transfers between devices  188 us (26%)
  local copies, waits for them, and re-layouts  110 us (15%)
  matrix products  83.4 us (12%)
  other arithmetic  55.5 us (8%)
  starting transfers between devices  15.6 us (2%)
  loops' own time  13.4 us (2%)
    all_to_all x1, blocking collectives, shards(): lax.all_to_all(out_value, 'seq', split_axis=0, concat_axis=0, tiled=True)  120 us
    all_to_all x1, waiting for transfers between devices, shards(): lax.all_to_all(out_key, 'seq', split_axis=0, concat_axis=0, tiled=True)  98.2 us
    all_to_all x1, blocking collectives, shards(): lax.all_to_all(sent_query, 'seq', split_axis=0, concat_axis=0, tiled=True)  65 us
    all_to_all x1, blocking collectives, shards(): lax.all_to_all(sent_key, 'seq', split_axis=0, concat_axis=0, tiled=True)  63.6 us
    all_to_all x1, waiting for transfers between devices, shards(): lax.all_to_all(back_sent, 'seq', split_axis=0, concat_axis=0, tiled=True)  57.8 us
    dot_general x20, matrix products, one_head(): jnp.dot(weights, head_part(pool_value, offset), preferred_element_type=jn...  46.2 us
    dot_general x20, matrix products, head_scores(): lax.dot_general(query_head, key_head, (((1,), (1,)), ((), ())), preferred...  37.2 us
    all_to_all x1, waiting for transfers between devices, shards(): lax.all_to_all(sent_value, 'seq', split_axis=0, concat_axis=0, tiled=True)  31.6 us
  transfers between devices with their start and end apart: 3, of which 3 were waited for; matrix products, arithmetic and copies ran while one was open for 6% of the time, Pallas kernels for 0%

commit v1 on v0

--- a/solution.py
+++ b/solution.py
@@ -2,6 +2,7 @@
 import jax.numpy as jnp
 from jax import lax
 from jax.sharding import PartitionSpec as P
+from jax.experimental import pallas as pl
 
 HEADS = 20
 HEAD_DIM = 128
@@ -79,20 +80,43 @@
     return jnp.where(mask, scores, masked_score)
 
 
+def attention_kernel(query_ref, key_ref, value_ref, mask_ref, out_ref, log_ref):
+    scores = lax.dot_general(
+        query_ref[...], key_ref[...], (((1,), (1,)), ((), ())), preferred_element_type=jnp.float32
+    ) * HEAD_DIM ** (-0.5)
+    scores = jnp.where(mask_ref[...] > 0, scores, masked_score)
+    row_max = jnp.max(scores, axis=1, keepdims=True)
+    log_total = row_max + jnp.log(jnp.sum(jnp.exp(scores - row_max), axis=1, keepdims=True))
+    weights = jnp.exp(scores - log_total).astype(jnp.bfloat16)
+    mixed = jnp.dot(weights, value_ref[...], preferred_element_type=jnp.float32)
+    out_ref[...] = mixed.astype(out_ref.dtype)
+    log_ref[...] = log_total
+
+
 def attend_pooled(own_query, pool_key, pool_value, mask):
-
-    def one_head(head_index):
-        offset = head_index * HEAD_DIM
-        scores = head_scores(head_part(own_query, offset), pool_key, offset, mask)
-        row_max = jnp.max(scores, axis=1, keepdims=True)
-        log_total = row_max + jnp.log(jnp.sum(jnp.exp(scores - row_max), axis=1, keepdims=True))
-        weights = jnp.exp(scores - log_total).astype(jnp.bfloat16)
-        mixed_rows = jnp.dot(
-            weights, head_part(pool_value, offset), preferred_element_type=jnp.float32
-        )
-        return (mixed_rows.astype(jnp.bfloat16), log_total[:, 0])
-
-    return lax.map(one_head, jnp.arange(HEADS, dtype=jnp.int32))
+    rows, channels = own_query.shape
+    pool = pool_key.shape[0]
+    heads = channels // HEAD_DIM
+    mask_values = mask.astype(jnp.float32)
+    mixed_rows, head_logs = pl.pallas_call(
+        attention_kernel,
+        grid=(heads,),
+        in_specs=[
+            pl.BlockSpec((rows, HEAD_DIM), lambda h: (0, h)),
+            pl.BlockSpec((pool, HEAD_DIM), lambda h: (0, h)),
+            pl.BlockSpec((pool, HEAD_DIM), lambda h: (0, h)),
+            pl.BlockSpec((rows, pool), lambda h: (0, 0)),
+        ],
+        out_specs=[
+            pl.BlockSpec((rows, HEAD_DIM), lambda h: (0, h)),
+            pl.BlockSpec((None, rows, 1), lambda h: (h, 0, 0)),
+        ],
+        out_shape=[
+            jax.ShapeDtypeStruct((rows, channels), jnp.bfloat16),
+            jax.ShapeDtypeStruct((heads, rows, 1), jnp.float32),
+        ],
+    )(own_query, pool_key, pool_value, mask_values)
+    return mixed_rows, head_logs[:, :, 0]
 
 
 def shards(query_feats, key_feats, value_feats, owner_map, pattern):
@@ -168,8 +192,7 @@
     pool_key = jnp.concatenate([own_key, far_key_rows], axis=0)
     pool_value = jnp.concatenate([own_value, far_value_rows], axis=0)
     pool_mask = jnp.concatenate([near_mask, far_mask], axis=1)
-    head_out, head_logs = attend_pooled(own_query, pool_key, pool_value, pool_mask)
-    mixed_rows = head_out.transpose(1, 0, 2).reshape(own_count * 64, channels)
+    mixed_rows, head_logs = attend_pooled(own_query, pool_key, pool_value, pool_mask)
     log_sums = (
         head_logs.reshape(HEADS, own_count, 64).transpose(1, 0, 2).reshape(1, own_count, HEADS * 64)
     )

time: 718 us -> 644 us (0.90)
  matrix products: 83.4 us -> 0 us
  Pallas kernels: 0 us -> 55.2 us
  local copies, waits for them, and re-layouts: 110 us -> 91.1 us
  loops' own time: 13.4 us -> 0 us
    dot_general x40 -> x0, matrix products: 83.4 us -> none  [the longest x20 46.2 us: one_head(): jnp.dot(weights, head_part(pool_value, offset), preferred_element_type=jn...]
    pallas_call x0 -> x1, Pallas kernels: none -> 55.2 us  [attend_pooled(): pl.pallas_call(attention_kernel, grid=(heads,), in_specs=[pl.BlockSpec((r...]
    another operation x1 -> x0, loops' own time: 13.4 us -> none  [attend_pooled(): return lax.map(one_head, jnp.arange(HEADS, dtype=jnp.int32))]
    dynamic_slice x20 -> x0, local copies, waits for them, and re-layouts: 12.3 us -> none  [attend_pooled(): return lax.map(one_head, jnp.arange(HEADS, dtype=jnp.int32))]
    reduce_sum x20 -> x0, other arithmetic: 11.5 us -> none  [one_head(): jnp.sum(jnp.exp(scores - row_max), axis=1, keepdims=True)]
  transfers between devices with their start and end apart: 3 -> 3, of which waited for: 3 -> 3; matrix products, arithmetic and copies ran while one was open for 6% -> 8% of each run, Pallas kernels for 0% -> 0%
where the time goes in v1:
time: 644 us; the launch traced here: 643 us
  blocking collectives  248 us (39%)
  waiting for transfers between devices  183 us (28%)
  local copies, waits for them, and re-layouts  91.1 us (14%)
  Pallas kernels  55.2 us (9%)
  other arithmetic  48.7 us (8%)
  starting transfers between devices  15.8 us (2%)
    all_to_all x1, blocking collectives, shards(): lax.all_to_all(out_value, 'seq', split_axis=0, concat_axis=0, tiled=True)  120 us
    all_to_all x1, waiting for transfers between devices, shards(): lax.all_to_all(out_key, 'seq', split_axis=0, concat_axis=0, tiled=True)  97.4 us
    all_to_all x1, blocking collectives, shards(): lax.all_to_all(sent_query, 'seq', split_axis=0, concat_axis=0, tiled=True)  65 us
    all_to_all x1, blocking collectives, shards(): lax.all_to_all(sent_key, 'seq', split_axis=0, concat_axis=0, tiled=True)  63.6 us
    pallas_call x1, Pallas kernels, attend_pooled(): pl.pallas_call(attention_kernel, grid=(heads,), in_specs=[pl.BlockSpec((r...  55.2 us
    all_to_all x1, waiting for transfers between devices, shards(): lax.all_to_all(back_sent, 'seq', split_axis=0, concat_axis=0, tiled=True)  53.9 us
    all_to_all x1, waiting for transfers between devices, shards(): lax.all_to_all(sent_value, 'seq', split_axis=0, concat_axis=0, tiled=True)  31.5 us
    gather x3, local copies, waits for them, and re-layouts, request_table(): entry_owner = jnp.take(owner_map, pattern)  17.1 us
  transfers between devices with their start and end apart: 3, of which 3 were waited for; matrix products, arithmetic and copies ran while one was open for 8% of the time, Pallas kernels for 0%

profile of v1, /device:TPU:13, one launch (start us, length us, event | category | flops | bytes accessed | tf_op | source)
XLA Modules:
  0.0 643.0 jit_solution(10389057537274450164)
XLA Ops:
  0.6 0.7 eq.186
  1.4 0.7 broadcast_compare_fusion.2
  2.0 0.7 fusion.1
  2.9 0.2 convert_reduce_fusion
  3.2 1.4 gather_fusion.4
  4.5 0.7 gather_fusion.5
  5.8 0.8 select_reduce_fusion.2
  6.7 0.6 gather_fusion
  7.9 4.3 reshape.463
  12.2 0.5 copy.51
  12.8 1.4 copy.52
  14.2 5.5 reshape.470
  19.8 2.3 copy.53
  22.0 2.9 copy.54
  25.0 2.2 gather_fusion.6
  27.2 4.0 gather_fusion.8
  31.2 4.3 reshape.476
  35.5 0.5 copy.57
  36.0 1.4 copy.58
  37.5 2.2 gather_fusion.11
  39.7 5.6 broadcast_select_fusion.7
  45.3 65.0 %all_to_all.30 = bf16[16,2,16,2560]{3,2,1,0:T(8,128)(2,1)} all-to-all(bf16[16,2,16,2560]{3,2,1,0:T(8,128)(2,1)S(1)} %bitcast.55), channel_id=1, replica_groups=mesh['groups'=2,'seq'=16] {'seq'}, dimensions={0} | all-to-all | bytes 5242880 | tf_op jit(solution)/shard_map/all_to_all | solution.py:157
  110.2 63.6 %all_to_all.31 = bf16[16,2,16,2560]{3,2,1,0:T(8,128)(2,1)} all-to-all(bf16[16,2,16,2560]{3,2,1,0:T(8,128)(2,1)S(1)} %bitcast.54), channel_id=1, replica_groups=mesh['groups'=2,'seq'=16] {'seq'}, dimensions={0} | all-to-all | bytes 5242880 | tf_op jit(solution)/shard_map/all_to_all | solution.py:158
  173.8 5.3 all-to-all-start.3
  179.4 0.2 reshape.665
  179.6 16.9 %gather_fusion.1 = s32[2944]{0:T(1024)S(1)} fusion(s32[128]{0:T(128)S(1)} %copy-done, s32[3072]{0:T(1024)S(1)} %pad_clamp_fusion), kind=kCustom, calls=%fused_computation.13 | custom fusion | bytes 35328 | tf_op jit(solution)/shard_map/jit(_take)/gather | solution.py:52
  196.5 0.2 reshape.664
  196.9 0.3 select_reduce_fusion.1
  197.3 0.2 fusion.2
  197.5 0.7 gather_fusion.2
  198.1 0.2 compare_reduce_fusion.2
  198.4 4.0 gather_fusion.7
  202.3 3.9 gather_fusion.9
  206.3 31.5 %all-to-all-done.3 = bf16[16,2,16,2560]{3,2,1,0:T(8,128)(2,1)S(1)} async-done(((bf16[16,2,16,2560]{3,2,1,0:T(8,128)(2,1)}), bf16[16,2,16,2560]{3,2,1,0:T(8,128)(2,1)S(1)}, u32[]{:S(2)}, u32[]{:S(2)}) %all-to-all-start.3) | async-done | bytes 2621472 | tf_op jit(solution)/shard_map/all_to_all | solution.py:159
  237.8 2.2 gather_fusion.12
  240.0 6.4 broadcast_select_fusion.4
  246.4 3.2 gather_fusion.10
  249.6 4.9 gather_fusion.13
  254.5 9.1 %broadcast_select_fusion = (bf16[16,64,2560]{2,1,0:T(8,128)(2,1)}, bf16[16,64,2560]{2,1,0:T(8,128)(2,1)}) fusion(bf16[16,64,2560]{2,1,0:T(8,128)(2,1)} %gather_fusion.13, pred[16]{0:T(512)(128)(4,1)S(1)} %get-tuple-element.35, bf16[16,64,2560]{2,1,0:T(8,128)(2,1)} %gather_fusion.10), kind=kLoop, calls=%fused_computation.18 | loop fusion | flops 5242880 | bytes 20971536 | tf_op jit(solution)/shard_map/jit(_take)/select_n | solution.py:182
  263.6 119.7 %all_to_all.32 = bf16[16,64,2560]{2,1,0:T(8,128)(2,1)} all-to-all(bf16[16,64,2560]{2,1,0:T(8,128)(2,1)} %get-tuple-element.43), channel_id=1, replica_groups=mesh['groups'=2,'seq'=16] {'seq'}, dimensions={0} | all-to-all | bytes 10485760 | tf_op jit(solution)/shard_map/all_to_all | solution.py:185
  383.4 5.4 all-to-all-start.2
  388.9 0.6 gather_fusion.3
  389.5 0.3 compare_reduce_fusion
  389.8 1.3 broadcast_in_dim.189
  391.1 3.0 reshape.483
  394.2 0.3 compare_reduce_fusion.1
  394.5 1.1 broadcast_in_dim.188
  395.5 1.8 reshape.482
  397.4 2.0 add_convert_fusion.mask_ref
  399.4 6.9 %pad_maximum_fusion.1.value_ref = bf16[1536,2560]{1,0:T(8,128)(2,1)} fusion(bf16[1024,2560]{1,0:T(8,128)(2,1)} %bitcast.40, bf16[512,2560]{1,0:T(8,128)(2,1)} %bitcast.39), kind=kLoop, calls=%fused_computation.17 | loop fusion | flops 15728640 | bytes 15728640 | tf_op jit(solution)/shard_map/concatenate | solution.py:193
  406.3 97.4 %all-to-all-done.2 = bf16[16,64,2560]{2,1,0:T(8,128)(2,1)} async-done(((bf16[16,64,2560]{2,1,0:T(8,128)(2,1)}), bf16[16,64,2560]{2,1,0:T(8,128)(2,1)}, u32[]{:S(2)}, u32[]{:S(2)}) %all-to-all-start.2) | async-done | bytes 5242912 | tf_op jit(solution)/shard_map/all_to_all | solution.py:184
  503.7 6.2 pad_maximum_fusion.key_ref
  509.8 55.2 %shard_map.68 = (bf16[512,2560]{1,0:T(8,128)(2,1)}, f32[20,512,1]{2,1,0:T(8,128)}) custom-call(bf16[512,2560]{1,0:T(8,128)(2,1)} %bitcast.56, bf16[1536,2560]{1,0:T(8,128)(2,1)} %pad_maximum_fusion.key_ref, bf16[1536,2560]{1,0:T(8,128)(2,1)} %pad_maximum_fusion.1.value_ref, f32[512,1536]{1,0:T(8,128)} %add_convert_fusion.mask_ref), custom_call_target="tpu_custom_call" | custom-call | tf_op jit(solution)/shard_map/pallas_call | solution.py:101
  565.1 2.5 gather_fusion.14
  567.5 1.8 broadcast_select_fusion.3
  569.3 5.1 all-to-all-start.5
  574.4 3.9 reduce.2
  578.5 0.7 reshape.490
  579.2 53.9 %all-to-all-done.5 = bf16[16,2,16,2560]{3,2,1,0:T(8,128)(2,1)S(1)} async-done(((bf16[16,2,16,2560]{3,2,1,0:T(8,128)(2,1)}), bf16[16,2,16,2560]{3,2,1,0:T(8,128)(2,1)S(1)}, u32[]{:S(2)}, u32[]{:S(2)}) %all-to-all-start.5) | async-done | bytes 2621472 | tf_op jit(solution)/shard_map/all_to_all | solution.py:211
  633.1 2.2 gather_fusion.15
  635.3 2.0 broadcast_select_fusion.2
  637.3 1.4 copy.60
  638.8 2.0 copy.61
  640.8 2.2 reshape.489
  (54 shorter events, 2.0 us)
Async XLA Ops:
  173.8 5.5 copy-start.1
  173.8 5.8 copy-start
  173.8 63.9 %all-to-all-start.3 = ((bf16[16,2,16,2560]{3,2,1,0:T(8,128)(2,1)}), bf16[16,2,16,2560]{3,2,1,0:T(8,128)(2,1)S(1)}, u32[]{:S(2)}, u32[]{:S(2)}) async-start(bf16[16,2,16,2560]{3,2,1,0:T(8,128)(2,1)} %bitcast.53), calls=%async_computation.3 | async-start | bytes 5242880 | tf_op jit(solution)/shard_map/all_to_all | solution.py:159
  383.4 120.3 %all-to-all-start.2 = ((bf16[16,64,2560]{2,1,0:T(8,128)(2,1)}), bf16[16,64,2560]{2,1,0:T(8,128)(2,1)}, u32[]{:S(2)}, u32[]{:S(2)}) async-start(bf16[16,64,2560]{2,1,0:T(8,128)(2,1)} %get-tuple-element.44), calls=%async_computation.2 | async-start | bytes 10485760 | tf_op jit(solution)/shard_map/all_to_all | solution.py:184
  569.3 63.8 %all-to-all-start.5 = ((bf16[16,2,16,2560]{3,2,1,0:T(8,128)(2,1)}), bf16[16,2,16,2560]{3,2,1,0:T(8,128)(2,1)S(1)}, u32[]{:S(2)}, u32[]{:S(2)}) async-start(bf16[16,2,16,2560]{3,2,1,0:T(8,128)(2,1)} %bitcast.45), calls=%async_computation.5 | async-start | bytes 5242880 | tf_op jit(solution)/shard_map/all_to_all | solution.py:211

commit v2 on v1

v2 whole, which is shorter than its diff:
```python
import jax
import jax.numpy as jnp
from jax import lax
from jax.sharding import PartitionSpec as P
from jax.experimental import pallas as pl

HEADS = 20
HEAD_DIM = 128
WIDTH = 64
FRAMES = 16


masked_score = -1e30


def frame_pieces(rows_in, strips):
    channels = rows_in.shape[1]
    shaped = rows_in.reshape(strips, 4, WIDTH // 4, 4, channels)
    return shaped.transpose(0, 2, 1, 3, 4).reshape(strips * (WIDTH // 4), 16, channels)


def frame_rows(pieces, strips):
    channels = pieces.shape[2]
    shaped = pieces.reshape(strips, WIDTH // 4, 4, 4, channels)
    return shaped.transpose(0, 2, 1, 3, 4).reshape(strips * 4 * WIDTH, channels)


def owner_tables(owner_map, group_size, piece_count):
    tile_count = owner_map.shape[0]
    devices = jnp.arange(group_size, dtype=jnp.int32)
    onehot = (owner_map[:, None] == devices[None, :]).astype(jnp.int32)
    running = jnp.cumsum(onehot, axis=0)
    own_rank = jnp.sum(onehot * running, axis=1) - 1
    by_class = owner_map.reshape(tile_count // piece_count, piece_count)
    local_iota = jnp.arange(piece_count, dtype=jnp.int32)
    earlier = (by_class[:, :, None] == by_class[:, None, :]) & (
        local_iota[None, None, :] < local_iota[None, :, None]
    )
    class_rank = jnp.sum(earlier.astype(jnp.int32), axis=2).reshape(tile_count)
    return (own_rank, class_rank)


def owned_tiles(owner_map, own_rank, device, own_count):
    tile_iota = jnp.arange(owner_map.shape[0], dtype=jnp.int32)
    slot_iota = jnp.arange(own_count, dtype=jnp.int32)
    match_rows = (owner_map[None, :] == device) & (own_rank[None, :] == slot_iota[:, None])
    return jnp.sum(jnp.where(match_rows, tile_iota[None, :], 0), axis=1)


def request_table(owner_map, pattern, group_size):
    devices = jnp.arange(group_size, dtype=jnp.int32)
    entry_owner = jnp.take(owner_map, pattern)
    foreign = entry_owner != owner_map[:, None]
    entry_hit = (entry_owner[:, :, None] == devices[None, None, :]) & foreign[:, :, None]
    per_tile = jnp.max(jnp.where(entry_hit, pattern[:, :, None], -1), axis=1)
    per_user = owner_map[None, :] == devices[:, None]
    return jnp.max(jnp.where(per_user[:, :, None], per_tile[None, :, :], -1), axis=1)


def supplier_of(tile_class, frame_slice, frame_devs):
    return (4 * (tile_class // frame_devs) + frame_slice) * frame_devs + tile_class % frame_devs


def expand_mask(block_mask):
    query_tiles = block_mask.shape[0]
    key_tiles = block_mask.shape[1]
    wide = jnp.broadcast_to(block_mask[:, None, :, None], (query_tiles, 64, key_tiles, 64))
    return wide.reshape(query_tiles * 64, key_tiles * 64)


def head_part(matrix, offset):
    return lax.dynamic_slice_in_dim(matrix, offset, HEAD_DIM, 1)


def head_scores(query_head, key_rows, offset, mask):
    key_head = head_part(key_rows, offset)
    scores = lax.dot_general(
        query_head, key_head, (((1,), (1,)), ((), ())), preferred_element_type=jnp.float32
    ) * HEAD_DIM ** (-0.5)
    return jnp.where(mask, scores, masked_score)


FAR_SLOTS = 4


def attention_kernel(
    query_ref, near_key_ref, near_value_ref, far_key_ref, far_value_ref, near_bias_ref,
    far_bias_ref, out_ref, log_ref
):
    query = query_ref[...]
    dims = (((1,), (1,)), ((), ()))
    scale = HEAD_DIM ** (-0.5)
    near_scores = lax.dot_general(
        query, near_key_ref[...], dims, preferred_element_type=jnp.float32
    ) * scale + near_bias_ref[...]
    far_scores = lax.dot_general(
        query, far_key_ref[...], dims, preferred_element_type=jnp.float32
    ) * scale + far_bias_ref[...]
    row_max = jnp.maximum(
        jnp.max(near_scores, axis=1, keepdims=True), jnp.max(far_scores, axis=1, keepdims=True)
    )
    near_exp = jnp.exp(near_scores - row_max)
    far_exp = jnp.exp(far_scores - row_max)
    total = jnp.sum(near_exp, axis=1, keepdims=True) + jnp.sum(far_exp, axis=1, keepdims=True)
    log_total = row_max + jnp.log(total)
    inverse = 1.0 / total
    near_weights = (near_exp * inverse).astype(jnp.bfloat16)
    far_weights = (far_exp * inverse).astype(jnp.bfloat16)
    mixed = jnp.dot(near_weights, near_value_ref[...], preferred_element_type=jnp.float32)
    mixed = mixed + jnp.dot(far_weights, far_value_ref[...], preferred_element_type=jnp.float32)
    out_ref[...] = mixed.astype(out_ref.dtype)
    log_ref[...] = log_total


def attend(query, near_key, near_value, far_key, far_value, near_bias, far_bias):
    rows, channels = query.shape
    near = near_key.shape[0]
    far = far_key.shape[0]
    heads = channels // HEAD_DIM
    return pl.pallas_call(
        attention_kernel,
        grid=(heads,),
        in_specs=[
            pl.BlockSpec((rows, HEAD_DIM), lambda h: (0, h)),
            pl.BlockSpec((near, HEAD_DIM), lambda h: (0, h)),
            pl.BlockSpec((near, HEAD_DIM), lambda h: (0, h)),
            pl.BlockSpec((far, HEAD_DIM), lambda h: (0, h)),
            pl.BlockSpec((far, HEAD_DIM), lambda h: (0, h)),
            pl.BlockSpec((rows, near), lambda h: (0, 0)),
            pl.BlockSpec((rows, far), lambda h: (0, 0)),
        ],
        out_specs=[
            pl.BlockSpec((rows, HEAD_DIM), lambda h: (0, h)),
            pl.BlockSpec((None, rows, 1), lambda h: (h, 0, 0)),
        ],
        out_shape=[
            jax.ShapeDtypeStruct((rows, channels), jnp.bfloat16),
            jax.ShapeDtypeStruct((heads, rows, 1), jnp.float32),
        ],
    )(query, near_key, near_value, far_key, far_value, near_bias, far_bias)


def class_of(devices, frame_devs):
    return devices // frame_devs // 4 * frame_devs + devices % frame_devs


def ranked_pick(candidates, wanted, slot_count):
    rank = jnp.cumsum(wanted.astype(jnp.int32), axis=-1) - 1
    slots = jnp.arange(slot_count, dtype=jnp.int32)
    hit = wanted[..., None] & (rank[..., None] == slots)
    picked = jnp.sum(jnp.where(hit, candidates[..., None], 0), axis=-2)
    return picked, jnp.any(hit, axis=-2)


def shards(query_feats, key_feats, value_feats, owner_map, pattern):
    group_size = lax.axis_size("seq")
    device = lax.axis_index("seq")
    local_rows, channels = query_feats.shape
    strips = local_rows // (4 * WIDTH)
    blocks = WIDTH // 4
    piece_count = strips * blocks
    tile_count = owner_map.shape[0]
    own_count = tile_count // group_size
    capacity = (piece_count + group_size - 1) // group_size
    frame_devs = group_size // FRAMES
    devices = jnp.arange(group_size, dtype=jnp.int32)
    local_iota = jnp.arange(piece_count, dtype=jnp.int32)
    cap_iota = jnp.arange(capacity, dtype=jnp.int32)
    slice_iota = jnp.arange(4, dtype=jnp.int32)
    token_iota = jnp.arange(16, dtype=jnp.int32)

    def piece_rows(pieces):
        strip = pieces // blocks
        column = pieces % blocks
        return (
            strip[..., None] * (4 * WIDTH)
            + (token_iota // 4) * WIDTH
            + column[..., None] * 4
            + token_iota % 4
        )

    own_rank, class_rank = owner_tables(owner_map, group_size, piece_count)
    my_class = class_of(device, frame_devs)
    my_tiles = my_class * piece_count + local_iota
    my_owner = jnp.take(owner_map, my_tiles)
    my_slot = jnp.take(class_rank, my_tiles)
    send_hit = (my_owner[None, None, :] == devices[:, None, None]) & (
        my_slot[None, None, :] == cap_iota[None, :, None]
    )
    send_index = jnp.sum(jnp.where(send_hit, local_iota[None, None, :], 0), axis=2)
    own_send_rows = piece_rows(send_index).reshape(-1)
    requests = request_table(owner_map, pattern, group_size)
    wanted = (requests >= 0) & (requests // piece_count == my_class)
    far_send_piece, _ = ranked_pick(requests % piece_count, wanted, FAR_SLOTS)
    far_send_rows = piece_rows(far_send_piece).reshape(-1)
    own_shape = (group_size, capacity * 16, channels)
    far_shape = (group_size, FAR_SLOTS * 16, channels)
    sent_query = jnp.take(query_feats, own_send_rows, axis=0).reshape(own_shape)
    sent_key = jnp.take(key_feats, own_send_rows, axis=0).reshape(own_shape)
    sent_value = jnp.take(value_feats, own_send_rows, axis=0).reshape(own_shape)
    sent_far_key = jnp.take(key_feats, far_send_rows, axis=0).reshape(far_shape)
    sent_far_value = jnp.take(value_feats, far_send_rows, axis=0).reshape(far_shape)

    def exchange(sent):
        got = lax.all_to_all(sent, "seq", split_axis=0, concat_axis=0, tiled=True)
        return got.reshape(-1, channels)

    got_query = exchange(sent_query)
    got_key = exchange(sent_key)
    got_value = exchange(sent_value)
    got_far_key = exchange(sent_far_key)
    got_far_value = exchange(sent_far_value)
    source_class = class_of(devices, frame_devs)
    class_tiles = source_class[:, None] * piece_count + local_iota[None, :]
    mine = jnp.take(owner_map, class_tiles) == device
    near_hit = mine[:, None, :] & (jnp.take(class_rank, class_tiles)[:, None, :] == cap_iota[None, :, None])
    near_tile = jnp.sum(jnp.where(near_hit, class_tiles[:, None, :], 0), axis=2)
    near_tile_rows = jnp.broadcast_to(near_tile[:, :, None], (group_size, capacity, 16)).reshape(-1)
    my_requests = jnp.take(requests, device, axis=0)
    far_wanted = (my_requests[None, :] >= 0) & (my_requests[None, :] // piece_count == source_class[:, None])
    far_tile, far_valid = ranked_pick(
        jnp.broadcast_to(my_requests[None, :], (group_size, group_size)), far_wanted, FAR_SLOTS
    )
    far_tile = jnp.where(far_valid, far_tile, -1)
    far_tile_rows = jnp.broadcast_to(far_tile[:, :, None], (group_size, FAR_SLOTS, 16)).reshape(-1)
    own_ids = owned_tiles(owner_map, own_rank, device, own_count)
    listed = jnp.take(pattern, own_ids, axis=0)
    near_ok = jnp.any(listed[:, :, None] == near_tile_rows[None, None, :], axis=1)
    far_ok = jnp.any(listed[:, :, None] == far_tile_rows[None, None, :], axis=1)
    query_own = jnp.take(own_rank, near_tile_rows)
    near_bias = jnp.where(jnp.take(near_ok, query_own, axis=0), 0.0, masked_score).astype(jnp.float32)
    far_bias = jnp.where(jnp.take(far_ok, query_own, axis=0), 0.0, masked_score).astype(jnp.float32)
    mixed_rows, head_logs = attend(
        got_query, got_key, got_value, got_far_key, got_far_value, near_bias, far_bias
    )
    own_class = own_ids // piece_count
    own_slot = jnp.take(class_rank, own_ids)
    gather_rows = (
        supplier_of(own_class[:, None], slice_iota[None, :], frame_devs) * capacity
        + own_slot[:, None]
    )
    log_rows = (gather_rows[:, :, None] * 16 + token_iota).reshape(-1)
    heads = channels // HEAD_DIM
    log_sums = (
        jnp.take(head_logs[:, :, 0], log_rows, axis=1)
        .reshape(heads, own_count, 64)
        .transpose(1, 0, 2)
        .reshape(1, own_count, heads * 64)
    )
    returned = exchange(mixed_rows.reshape(own_shape))
    local_iota_rows = jnp.arange(local_rows, dtype=jnp.int32)
    strip = local_iota_rows // (4 * WIDTH)
    height = local_iota_rows % (4 * WIDTH) // WIDTH
    column = local_iota_rows % WIDTH
    piece = strip * blocks + column // 4
    token = height * 4 + column % 4
    back_rows = (jnp.take(my_owner, piece) * capacity + jnp.take(my_slot, piece)) * 16 + token
    attended = jnp.take(returned, back_rows, axis=0)
    return (attended, log_sums)


def solution(mesh):
    placed = (
        P(("groups", "seq"), None),
        P(("groups", "seq"), None),
        P(("groups", "seq"), None),
        P("groups"),
        P("groups", None),
    )
    return jax.shard_map(
        shards,
        mesh=mesh,
        in_specs=placed,
        out_specs=(P(("groups", "seq"), None), P(("groups", "seq"), None, None)),
        check_vma=False,
    )
```

time: 644 us -> 585 us (0.908)
  waiting for transfers between devices: 183 us -> 114 us
  other arithmetic: 48.7 us -> 64.1 us
    all_to_all x3, waiting for transfers between devices: 183 us -> 114 us  [exchange(): got = lax.all_to_all(sent, 'seq', split_axis=0, concat_axis=0, tiled=True)]
    and x4 -> x6, other arithmetic: 0.04 us -> 40 us  [the longest x1 39.9 us: shards(): attended = jnp.take(returned, back_rows, axis=0)]
    gather x11 -> x19, local copies, waits for them, and re-layouts: 32 us -> 60.1 us  [the longest x1 12.5 us: shards(): jnp.take(value_feats, far_send_rows, axis=0).reshape(far_shape)]
    reshape x12 -> x3, local copies, waits for them, and re-layouts: 28 us -> 0.9 us  [the longest x1 0.7 us: shards(): log_sums = jnp.take(head_logs[:, :, 0], log_rows, axis=1).reshape(heads,...]
    concatenate x2 -> x0, other arithmetic: 13 us -> none  [the longest x1 6.89 us: shards(): pool_value = jnp.concatenate([own_value, far_value_rows], axis=0)]
    select_n x10 -> x16, other arithmetic: 24.9 us -> 20.9 us  [the longest x1 9.21 us: shards(): jnp.take(value_feats, far_send_rows, axis=0).reshape(far_shape)]
  transfers between devices with their start and end apart: 3 -> 3, of which waited for: 3 -> 3; matrix products, arithmetic and copies ran while one was open for 8% -> 20% of each run, Pallas kernels for 0% -> 0%
where the time goes in v2:
time: 585 us; the launch traced here: 583 us
  blocking collectives  248 us (42%)
  waiting for transfers between devices  114 us (19%)
  local copies, waits for them, and re-layouts  89.3 us (15%)
  other arithmetic  64.1 us (11%)
  Pallas kernels  50.8 us (9%)
  starting transfers between devices  15.6 us (3%)
    all_to_all x3, blocking collectives, exchange(): got = lax.all_to_all(sent, 'seq', split_axis=0, concat_axis=0, tiled=True)  248 us
    all_to_all x3, waiting for transfers between devices, exchange(): got = lax.all_to_all(sent, 'seq', split_axis=0, concat_axis=0, tiled=True)  114 us
    pallas_call x1, Pallas kernels, attend(): pl.pallas_call(attention_kernel, grid=(heads,), in_specs=[pl.BlockSpec((r...  50.8 us
    and x1, other arithmetic, shards(): attended = jnp.take(returned, back_rows, axis=0)  39.9 us
    gather x3, local copies, waits for them, and re-layouts, request_table(): entry_owner = jnp.take(owner_map, pattern)  17.1 us
    all_to_all x3, starting transfers between devices, exchange(): got = lax.all_to_all(sent, 'seq', split_axis=0, concat_axis=0, tiled=True)  15.6 us
    gather x1, local copies, waits for them, and re-layouts, shards(): jnp.take(value_feats, far_send_rows, axis=0).reshape(far_shape)  12.5 us
  transfers between devices with their start and end apart: 3, of which 3 were waited for; matrix products, arithmetic and copies ran while one was open for 20% of the time, Pallas kernels for 0%

profile of v2, /device:TPU:13, one launch (start us, length us, event | category | flops | bytes accessed | tf_op | source)
XLA Modules:
  0.0 583.4 jit_solution(1404843086523329628)
XLA Ops:
  0.7 0.9 eq.243
  1.6 0.2 convert_reduce_fusion
  1.9 1.4 gather_fusion.7
  3.3 0.7 gather_fusion.8
  4.0 0.1 select_reduce_fusion.6
  4.3 0.1 add_add_fusion.1
  4.6 8.2 %gather_fusion.9 = bf16[512,2560]{1,0:T(8,128)(2,1)} fusion(bf16[512,2560]{1,0:T(8,128)(2,1)} %param.15, s32[1024]{0:T(1024)S(1)} %pad_clamp_fusion.7), kind=kCustom, calls=%fused_computation.1.clone | custom fusion | bytes 5244928 | tf_op jit(solution)/shard_map/jit(_take)/gather | solution.py:198
  12.8 3.5 gather_fusion.10
  16.3 8.2 %gather_fusion.11 = bf16[512,2560]{1,0:T(8,128)(2,1)} fusion(bf16[512,2560]{1,0:T(8,128)(2,1)} %param.17, s32[1024]{0:T(1024)S(1)} %pad_clamp_fusion.7), kind=kCustom, calls=%fused_computation.6.clone | custom fusion | bytes 5244928 | tf_op jit(solution)/shard_map/jit(_take)/gather | solution.py:200
  24.4 4.8 broadcast_select_fusion.3
  29.2 65.0 %all_to_all.30 = bf16[16,32,2560]{2,1,0:T(8,128)(2,1)} all-to-all(bf16[16,32,2560]{2,1,0:T(8,128)(2,1)S(1)} %bitcast.99), channel_id=1, replica_groups=mesh['groups'=2,'seq'=16] {'seq'}, dimensions={0} | all-to-all | bytes 5242880 | tf_op jit(solution)/shard_map/all_to_all | solution.py:205
  94.2 63.6 %all_to_all.31 = bf16[16,32,2560]{2,1,0:T(8,128)(2,1)} all-to-all(bf16[16,32,2560]{2,1,0:T(8,128)(2,1)S(1)} %bitcast.98), channel_id=1, replica_groups=mesh['groups'=2,'seq'=16] {'seq'}, dimensions={0} | all-to-all | bytes 5242880 | tf_op jit(solution)/shard_map/all_to_all | solution.py:205
  157.8 5.3 all-to-all-start.2
  163.1 0.1 copy.38
  163.2 0.2 reshape.977
  163.4 16.9 %gather_fusion = s32[2944]{0:T(1024)S(1)} fusion(s32[128]{0:T(128)S(1)} %copy-done.2, s32[3072]{0:T(1024)S(1)} %pad_clamp_fusion), kind=kCustom, calls=%fused_computation.10 | custom fusion | bytes 35328 | tf_op jit(solution)/shard_map/jit(_take)/gather | solution.py:52
  180.3 0.2 reshape.976
  180.7 0.3 select_reduce_fusion.1
  181.1 0.2 reduce_window_sum.28
  181.2 0.1 select_reduce_fusion.4
  181.6 0.1 add_add_fusion
  181.8 6.3 %gather_fusion.12 = bf16[1024,2560]{1,0:T(8,128)(2,1)} fusion(bf16[512,2560]{1,0:T(8,128)(2,1)S(1)} %copy-done, s32[1024]{0:T(1024)S(1)} %fusion.18), kind=kCustom, calls=%fused_computation.2.clone | custom fusion | bytes 10489856 | tf_op jit(solution)/shard_map/jit(_take)/gather | solution.py:201
  188.1 12.5 %gather_fusion.13 = bf16[1024,2560]{1,0:T(8,128)(2,1)} fusion(bf16[512,2560]{1,0:T(8,128)(2,1)} %param.17, s32[1024]{0:T(1024)S(1)} %fusion.18), kind=kCustom, calls=%fused_computation.8.clone | custom fusion | bytes 10489856 | tf_op jit(solution)/shard_map/jit(_take)/gather | solution.py:202
  200.6 9.2 %broadcast_select_fusion = (bf16[1024,2560]{1,0:T(8,128)(2,1)}, bf16[1024,2560]{1,0:T(8,128)(2,1)}) fusion(bf16[1024,2560]{1,0:T(8,128)(2,1)} %gather_fusion.13, pred[1024]{0:T(1024)(128)(4,1)S(1)} %compare_and_fusion.3, bf16[1024,2560]{1,0:T(8,128)(2,1)} %gather_fusion.12), kind=kLoop, calls=%fused_computation.17 | loop fusion | flops 5242880 | bytes 20972544 | tf_op jit(solution)/shard_map/jit(_take)/select_n | solution.py:202
  209.8 12.0 %all-to-all-done.2 = bf16[16,32,2560]{2,1,0:T(8,128)(2,1)} async-done(((bf16[16,32,2560]{2,1,0:T(8,128)(2,1)}), bf16[16,32,2560]{2,1,0:T(8,128)(2,1)}, u32[]{:S(2)}, u32[]{:S(2)}) %all-to-all-start.2) | async-done | bytes 2621472 | tf_op jit(solution)/shard_map/all_to_all | solution.py:205
  221.8 119.7 %all_to_all.32 = bf16[16,64,2560]{2,1,0:T(8,128)(2,1)} all-to-all(bf16[16,64,2560]{2,1,0:T(8,128)(2,1)} %bitcast.96), channel_id=1, replica_groups=mesh['groups'=2,'seq'=16] {'seq'}, dimensions={0} | all-to-all | bytes 10485760 | tf_op jit(solution)/shard_map/all_to_all | solution.py:205
  341.6 5.4 all-to-all-start.4
  346.9 0.1 copy.43
  347.2 3.3 gather_fusion.14
  350.6 3.3 gather_fusion.15
  354.2 0.1 select_reduce_fusion.5
  354.5 0.1 reshape.783
  354.6 0.1 reshape.782
  354.8 0.2 reduce_window_sum.30
  355.0 0.1 fusion.4
  355.2 0.2 select_reduce_fusion.3
  355.5 0.1 eq.284
  355.7 0.2 reduce_window_sum.29
  355.9 0.2 select_reduce_fusion.2
  356.1 0.1 select_reduce_fusion.7
  356.2 0.6 gather_fusion.5
  356.8 0.6 gather_fusion.2
  357.6 3.3 gather_fusion.1
  361.0 0.2 compare_reduce_fusion
  361.2 1.9 gather_fusion.4
  363.1 0.1 compare_reduce_fusion.1
  363.2 1.8 gather_fusion.3
  365.0 1.2 select_select_fusion.1.near_bias_ref
  366.2 1.7 select_select_fusion.far_bias_ref
  368.0 93.9 %all-to-all-done.4 = bf16[16,64,2560]{2,1,0:T(8,128)(2,1)} async-done(((bf16[16,64,2560]{2,1,0:T(8,128)(2,1)}), bf16[16,64,2560]{2,1,0:T(8,128)(2,1)}, u32[]{:S(2)}, u32[]{:S(2)}) %all-to-all-start.4) | async-done | bytes 5242912 | tf_op jit(solution)/shard_map/all_to_all | solution.py:205
  461.9 50.8 %shard_map.68 = (bf16[512,2560]{1,0:T(8,128)(2,1)}, f32[20,512,1]{2,1,0:T(8,128)}) custom-call(bf16[512,2560]{1,0:T(8,128)(2,1)} %bitcast.100, bf16[512,2560]{1,0:T(8,128)(2,1)} %bitcast.101, bf16[512,2560]{1,0:T(8,128)(2,1)} %bitcast.69.near_value_ref, bf16[1024,2560]{1,0:T(8,128)(2,1)} %bitcast.94, bf16[1024,2560]{1,0:T(8,128)(2,1)} %bitcast.73.far_value_ref, ...), custom_call_target="tpu_custom_call" | custom-call | tf_op jit(solution)/shard_map/pallas_call | solution.py:120
  512.7 4.9 all-to-all-start.5
  517.9 0.7 fusion.45
  518.6 0.7 fusion.47
  519.3 0.7 fusion.44
  520.1 0.7 fusion.46
  520.8 39.9 %compare_and_fusion.5 = (pred[512]{0:T(512)(128)(4,1)S(1)}, s32[512]{0:T(512)S(1)}) fusion(s32[]{:T(128)} %bitcast.63, s32[]{:T(128)} %bitcast.62, s32[]{:T(128)} %bitcast.61, s32[]{:T(128)} %bitcast.60, s32[]{:T(128)} %bitcast.59, s32[]{:T(128)} %bitcast.58, s32[]{:T(128)} %bitcast.57, s32[]{:T(128)} %bitcast.56, s32[]{:T(128)} %bitcast.55, s32[]{:T(128)} %bitcast.54, ...), kind=kLoop, calls=%fused_computation.152 | loop fusion | flops 85504 | bytes 2816 | tf_op jit(solution)/shard_map/jit(_take)/and | solution.py:258
  560.8 5.2 copy.49
  566.0 1.0 gather_fusion.6
  567.0 0.1 copy.48
  567.2 0.7 reshape.786
  567.9 8.4 %all-to-all-done.5 = bf16[16,32,2560]{2,1,0:T(8,128)(2,1)S(1)} async-done(((bf16[16,32,2560]{2,1,0:T(8,128)(2,1)}), bf16[16,32,2560]{2,1,0:T(8,128)(2,1)S(1)}, u32[]{:S(2)}, u32[]{:S(2)}) %all-to-all-start.5) | async-done | bytes 2621472 | tf_op jit(solution)/shard_map/all_to_all | solution.py:205
  576.3 3.5 gather_fusion.16
  579.8 3.7 broadcast_select_fusion.2
  (76 shorter events, 2.5 us)
Async XLA Ops:
  0.6 12.1 %copy-start = (bf16[512,2560]{1,0:T(8,128)(2,1)S(1)}, bf16[512,2560]{1,0:T(8,128)(2,1)}, u32[]{:S(2)}) copy-start(bf16[512,2560]{1,0:T(8,128)(2,1)} %param.16) | copy-start | bytes 7864324
  157.8 5.3 copy-start.3
  157.8 5.6 copy-start.2
  157.8 64.1 %all-to-all-start.2 = ((bf16[16,32,2560]{2,1,0:T(8,128)(2,1)}), bf16[16,32,2560]{2,1,0:T(8,128)(2,1)}, u32[]{:S(2)}, u32[]{:S(2)}) async-start(bf16[16,32,2560]{2,1,0:T(8,128)(2,1)} %bitcast.97), calls=%async_computation.2 | async-start | bytes 5242880 | tf_op jit(solution)/shard_map/all_to_all | solution.py:205
  341.6 120.3 %all-to-all-start.4 = ((bf16[16,64,2560]{2,1,0:T(8,128)(2,1)}), bf16[16,64,2560]{2,1,0:T(8,128)(2,1)}, u32[]{:S(2)}, u32[]{:S(2)}) async-start(bf16[16,64,2560]{2,1,0:T(8,128)(2,1)} %bitcast.95), calls=%async_computation.4 | async-start | bytes 10485760 | tf_op jit(solution)/shard_map/all_to_all | solution.py:205
  512.7 63.6 %all-to-all-start.5 = ((bf16[16,32,2560]{2,1,0:T(8,128)(2,1)}), bf16[16,32,2560]{2,1,0:T(8,128)(2,1)S(1)}, u32[]{:S(2)}, u32[]{:S(2)}) async-start(bf16[16,32,2560]{2,1,0:T(8,128)(2,1)} %bitcast.102), calls=%async_computation.5 | async-start | bytes 5242880 | tf_op jit(solution)/shard_map/all_to_all | solution.py:205
  579.8 3.7 copy-start.1

commit v3 on v2

--- a/solution.py
+++ b/solution.py
@@ -81,20 +81,25 @@
 
 
 FAR_SLOTS = 4
+HEAD_CHUNKS = 2
 
 
 def attention_kernel(
-    query_ref, near_key_ref, near_value_ref, far_key_ref, far_value_ref, near_bias_ref,
+    far_key_ref, far_value_ref, query_ref, near_key_ref, near_value_ref, near_bias_ref,
     far_bias_ref, out_ref, log_ref
 ):
-    query = query_ref[...]
+    def flat(ref):
+        block = ref[...]
+        return block.reshape(block.shape[0] * block.shape[1], block.shape[2])
+
+    query = flat(query_ref)
     dims = (((1,), (1,)), ((), ()))
     scale = HEAD_DIM ** (-0.5)
     near_scores = lax.dot_general(
-        query, near_key_ref[...], dims, preferred_element_type=jnp.float32
+        query, flat(near_key_ref), dims, preferred_element_type=jnp.float32
     ) * scale + near_bias_ref[...]
     far_scores = lax.dot_general(
-        query, far_key_ref[...], dims, preferred_element_type=jnp.float32
+        query, flat(far_key_ref), dims, preferred_element_type=jnp.float32
     ) * scale + far_bias_ref[...]
     row_max = jnp.maximum(
         jnp.max(near_scores, axis=1, keepdims=True), jnp.max(far_scores, axis=1, keepdims=True)
@@ -106,38 +111,41 @@
     inverse = 1.0 / total
     near_weights = (near_exp * inverse).astype(jnp.bfloat16)
     far_weights = (far_exp * inverse).astype(jnp.bfloat16)
-    mixed = jnp.dot(near_weights, near_value_ref[...], preferred_element_type=jnp.float32)
-    mixed = mixed + jnp.dot(far_weights, far_value_ref[...], preferred_element_type=jnp.float32)
-    out_ref[...] = mixed.astype(out_ref.dtype)
+    mixed = jnp.dot(near_weights, flat(near_value_ref), preferred_element_type=jnp.float32)
+    mixed = mixed + jnp.dot(far_weights, flat(far_value_ref), preferred_element_type=jnp.float32)
+    out_ref[...] = mixed.astype(out_ref.dtype).reshape(out_ref.shape)
     log_ref[...] = log_total
 
 
-def attend(query, near_key, near_value, far_key, far_value, near_bias, far_bias):
-    rows, channels = query.shape
-    near = near_key.shape[0]
-    far = far_key.shape[0]
+def attend(got, unit, near_bias, far_bias):
+    group_size, _, channels = got.shape
+    far_rows = FAR_SLOTS * 16
+    rows = group_size * unit
     heads = channels // HEAD_DIM
+    base = 2 * far_rows // unit
+    far_spec = (group_size, far_rows, HEAD_DIM)
+    own_spec = (group_size, unit, HEAD_DIM)
     return pl.pallas_call(
         attention_kernel,
         grid=(heads,),
         in_specs=[
-            pl.BlockSpec((rows, HEAD_DIM), lambda h: (0, h)),
-            pl.BlockSpec((near, HEAD_DIM), lambda h: (0, h)),
-            pl.BlockSpec((near, HEAD_DIM), lambda h: (0, h)),
-            pl.BlockSpec((far, HEAD_DIM), lambda h: (0, h)),
-            pl.BlockSpec((far, HEAD_DIM), lambda h: (0, h)),
-            pl.BlockSpec((rows, near), lambda h: (0, 0)),
-            pl.BlockSpec((rows, far), lambda h: (0, 0)),
+            pl.BlockSpec(far_spec, lambda h: (0, 0, h)),
+            pl.BlockSpec(far_spec, lambda h: (0, 1, h)),
+            pl.BlockSpec(own_spec, lambda h: (0, base, h)),
+            pl.BlockSpec(own_spec, lambda h: (0, base + 1, h)),
+            pl.BlockSpec(own_spec, lambda h: (0, base + 2, h)),
+            pl.BlockSpec((rows, rows), lambda h: (0, 0)),
+            pl.BlockSpec((rows, group_size * far_rows), lambda h: (0, 0)),
         ],
         out_specs=[
-            pl.BlockSpec((rows, HEAD_DIM), lambda h: (0, h)),
+            pl.BlockSpec(own_spec, lambda h: (0, 0, h)),
             pl.BlockSpec((None, rows, 1), lambda h: (h, 0, 0)),
         ],
         out_shape=[
-            jax.ShapeDtypeStruct((rows, channels), jnp.bfloat16),
+            jax.ShapeDtypeStruct((group_size, unit, channels), jnp.bfloat16),
             jax.ShapeDtypeStruct((heads, rows, 1), jnp.float32),
         ],
-    )(query, near_key, near_value, far_key, far_value, near_bias, far_bias)
+    )(got, got, got, got, got, near_bias, far_bias)
 
 
 def class_of(devices, frame_devs):
@@ -162,6 +170,7 @@
     tile_count = owner_map.shape[0]
     own_count = tile_count // group_size
     capacity = (piece_count + group_size - 1) // group_size
+    unit = capacity * 16
     frame_devs = group_size // FRAMES
     devices = jnp.arange(group_size, dtype=jnp.int32)
     local_iota = jnp.arange(piece_count, dtype=jnp.int32)
@@ -188,51 +197,64 @@
         my_slot[None, None, :] == cap_iota[None, :, None]
     )
     send_index = jnp.sum(jnp.where(send_hit, local_iota[None, None, :], 0), axis=2)
-    own_send_rows = piece_rows(send_index).reshape(-1)
+    own_send_rows = piece_rows(send_index).reshape(group_size, unit)
     requests = request_table(owner_map, pattern, group_size)
     wanted = (requests >= 0) & (requests // piece_count == my_class)
     far_send_piece, _ = ranked_pick(requests % piece_count, wanted, FAR_SLOTS)
-    far_send_rows = piece_rows(far_send_piece).reshape(-1)
-    own_shape = (group_size, capacity * 16, channels)
-    far_shape = (group_size, FAR_SLOTS * 16, channels)
-    sent_query = jnp.take(query_feats, own_send_rows, axis=0).reshape(own_shape)
-    sent_key = jnp.take(key_feats, own_send_rows, axis=0).reshape(own_shape)
-    sent_value = jnp.take(value_feats, own_send_rows, axis=0).reshape(own_shape)
-    sent_far_key = jnp.take(key_feats, far_send_rows, axis=0).reshape(far_shape)
-    sent_far_value = jnp.take(value_feats, far_send_rows, axis=0).reshape(far_shape)
-
-    def exchange(sent):
-        got = lax.all_to_all(sent, "seq", split_axis=0, concat_axis=0, tiled=True)
-        return got.reshape(-1, channels)
-
-    got_query = exchange(sent_query)
-    got_key = exchange(sent_key)
-    got_value = exchange(sent_value)
-    got_far_key = exchange(sent_far_key)
-    got_far_value = exchange(sent_far_value)
+    far_send_rows = piece_rows(far_send_piece).reshape(group_size, FAR_SLOTS * 16)
+    send_rows = jnp.concatenate(
+        [
+            far_send_rows + local_rows,
+            far_send_rows + 2 * local_rows,
+            own_send_rows,
+            own_send_rows + local_rows,
+            own_send_rows + 2 * local_rows,
+        ],
+        axis=1,
+    ).reshape(-1)
     source_class = class_of(devices, frame_devs)
     class_tiles = source_class[:, None] * piece_count + local_iota[None, :]
     mine = jnp.take(owner_map, class_tiles) == device
-    near_hit = mine[:, None, :] & (jnp.take(class_rank, class_tiles)[:, None, :] == cap_iota[None, :, None])
+    near_hit = mine[:, None, :] & (
+        jnp.take(class_rank, class_tiles)[:, None, :] == cap_iota[None, :, None]
+    )
     near_tile = jnp.sum(jnp.where(near_hit, class_tiles[:, None, :], 0), axis=2)
     near_tile_rows = jnp.broadcast_to(near_tile[:, :, None], (group_size, capacity, 16)).reshape(-1)
     my_requests = jnp.take(requests, device, axis=0)
-    far_wanted = (my_requests[None, :] >= 0) & (my_requests[None, :] // piece_count == source_class[:, None])
+    far_wanted = (my_requests[None, :] >= 0) & (
+        my_requests[None, :] // piece_count == source_class[:, None]
+    )
     far_tile, far_valid = ranked_pick(
         jnp.broadcast_to(my_requests[None, :], (group_size, group_size)), far_wanted, FAR_SLOTS
     )
     far_tile = jnp.where(far_valid, far_tile, -1)
-    far_tile_rows = jnp.broadcast_to(far_tile[:, :, None], (group_size, FAR_SLOTS, 16)).reshape(-1)
+    far_tile_rows = jnp.broadcast_to(
+        far_tile[:, :, None], (group_size, FAR_SLOTS, 16)
+    ).reshape(-1)
     own_ids = owned_tiles(owner_map, own_rank, device, own_count)
     listed = jnp.take(pattern, own_ids, axis=0)
     near_ok = jnp.any(listed[:, :, None] == near_tile_rows[None, None, :], axis=1)
     far_ok = jnp.any(listed[:, :, None] == far_tile_rows[None, None, :], axis=1)
     query_own = jnp.take(own_rank, near_tile_rows)
-    near_bias = jnp.where(jnp.take(near_ok, query_own, axis=0), 0.0, masked_score).astype(jnp.float32)
-    far_bias = jnp.where(jnp.take(far_ok, query_own, axis=0), 0.0, masked_score).astype(jnp.float32)
-    mixed_rows, head_logs = attend(
-        got_query, got_key, got_value, got_far_key, got_far_value, near_bias, far_bias
-    )
+    near_bias = jnp.where(jnp.take(near_ok, query_own, axis=0), 0.0, masked_score)
+    far_bias = jnp.where(jnp.take(far_ok, query_own, axis=0), 0.0, masked_score)
+    near_bias = near_bias.astype(jnp.float32)
+    far_bias = far_bias.astype(jnp.float32)
+    chunk_width = channels // HEAD_CHUNKS
+    outputs = []
+    logs = []
+    for chunk in range(HEAD_CHUNKS):
+        columns = slice(chunk * chunk_width, (chunk + 1) * chunk_width)
+        stacked = jnp.concatenate(
+            [query_feats[:, columns], key_feats[:, columns], value_feats[:, columns]], axis=0
+        )
+        sent = jnp.take(stacked, send_rows, axis=0).reshape(group_size, -1, chunk_width)
+        got = lax.all_to_all(sent, "seq", split_axis=0, concat_axis=0, tiled=True)
+        mixed, head_logs = attend(got, unit, near_bias, far_bias)
+        returned = lax.all_to_all(mixed, "seq", split_axis=0, concat_axis=0, tiled=True)
+        outputs.append(returned.reshape(-1, chunk_width))
+        logs.append(head_logs[:, :, 0])
+    head_logs = jnp.concatenate(logs, axis=0)
     own_class = own_ids // piece_count
     own_slot = jnp.take(class_rank, own_ids)
     gather_rows = (
@@ -242,12 +264,11 @@
     log_rows = (gather_rows[:, :, None] * 16 + token_iota).reshape(-1)
     heads = channels // HEAD_DIM
     log_sums = (
-        jnp.take(head_logs[:, :, 0], log_rows, axis=1)
+        jnp.take(head_logs, log_rows, axis=1)
         .reshape(heads, own_count, 64)
         .transpose(1, 0, 2)
         .reshape(1, own_count, heads * 64)
     )
-    returned = exchange(mixed_rows.reshape(own_shape))
     local_iota_rows = jnp.arange(local_rows, dtype=jnp.int32)
     strip = local_iota_rows // (4 * WIDTH)
     height = local_iota_rows % (4 * WIDTH) // WIDTH
@@ -255,7 +276,7 @@
     piece = strip * blocks + column // 4
     token = height * 4 + column % 4
     back_rows = (jnp.take(my_owner, piece) * capacity + jnp.take(my_slot, piece)) * 16 + token
-    attended = jnp.take(returned, back_rows, axis=0)
+    attended = jnp.take(jnp.concatenate(outputs, axis=1), back_rows, axis=0)
     return (attended, log_sums)
 
 

time: 585 us -> 601 us (1.027)
  blocking collectives: 248 us -> 205 us
  waiting for transfers between devices: 114 us -> 155 us
  other arithmetic: 64.1 us -> 73.5 us
    all_to_all x3 -> x1, blocking collectives: 248 us -> 205 us  [shards(): got = lax.all_to_all(sent, 'seq', split_axis=0, concat_axis=0, tiled=True)]
    all_to_all x3, waiting for transfers between devices: 114 us -> 155 us  [the longest x1 151 us: shards(): got = lax.all_to_all(sent, 'seq', split_axis=0, concat_axis=0, tiled=True)]
    gather x9 -> x6, local copies, waits for them, and re-layouts: 45.3 us -> 50.2 us  [the longest x2 43.6 us: shards(): jnp.take(stacked, send_rows, axis=0).reshape(group_size, -1, chunk_width)]
    pallas_call x1 -> x2, Pallas kernels: 50.8 us -> 53.8 us  [attend(): pl.pallas_call(attention_kernel, grid=(heads,), in_specs=[pl.BlockSpec(fa...]
    select_n x6 -> x5, other arithmetic: 19.4 us -> 17.2 us  [the longest x2 12 us: shards(): jnp.take(stacked, send_rows, axis=0).reshape(group_size, -1, chunk_width)]
    and x4 -> x3, other arithmetic: 40 us -> 39.9 us  [the longest x1 39.9 us: shards(): attended = jnp.take(jnp.concatenate(outputs, axis=1), back_rows, axis=0)]
  transfers between devices with their start and end apart: 3 -> 3, of which waited for: 3 -> 2; matrix products, arithmetic and copies ran while one was open for 20% -> 12% of each run, Pallas kernels for 0% -> 9%
where the time goes in v3:
time: 601 us; the launch traced here: 599 us
  blocking collectives  205 us (34%)
  waiting for transfers between devices  155 us (26%)
  local copies, waits for them, and re-layouts  94 us (16%)
  other arithmetic  73.5 us (12%)
  Pallas kernels  53.8 us (9%)
  starting transfers between devices  15.6 us (3%)
    all_to_all x1, blocking collectives, shards(): got = lax.all_to_all(sent, 'seq', split_axis=0, concat_axis=0, tiled=True)  205 us
    all_to_all x1, waiting for transfers between devices, shards(): got = lax.all_to_all(sent, 'seq', split_axis=0, concat_axis=0, tiled=True)  151 us
    pallas_call x2, Pallas kernels, attend(): pl.pallas_call(attention_kernel, grid=(heads,), in_specs=[pl.BlockSpec(fa...  53.8 us
    gather x2, local copies, waits for them, and re-layouts, shards(): jnp.take(stacked, send_rows, axis=0).reshape(group_size, -1, chunk_width)  43.6 us
    and x1, other arithmetic, shards(): attended = jnp.take(jnp.concatenate(outputs, axis=1), back_rows, axis=0)  39.9 us
    gather x3, local copies, waits for them, and re-layouts, request_table(): entry_owner = jnp.take(owner_map, pattern)  17.1 us
    select_n x2, other arithmetic, shards(): jnp.take(stacked, send_rows, axis=0).reshape(group_size, -1, chunk_width)  12 us
  transfers between devices with their start and end apart: 3, of which 2 were waited for; matrix products, arithmetic and copies ran while one was open for 12% of the time, Pallas kernels for 9%

profile of v3, /device:TPU:13, one launch (start us, length us, event | category | flops | bytes accessed | tf_op | source)
XLA Modules:
  0.0 598.5 jit_solution(15913261681288926050)
XLA Ops:
  0.7 0.7 iota_compare_fusion.7
  1.4 0.7 eq.240
  2.1 0.7 compare_select_fusion.1
  2.8 0.1 copy.44
  2.9 0.2 reshape.911
  3.2 16.9 %gather_fusion = s32[2944]{0:T(1024)S(1)} fusion(s32[128]{0:T(128)S(1)} %copy-done, s32[3072]{0:T(1024)S(1)} %pad_clamp_fusion.1), kind=kCustom, calls=%fused_computation.6 | custom fusion | bytes 35328 | tf_op jit(solution)/shard_map/jit(_take)/gather | solution.py:52
  20.1 0.2 reshape.910
  20.5 0.3 select_reduce_fusion.1
  20.8 0.2 reduce_window_sum.28
  21.0 0.1 select_reduce_fusion.4
  21.9 0.2 convert_reduce_fusion
  22.2 0.7 gather_fusion.8
  22.9 0.7 gather_fusion.9
  23.6 0.1 select_reduce_fusion.6
  24.7 0.2 fusion.43
  24.9 1.6 copy-done.4
  26.4 0.2 fusion.44
  26.6 1.6 copy-done.5
  28.2 0.2 fusion.45
  28.3 3.6 pad_maximum_fusion
  31.9 21.8 %gather_fusion.13 = bf16[3584,1280]{1,0:T(8,128)(2,1)} fusion(bf16[1536,1280]{1,0:T(8,128)(2,1)} %get-tuple-element.121, s32[4096]{0:T(1024)S(1)} %pad_clamp_fusion), kind=kCustom, calls=%fused_computation.4.clone | custom fusion | bytes 18364416 | tf_op jit(solution)/shard_map/jit(_take)/gather | solution.py:251
  53.7 21.8 %gather_fusion.10 = bf16[3584,1280]{1,0:T(8,128)(2,1)} fusion(bf16[1536,1280]{1,0:T(8,128)(2,1)} %get-tuple-element.120, s32[4096]{0:T(1024)S(1)} %pad_clamp_fusion), kind=kCustom, calls=%fused_computation.1.clone | custom fusion | bytes 18364416 | tf_op jit(solution)/shard_map/jit(_take)/gather | solution.py:251
  75.5 12.0 %broadcast_select_fusion.1 = (bf16[3584,1280]{1,0:T(8,128)(2,1)S(1)}, bf16[3584,1280]{1,0:T(8,128)(2,1)}) fusion(bf16[3584,1280]{1,0:T(8,128)(2,1)} %gather_fusion.10, pred[3584]{0:T(1024)(128)(4,1)S(1)} %compare_and_fusion, bf16[3584,1280]{1,0:T(8,128)(2,1)} %gather_fusion.13), kind=kLoop, calls=%fused_computation.15 | loop fusion | flops 9175040 | bytes 36703744 | tf_op jit(solution)/shard_map/jit(_take)/select_n | solution.py:251
  87.5 205.4 %all_to_all.20.far_key_ref.far_value_ref.query_ref.near_key_ref.near_value_ref = bf16[16,224,1280]{2,1,0:T(8,128)(2,1)} all-to-all(bf16[16,224,1280]{2,1,0:T(8,128)(2,1)S(1)} %bitcast.85), channel_id=1, replica_groups=mesh['groups'=2,'seq'=16] {'seq'}, dimensions={0} | all-to-all | bytes 18350080 | tf_op jit(solution)/shard_map/all_to_all | solution.py:252
  293.0 5.8 all-to-all-start.2
  299.0 3.3 gather_fusion.11
  302.4 3.3 gather_fusion.12
  306.0 0.1 select_reduce_fusion.5
  306.6 0.2 reduce_window_sum.30
  306.8 0.1 fusion.4
  307.0 0.2 select_reduce_fusion.3
  307.5 0.2 reduce_window_sum.29
  307.7 0.2 select_reduce_fusion.2
  307.9 0.1 select_reduce_fusion.7
  308.0 0.6 gather_fusion.6
  308.6 0.6 gather_fusion.2
  309.4 3.3 gather_fusion.1
  312.8 0.2 compare_reduce_fusion
  313.0 1.9 gather_fusion.4
  314.9 0.1 compare_reduce_fusion.1
  315.0 1.8 gather_fusion.3
  316.8 1.2 select_select_fusion.1.near_bias_ref
  318.0 1.6 select_select_fusion.far_bias_ref
  319.6 26.9 %shard_map.68 = (bf16[16,32,1280]{2,1,0:T(8,128)(2,1)}, f32[10,512,1]{2,1,0:T(8,128)}) custom-call(bf16[16,224,1280]{2,1,0:T(8,128)(2,1)} %all_to_all.20.far_key_ref.far_value_ref.query_ref.near_key_ref.near_value_ref, bf16[16,224,1280]{2,1,0:T(8,128)(2,1)} %all_to_all.20.far_key_ref.far_value_ref.query_ref.near_key_ref.near_value_ref, ...), custom_call_target="tpu_custom_call" | custom-call | tf_op jit(solution)/shard_map/pallas_call | solution.py:128
  346.5 151.4 %all-to-all-done.2.far_key_ref.far_value_ref.query_ref.near_key_ref.near_value_ref = bf16[16,224,1280]{2,1,0:T(8,128)(2,1)} async-done(((bf16[16,224,1280]{2,1,0:T(8,128)(2,1)}), bf16[16,224,1280]{2,1,0:T(8,128)(2,1)}, u32[]{:S(2)}, u32[]{:S(2)}) %all-to-all-start.2) | async-done | bytes 9175072 | tf_op jit(solution)/shard_map/all_to_all | solution.py:252
  498.0 4.9 all-to-all-start.1
  502.9 26.9 %shard_map.69 = (bf16[16,32,1280]{2,1,0:T(8,128)(2,1)}, f32[10,512,1]{2,1,0:T(8,128)}) custom-call(bf16[16,224,1280]{2,1,0:T(8,128)(2,1)} %all-to-all-done.2.far_key_ref.far_value_ref.query_ref.near_key_ref.near_value_ref, bf16[16,224,1280]{2,1,0:T(8,128)(2,1)} %all-to-all-done.2.far_key_ref.far_value_ref.query_ref.near_key_ref.near_value_ref, ...), custom_call_target="tpu_custom_call" | custom-call | tf_op jit(solution)/shard_map/pallas_call | solution.py:128
  529.8 3.7 all-to-all-done.1
  533.4 4.9 all-to-all-start.3
  538.6 0.7 fusion.47
  539.3 0.7 fusion.49
  540.0 0.7 fusion.46
  540.8 0.7 fusion.48
  541.5 39.9 %compare_and_fusion.8 = (pred[512]{0:T(512)(128)(4,1)S(1)}, s32[512]{0:T(512)S(1)}) fusion(s32[]{:T(128)} %bitcast.63, s32[]{:T(128)} %bitcast.62, s32[]{:T(128)} %bitcast.61, s32[]{:T(128)} %bitcast.60, s32[]{:T(128)} %bitcast.59, s32[]{:T(128)} %bitcast.58, s32[]{:T(128)} %bitcast.57, s32[]{:T(128)} %bitcast.56, s32[]{:T(128)} %bitcast.55, s32[]{:T(128)} %bitcast.54, ...), kind=kLoop, calls=%fused_computation.161 | loop fusion | flops 85504 | bytes 2816 | tf_op jit(solution)/shard_map/jit(_take)/and | solution.py:279
  581.4 2.5 reduce
  583.9 2.5 reduce.1
  586.5 0.1 copy.55
  586.6 1.0 gather_fusion.7
  587.6 0.1 copy.56
  587.8 0.7 reshape.752
  588.5 1.1 copy-done.2
  589.6 1.9 pad_maximum_fusion.2
  591.5 3.5 gather_fusion.5
  595.0 3.5 broadcast_select_fusion.2
  (101 shorter events, 4.0 us)
Async XLA Ops:
  0.6 2.5 copy-start
  3.2 17.2 %copy-start.6 = (s32[128,23]{0,1:T(8,128)S(1)}, s32[128,23]{0,1:T(8,128)}, u32[]{:S(2)}) copy-start(s32[128,23]{0,1:T(8,128)} %param.17) | copy-start | bytes 35332
  3.2 21.5 %copy-start.3 = (bf16[512,2560]{1,0:T(8,128)(2,1)S(1)}, bf16[512,2560]{1,0:T(8,128)(2,1)}, u32[]{:S(2)}) copy-start(bf16[512,2560]{1,0:T(8,128)(2,1)} %param.13) | copy-start | bytes 7864324
  24.7 1.7 copy-start.4
  26.4 1.7 copy-start.5
  293.0 205.0 %all-to-all-start.2 = ((bf16[16,224,1280]{2,1,0:T(8,128)(2,1)}), bf16[16,224,1280]{2,1,0:T(8,128)(2,1)}, u32[]{:S(2)}, u32[]{:S(2)}) async-start(bf16[16,224,1280]{2,1,0:T(8,128)(2,1)} %bitcast.84), calls=%async_computation.2 | async-start | bytes 18350080 | tf_op jit(solution)/shard_map/all_to_all | solution.py:252
  498.0 35.5 %all-to-all-start.1 = ((bf16[16,32,1280]{2,1,0:T(8,128)(2,1)}), bf16[16,32,1280]{2,1,0:T(8,128)(2,1)S(1)}, u32[]{:S(2)}, u32[]{:S(2)}) async-start(bf16[16,32,1280]{2,1,0:T(8,128)(2,1)} %get-tuple-element.10), calls=%async_computation.1 | async-start | bytes 2621440 | tf_op jit(solution)/shard_map/all_to_all | solution.py:254
  533.4 50.5 %copy-start.1 = (bf16[16,32,1280]{2,1,0:T(8,128)(2,1)}, bf16[16,32,1280]{2,1,0:T(8,128)(2,1)S(1)}, u32[]{:S(2)}) copy-start(bf16[16,32,1280]{2,1,0:T(8,128)(2,1)S(1)} %all-to-all-done.1) | copy-start | bytes 3932164
  533.4 55.1 %all-to-all-start.3 = ((bf16[16,32,1280]{2,1,0:T(8,128)(2,1)}), bf16[16,32,1280]{2,1,0:T(8,128)(2,1)S(1)}, u32[]{:S(2)}, u32[]{:S(2)}) async-start(bf16[16,32,1280]{2,1,0:T(8,128)(2,1)} %get-tuple-element.11), calls=%async_computation.3 | async-start | bytes 2621440 | tf_op jit(solution)/shard_map/all_to_all | solution.py:254
  588.5 1.1 copy-start.2

commit v4 on v3

--- a/solution.py
+++ b/solution.py
@@ -202,16 +202,6 @@
     wanted = (requests >= 0) & (requests // piece_count == my_class)
     far_send_piece, _ = ranked_pick(requests % piece_count, wanted, FAR_SLOTS)
     far_send_rows = piece_rows(far_send_piece).reshape(group_size, FAR_SLOTS * 16)
-    send_rows = jnp.concatenate(
-        [
-            far_send_rows + local_rows,
-            far_send_rows + 2 * local_rows,
-            own_send_rows,
-            own_send_rows + local_rows,
-            own_send_rows + 2 * local_rows,
-        ],
-        axis=1,
-    ).reshape(-1)
     source_class = class_of(devices, frame_devs)
     class_tiles = source_class[:, None] * piece_count + local_iota[None, :]
     mine = jnp.take(owner_map, class_tiles) == device
@@ -243,12 +233,18 @@
     chunk_width = channels // HEAD_CHUNKS
     outputs = []
     logs = []
+    taken = lax.optimization_barrier(
+        (
+            jnp.take(key_feats, far_send_rows.reshape(-1), axis=0).reshape(group_size, -1, channels),
+            jnp.take(value_feats, far_send_rows.reshape(-1), axis=0).reshape(group_size, -1, channels),
+            jnp.take(query_feats, own_send_rows.reshape(-1), axis=0).reshape(group_size, -1, channels),
+            jnp.take(key_feats, own_send_rows.reshape(-1), axis=0).reshape(group_size, -1, channels),
+            jnp.take(value_feats, own_send_rows.reshape(-1), axis=0).reshape(group_size, -1, channels),
+        )
+    )
     for chunk in range(HEAD_CHUNKS):
         columns = slice(chunk * chunk_width, (chunk + 1) * chunk_width)
-        stacked = jnp.concatenate(
-            [query_feats[:, columns], key_feats[:, columns], value_feats[:, columns]], axis=0
-        )
-        sent = jnp.take(stacked, send_rows, axis=0).reshape(group_size, -1, chunk_width)
+        sent = jnp.concatenate([part[:, :, columns] for part in taken], axis=1)
         got = lax.all_to_all(sent, "seq", split_axis=0, concat_axis=0, tiled=True)
         mixed, head_logs = attend(got, unit, near_bias, far_bias)
         returned = lax.all_to_all(mixed, "seq", split_axis=0, concat_axis=0, tiled=True)

time: 601 us -> 591 us (0.983)
    gather x2 -> x5, local copies, waits for them, and re-layouts: 43.6 us -> 34.2 us  [the longest x1 12.5 us: shards(): jnp.take(value_feats, far_send_rows.reshape(-1), axis=0)]
    unnamed x15 -> x31, local copies, waits for them, and re-layouts: 4.31 us -> 10.6 us
    select_n x2 -> x3, other arithmetic: 12 us -> 9.48 us  [the longest x1 6.03 us: shards(): jnp.take(value_feats, far_send_rows.reshape(-1), axis=0)]
where the time goes in v4:
time: 591 us; the launch traced here: 589 us
  blocking collectives  205 us (35%)
  waiting for transfers between devices  155 us (26%)
  local copies, waits for them, and re-layouts  90.6 us (15%)
  other arithmetic  67.8 us (11%)
  Pallas kernels  53.8 us (9%)
  starting transfers between devices  15.6 us (3%)
    all_to_all x1, blocking collectives, shards(): got = lax.all_to_all(sent, 'seq', split_axis=0, concat_axis=0, tiled=True)  205 us
    all_to_all x1, waiting for transfers between devices, shards(): got = lax.all_to_all(sent, 'seq', split_axis=0, concat_axis=0, tiled=True)  151 us
    pallas_call x2, Pallas kernels, attend(): pl.pallas_call(attention_kernel, grid=(heads,), in_specs=[pl.BlockSpec(fa...  53.8 us
    and x1, other arithmetic, shards(): attended = jnp.take(jnp.concatenate(outputs, axis=1), back_rows, axis=0)  39.9 us
    gather x3, local copies, waits for them, and re-layouts, request_table(): entry_owner = jnp.take(owner_map, pattern)  17.1 us
    gather x1, local copies, waits for them, and re-layouts, shards(): jnp.take(value_feats, far_send_rows.reshape(-1), axis=0)  12.5 us
  transfers between devices with their start and end apart: 3, of which 2 were waited for; matrix products, arithmetic and copies ran while one was open for 12% of the time, Pallas kernels for 9%

profile of v4, /device:TPU:13, one launch (start us, length us, event | category | flops | bytes accessed | tf_op | source)
XLA Modules:
  0.0 589.2 jit_solution(11164873354091697438)
XLA Ops:
  0.7 0.8 iota_compare_fusion.7
  1.5 0.7 eq.254
  2.3 0.7 compare_select_fusion
  3.1 0.2 reshape.955
  3.3 16.9 %gather_fusion = s32[2944]{0:T(1024)S(1)} fusion(s32[128]{0:T(128)S(1)} %copy-done.2, s32[3072]{0:T(1024)S(1)} %pad_clamp_fusion), kind=kCustom, calls=%fused_computation.10 | custom fusion | bytes 35328 | tf_op jit(solution)/shard_map/jit(_take)/gather | solution.py:52
  20.2 0.2 reshape.954
  20.6 0.3 select_reduce_fusion.1
  21.0 0.2 reduce_window_sum.28
  21.1 0.1 select_reduce_fusion.4
  21.7 0.7 gather_fusion.9
  22.4 0.2 convert_reduce_fusion
  22.7 0.7 gather_fusion.10
  24.0 6.3 %gather_fusion.7 = bf16[1024,2560]{1,0:T(8,128)(2,1)} fusion(bf16[512,2560]{1,0:T(8,128)(2,1)S(1)} %copy-done, s32[1024]{0:T(1024)S(1)} %get-tuple-element.137), kind=kCustom, calls=%fused_computation.clone | custom fusion | bytes 10489856 | tf_op jit(solution)/shard_map/jit(_take)/gather | solution.py:238
  30.3 12.5 %gather_fusion.8 = bf16[1024,2560]{1,0:T(8,128)(2,1)} fusion(bf16[512,2560]{1,0:T(8,128)(2,1)} %param.17, s32[1024]{0:T(1024)S(1)} %get-tuple-element.137), kind=kCustom, calls=%fused_computation.4.clone | custom fusion | bytes 10489856 | tf_op jit(solution)/shard_map/jit(_take)/gather | solution.py:239
  42.8 3.5 gather_fusion.12
  46.4 8.3 %gather_fusion.13 = bf16[512,2560]{1,0:T(8,128)(2,1)} fusion(bf16[512,2560]{1,0:T(8,128)(2,1)} %param.17, s32[1024]{0:T(1024)S(1)} %get-tuple-element.136), kind=kCustom, calls=%fused_computation.7.clone | custom fusion | bytes 5244928 | tf_op jit(solution)/shard_map/jit(_take)/gather | solution.py:242
  54.7 3.5 gather_fusion.11
  58.2 6.0 %broadcast_select_fusion = (bf16[1024,2560]{1,0:T(8,128)(2,1)S(1)}, bf16[1024,2560]{1,0:T(8,128)(2,1)S(1)}) fusion(bf16[1024,2560]{1,0:T(8,128)(2,1)} %gather_fusion.8, pred[1024]{0:T(1024)(128)(4,1)S(1)} %compare_and_fusion.3, bf16[1024,2560]{1,0:T(8,128)(2,1)} %gather_fusion.7), kind=kLoop, calls=%fused_computation.17 | loop fusion | flops 5242880 | bytes 20972544 | tf_op jit(solution)/shard_map/jit(_take)/select_n | solution.py:239
  64.3 0.3 copy-done.6
  64.6 3.4 broadcast_select_fusion.3
  68.0 2.0 slice_dynamic-update-slice_fusion.3
  70.0 1.9 slice_dynamic-update-slice_fusion.2
  71.9 0.7 copy-done.9
  72.6 1.3 slice_dynamic-update-slice_fusion.9
  73.9 0.9 copy-done.8
  74.9 1.3 slice_dynamic-update-slice_fusion.8
  76.2 0.9 copy-done.7
  77.1 1.3 slice_dynamic-update-slice_fusion.7
  78.4 205.4 %all_to_all.20.far_key_ref.far_value_ref.query_ref.near_key_ref.near_value_ref = bf16[16,224,1280]{2,1,0:T(8,128)(2,1)} all-to-all(bf16[16,224,1280]{2,1,0:T(8,128)(2,1)S(1)} %get-tuple-element.50), channel_id=1, replica_groups=mesh['groups'=2,'seq'=16] {'seq'}, dimensions={0} | all-to-all | bytes 18350080 | tf_op jit(solution)/shard_map/all_to_all | solution.py:248
  283.8 5.8 all-to-all-start.2
  289.9 3.3 gather_fusion.14
  293.2 3.3 gather_fusion.15
  297.5 0.2 reduce_window_sum.30
  297.6 0.1 fusion.4
  297.8 0.2 select_reduce_fusion.3
  298.3 0.2 reduce_window_sum.29
  298.5 0.2 select_reduce_fusion.2
  298.8 0.6 gather_fusion.5
  299.5 0.6 gather_fusion.2
  300.2 3.3 gather_fusion.1
  303.9 0.2 compare_reduce_fusion
  304.0 1.9 gather_fusion.4
  306.1 1.8 gather_fusion.3
  307.9 1.2 select_select_fusion.1.near_bias_ref
  309.1 1.6 select_select_fusion.far_bias_ref
  310.7 26.9 %shard_map.68 = (bf16[16,32,1280]{2,1,0:T(8,128)(2,1)}, f32[10,512,1]{2,1,0:T(8,128)}) custom-call(bf16[16,224,1280]{2,1,0:T(8,128)(2,1)} %all_to_all.20.far_key_ref.far_value_ref.query_ref.near_key_ref.near_value_ref, bf16[16,224,1280]{2,1,0:T(8,128)(2,1)} %all_to_all.20.far_key_ref.far_value_ref.query_ref.near_key_ref.near_value_ref, ...), custom_call_target="tpu_custom_call" | custom-call | tf_op jit(solution)/shard_map/pallas_call | solution.py:128
  337.6 151.2 %all-to-all-done.2.far_key_ref.far_value_ref.query_ref.near_key_ref.near_value_ref = bf16[16,224,1280]{2,1,0:T(8,128)(2,1)} async-done(((bf16[16,224,1280]{2,1,0:T(8,128)(2,1)}), bf16[16,224,1280]{2,1,0:T(8,128)(2,1)}, u32[]{:S(2)}, u32[]{:S(2)}) %all-to-all-start.2) | async-done | bytes 9175072 | tf_op jit(solution)/shard_map/all_to_all | solution.py:248
  488.8 4.9 all-to-all-start.1
  493.7 26.9 %shard_map.69 = (bf16[16,32,1280]{2,1,0:T(8,128)(2,1)}, f32[10,512,1]{2,1,0:T(8,128)}) custom-call(bf16[16,224,1280]{2,1,0:T(8,128)(2,1)} %all-to-all-done.2.far_key_ref.far_value_ref.query_ref.near_key_ref.near_value_ref, bf16[16,224,1280]{2,1,0:T(8,128)(2,1)} %all-to-all-done.2.far_key_ref.far_value_ref.query_ref.near_key_ref.near_value_ref, ...), custom_call_target="tpu_custom_call" | custom-call | tf_op jit(solution)/shard_map/pallas_call | solution.py:128
  520.6 3.7 all-to-all-done.1
  524.3 4.9 all-to-all-start.3
  529.2 0.7 fusion.45
  529.9 0.7 fusion.47
  530.6 0.7 fusion.44
  531.3 0.7 fusion.46
  532.1 39.9 %compare_and_fusion.5 = (pred[512]{0:T(512)(128)(4,1)S(1)}, s32[512]{0:T(512)S(1)}) fusion(s32[]{:T(128)} %bitcast.63, s32[]{:T(128)} %bitcast.62, s32[]{:T(128)} %bitcast.61, s32[]{:T(128)} %bitcast.60, s32[]{:T(128)} %bitcast.59, s32[]{:T(128)} %bitcast.58, s32[]{:T(128)} %bitcast.57, s32[]{:T(128)} %bitcast.56, s32[]{:T(128)} %bitcast.55, s32[]{:T(128)} %bitcast.54, ...), kind=kLoop, calls=%fused_computation.164 | loop fusion | flops 85504 | bytes 2816 | tf_op jit(solution)/shard_map/jit(_take)/and | solution.py:275
  572.0 2.5 reduce
  574.5 2.5 reduce.1
  577.1 1.0 gather_fusion.6
  578.4 0.7 reshape.764
  579.1 1.1 copy-done.11
  580.1 1.9 pad_maximum_fusion
  582.0 3.5 gather_fusion.16
  585.5 3.7 broadcast_select_fusion.2
  (103 shorter events, 4.0 us)
Async XLA Ops:
  0.6 23.4 %copy-start = (bf16[512,2560]{1,0:T(8,128)(2,1)S(1)}, bf16[512,2560]{1,0:T(8,128)(2,1)}, u32[]{:S(2)}) copy-start(bf16[512,2560]{1,0:T(8,128)(2,1)} %param.16) | copy-start | bytes 7864324
  0.6 2.6 copy-start.2
  3.3 17.2 %copy-start.12 = (s32[128,23]{0,1:T(8,128)S(1)}, s32[128,23]{0,1:T(8,128)}, u32[]{:S(2)}) copy-start(s32[128,23]{0,1:T(8,128)} %param.19) | copy-start | bytes 35332
  46.4 8.3 %copy-start.3 = (bf16[512,2560]{1,0:T(8,128)(2,1)S(1)}, bf16[512,2560]{1,0:T(8,128)(2,1)}, u32[]{:S(2)}) copy-start(bf16[512,2560]{1,0:T(8,128)(2,1)} %param.15) | copy-start | bytes 7864324
  58.2 6.0 %copy-start.4 = (bf16[512,2560]{1,0:T(8,128)(2,1)S(1)}, bf16[512,2560]{1,0:T(8,128)(2,1)}, u32[]{:S(2)}) copy-start(bf16[512,2560]{1,0:T(8,128)(2,1)} %gather_fusion.12) | copy-start | bytes 7864324
  58.2 6.1 %copy-start.5 = (bf16[512,2560]{1,0:T(8,128)(2,1)S(1)}, bf16[512,2560]{1,0:T(8,128)(2,1)}, u32[]{:S(2)}) copy-start(bf16[512,2560]{1,0:T(8,128)(2,1)} %gather_fusion.13) | copy-start | bytes 7864324
  58.2 6.4 %copy-start.6 = (bf16[512,2560]{1,0:T(8,128)(2,1)S(1)}, bf16[512,2560]{1,0:T(8,128)(2,1)}, u32[]{:S(2)}) copy-start(bf16[512,2560]{1,0:T(8,128)(2,1)} %gather_fusion.11) | copy-start | bytes 7864324
  70.0 2.6 copy-start.9
  72.6 2.2 copy-start.8
  74.9 2.2 copy-start.7
  283.8 205.0 %all-to-all-start.2 = ((bf16[16,224,1280]{2,1,0:T(8,128)(2,1)}), bf16[16,224,1280]{2,1,0:T(8,128)(2,1)}, u32[]{:S(2)}, u32[]{:S(2)}) async-start(bf16[16,224,1280]{2,1,0:T(8,128)(2,1)} %get-tuple-element.51), calls=%async_computation.2 | async-start | bytes 18350080 | tf_op jit(solution)/shard_map/all_to_all | solution.py:248
  488.8 35.5 %all-to-all-start.1 = ((bf16[16,32,1280]{2,1,0:T(8,128)(2,1)}), bf16[16,32,1280]{2,1,0:T(8,128)(2,1)S(1)}, u32[]{:S(2)}, u32[]{:S(2)}) async-start(bf16[16,32,1280]{2,1,0:T(8,128)(2,1)} %get-tuple-element.21), calls=%async_computation.1 | async-start | bytes 2621440 | tf_op jit(solution)/shard_map/all_to_all | solution.py:250
  524.3 50.2 %copy-start.10 = (bf16[16,32,1280]{2,1,0:T(8,128)(2,1)}, bf16[16,32,1280]{2,1,0:T(8,128)(2,1)S(1)}, u32[]{:S(2)}) copy-start(bf16[16,32,1280]{2,1,0:T(8,128)(2,1)S(1)} %all-to-all-done.1) | copy-start | bytes 3932164
  524.3 54.8 %all-to-all-start.3 = ((bf16[16,32,1280]{2,1,0:T(8,128)(2,1)}), bf16[16,32,1280]{2,1,0:T(8,128)(2,1)S(1)}, u32[]{:S(2)}, u32[]{:S(2)}) async-start(bf16[16,32,1280]{2,1,0:T(8,128)(2,1)} %get-tuple-element.22), calls=%async_computation.3 | async-start | bytes 2621440 | tf_op jit(solution)/shard_map/all_to_all | solution.py:250
  579.1 1.1 copy-start.11
  585.5 3.7 copy-start.1

commit v5 on v4

--- a/solution.py
+++ b/solution.py
@@ -47,9 +47,21 @@
     return jnp.sum(jnp.where(match_rows, tile_iota[None, :], 0), axis=1)
 
 
+def pick(table, index):
+    iota = jnp.arange(table.shape[0], dtype=jnp.int32)
+    hit = index[..., None] == iota
+    return jnp.sum(jnp.where(hit, table, 0), axis=-1).astype(table.dtype)
+
+
+def pick_rows(table, index):
+    iota = jnp.arange(table.shape[0], dtype=jnp.int32)
+    hit = (index[..., None] == iota)[..., None]
+    return jnp.sum(jnp.where(hit, table, 0), axis=-2).astype(table.dtype)
+
+
 def request_table(owner_map, pattern, group_size):
     devices = jnp.arange(group_size, dtype=jnp.int32)
-    entry_owner = jnp.take(owner_map, pattern)
+    entry_owner = pick(owner_map, pattern)
     foreign = entry_owner != owner_map[:, None]
     entry_hit = (entry_owner[:, :, None] == devices[None, None, :]) & foreign[:, :, None]
     per_tile = jnp.max(jnp.where(entry_hit, pattern[:, :, None], -1), axis=1)
@@ -191,8 +203,8 @@
     own_rank, class_rank = owner_tables(owner_map, group_size, piece_count)
     my_class = class_of(device, frame_devs)
     my_tiles = my_class * piece_count + local_iota
-    my_owner = jnp.take(owner_map, my_tiles)
-    my_slot = jnp.take(class_rank, my_tiles)
+    my_owner = lax.dynamic_slice_in_dim(owner_map, my_class * piece_count, piece_count)
+    my_slot = lax.dynamic_slice_in_dim(class_rank, my_class * piece_count, piece_count)
     send_hit = (my_owner[None, None, :] == devices[:, None, None]) & (
         my_slot[None, None, :] == cap_iota[None, :, None]
     )
@@ -204,13 +216,15 @@
     far_send_rows = piece_rows(far_send_piece).reshape(group_size, FAR_SLOTS * 16)
     source_class = class_of(devices, frame_devs)
     class_tiles = source_class[:, None] * piece_count + local_iota[None, :]
-    mine = jnp.take(owner_map, class_tiles) == device
+    class_count = tile_count // piece_count
+    mine = pick_rows(owner_map.reshape(class_count, piece_count), source_class) == device
     near_hit = mine[:, None, :] & (
-        jnp.take(class_rank, class_tiles)[:, None, :] == cap_iota[None, :, None]
+        pick_rows(class_rank.reshape(class_count, piece_count), source_class)[:, None, :]
+        == cap_iota[None, :, None]
     )
     near_tile = jnp.sum(jnp.where(near_hit, class_tiles[:, None, :], 0), axis=2)
     near_tile_rows = jnp.broadcast_to(near_tile[:, :, None], (group_size, capacity, 16)).reshape(-1)
-    my_requests = jnp.take(requests, device, axis=0)
+    my_requests = lax.dynamic_index_in_dim(requests, device, axis=0, keepdims=False)
     far_wanted = (my_requests[None, :] >= 0) & (
         my_requests[None, :] // piece_count == source_class[:, None]
     )
@@ -222,10 +236,10 @@
         far_tile[:, :, None], (group_size, FAR_SLOTS, 16)
     ).reshape(-1)
     own_ids = owned_tiles(owner_map, own_rank, device, own_count)
-    listed = jnp.take(pattern, own_ids, axis=0)
+    listed = pick_rows(pattern, own_ids)
     near_ok = jnp.any(listed[:, :, None] == near_tile_rows[None, None, :], axis=1)
     far_ok = jnp.any(listed[:, :, None] == far_tile_rows[None, None, :], axis=1)
-    query_own = jnp.take(own_rank, near_tile_rows)
+    query_own = pick(own_rank, near_tile_rows)
     near_bias = jnp.where(jnp.take(near_ok, query_own, axis=0), 0.0, masked_score)
     far_bias = jnp.where(jnp.take(far_ok, query_own, axis=0), 0.0, masked_score)
     near_bias = near_bias.astype(jnp.float32)
@@ -252,7 +266,7 @@
         logs.append(head_logs[:, :, 0])
     head_logs = jnp.concatenate(logs, axis=0)
     own_class = own_ids // piece_count
-    own_slot = jnp.take(class_rank, own_ids)
+    own_slot = pick(class_rank, own_ids)
     gather_rows = (
         supplier_of(own_class[:, None], slice_iota[None, :], frame_devs) * capacity
         + own_slot[:, None]
@@ -271,7 +285,7 @@
     column = local_iota_rows % WIDTH
     piece = strip * blocks + column // 4
     token = height * 4 + column % 4
-    back_rows = (jnp.take(my_owner, piece) * capacity + jnp.take(my_slot, piece)) * 16 + token
+    back_rows = (pick(my_owner, piece) * capacity + pick(my_slot, piece)) * 16 + token
     attended = jnp.take(jnp.concatenate(outputs, axis=1), back_rows, axis=0)
     return (attended, log_sums)
 

time: 591 us -> 549 us (0.929)
  other arithmetic: 67.8 us -> 28.7 us
  local copies, waits for them, and re-layouts: 90.6 us -> 54.8 us
  waiting for transfers between devices: 155 us -> 189 us
    and x1, other arithmetic: 39.9 us -> 0.02 us  [shards(): attended = jnp.take(jnp.concatenate(outputs, axis=1), back_rows, axis=0)]
    gather x16 -> x0, local copies, waits for them, and re-layouts: 32.8 us -> none  [the longest x3 17.1 us: request_table(): entry_owner = jnp.take(owner_map, pattern)]
    all_to_all x2, waiting for transfers between devices: 3.67 us -> 26.9 us  [shards(): lax.all_to_all(mixed, 'seq', split_axis=0, concat_axis=0, tiled=True)]
    all_to_all x1, waiting for transfers between devices: 151 us -> 162 us  [shards(): got = lax.all_to_all(sent, 'seq', split_axis=0, concat_axis=0, tiled=True)]
  transfers between devices with their start and end apart: 3 -> 3, of which waited for: 2 -> 3; matrix products, arithmetic and copies ran while one was open for 12% -> 3% of each run, Pallas kernels for 9% -> 10%
where the time goes in v5:
time: 549 us; the launch traced here: 548 us
  blocking collectives  205 us (37%)
  waiting for transfers between devices  189 us (34%)
  local copies, waits for them, and re-layouts  54.8 us (10%)
  Pallas kernels  53.8 us (10%)
  other arithmetic  28.7 us (5%)
  starting transfers between devices  15.7 us (3%)
    all_to_all x1, blocking collectives, shards(): got = lax.all_to_all(sent, 'seq', split_axis=0, concat_axis=0, tiled=True)  205 us
    all_to_all x1, waiting for transfers between devices, shards(): got = lax.all_to_all(sent, 'seq', split_axis=0, concat_axis=0, tiled=True)  162 us
    pallas_call x2, Pallas kernels, attend(): pl.pallas_call(attention_kernel, grid=(heads,), in_specs=[pl.BlockSpec(fa...  53.8 us
    all_to_all x2, waiting for transfers between devices, shards(): lax.all_to_all(mixed, 'seq', split_axis=0, concat_axis=0, tiled=True)  26.9 us
    gather x1, local copies, waits for them, and re-layouts, shards(): jnp.take(value_feats, far_send_rows.reshape(-1), axis=0)  12.5 us
  transfers between devices with their start and end apart: 3, of which 3 were waited for; matrix products, arithmetic and copies ran while one was open for 3% of the time, Pallas kernels for 10%

profile of v5, /device:TPU:13, one launch (start us, length us, event | category | flops | bytes accessed | tf_op | source)
XLA Modules:
  0.0 548.5 jit_solution(6045831038359698479)
XLA Ops:
  0.7 0.8 iota_compare_fusion.10
  1.5 1.8 select_reduce_fusion
  3.2 0.7 broadcast_compare_fusion
  3.9 0.8 select_reduce_fusion.2
  4.7 0.3 select_reduce_fusion.3
  5.1 0.2 reduce_window_sum.28
  5.2 0.1 select_reduce_fusion.11
  5.6 0.1 add_add_fusion
  5.8 0.7 eq.369
  6.6 12.5 %gather_fusion.4 = bf16[1024,2560]{1,0:T(8,128)(2,1)} fusion(bf16[512,2560]{1,0:T(8,128)(2,1)} %param.11, s32[1024]{0:T(1024)S(1)} %fusion.18), kind=kCustom, calls=%fused_computation.2.clone | custom fusion | bytes 10489856 | tf_op jit(solution)/shard_map/jit(_take)/gather | solution.py:253
  19.1 6.3 %gather_fusion.3 = bf16[1024,2560]{1,0:T(8,128)(2,1)} fusion(bf16[512,2560]{1,0:T(8,128)(2,1)S(1)} %copy-done, s32[1024]{0:T(1024)S(1)} %fusion.18), kind=kCustom, calls=%fused_computation.clone | custom fusion | bytes 10489856 | tf_op jit(solution)/shard_map/jit(_take)/gather | solution.py:252
  25.4 0.2 convert_reduce_fusion
  25.9 0.1 select_reduce_fusion.13
  26.2 0.1 add_add_fusion.1
  26.4 3.5 gather_fusion.6
  29.9 8.3 %gather_fusion.7 = bf16[512,2560]{1,0:T(8,128)(2,1)} fusion(bf16[512,2560]{1,0:T(8,128)(2,1)} %param.11, s32[1024]{0:T(1024)S(1)} %pad_clamp_fusion.3), kind=kCustom, calls=%fused_computation.4.clone | custom fusion | bytes 5244928 | tf_op jit(solution)/shard_map/jit(_take)/gather | solution.py:256
  38.3 3.5 gather_fusion.5
  41.8 6.0 %broadcast_select_fusion = (bf16[1024,2560]{1,0:T(8,128)(2,1)S(1)}, bf16[1024,2560]{1,0:T(8,128)(2,1)S(1)}) fusion(bf16[1024,2560]{1,0:T(8,128)(2,1)} %gather_fusion.4, pred[1024]{0:T(1024)(128)(4,1)S(1)} %compare_and_fusion.2, bf16[1024,2560]{1,0:T(8,128)(2,1)} %gather_fusion.3), kind=kLoop, calls=%fused_computation.9 | loop fusion | flops 5242880 | bytes 20972544 | tf_op jit(solution)/shard_map/jit(_take)/select_n | solution.py:253
  47.8 0.3 copy-done.5
  48.1 0.9 broadcast_select_fusion.3
  49.1 2.0 slice_dynamic-update-slice_fusion.3
  51.1 1.9 slice_dynamic-update-slice_fusion.2
  53.0 1.3 slice_dynamic-update-slice_fusion.9
  54.3 1.3 slice_dynamic-update-slice_fusion.8
  55.6 1.3 slice_dynamic-update-slice_fusion.7
  56.9 205.4 %all_to_all.20.far_key_ref.far_value_ref.query_ref.near_key_ref.near_value_ref = bf16[16,224,1280]{2,1,0:T(8,128)(2,1)} all-to-all(bf16[16,224,1280]{2,1,0:T(8,128)(2,1)S(1)} %get-tuple-element.34), channel_id=1, replica_groups=mesh['groups'=2,'seq'=16] {'seq'}, dimensions={0} | all-to-all | bytes 18350080 | tf_op jit(solution)/shard_map/all_to_all | solution.py:262
  262.3 5.9 %all-to-all-start.2 = ((bf16[16,224,1280]{2,1,0:T(8,128)(2,1)}), bf16[16,224,1280]{2,1,0:T(8,128)(2,1)}, u32[]{:S(2)}, u32[]{:S(2)}) async-start(bf16[16,224,1280]{2,1,0:T(8,128)(2,1)} %get-tuple-element.35), calls=%async_computation.2 | async-start | bytes 18350080 | tf_op jit(solution)/shard_map/all_to_all | solution.py:262
  268.3 0.2 reduce_window_sum.30
  268.5 0.1 fusion.4
  268.7 0.2 select_reduce_fusion.8
  269.0 0.1 eq.409
  269.2 0.2 reduce_window_sum.29
  269.4 0.2 select_reduce_fusion.7
  269.6 0.1 select_reduce_fusion.15
  269.7 0.2 select_reduce_fusion.14
  270.0 0.1 add.443
  270.3 0.1 select_reduce_fusion.12
  270.6 0.1 eq.384
  270.7 0.2 select_reduce_fusion.1
  271.1 0.5 select_reduce_fusion.4
  271.5 0.2 compare_reduce_fusion
  271.7 1.9 gather_fusion.1
  273.6 0.1 compare_reduce_fusion.1
  273.8 1.8 gather_fusion
  275.5 1.2 select_select_fusion.1.near_bias_ref
  276.7 1.6 select_select_fusion.far_bias_ref
  278.4 26.9 %shard_map.68 = (bf16[16,32,1280]{2,1,0:T(8,128)(2,1)}, f32[10,512,1]{2,1,0:T(8,128)}) custom-call(bf16[16,224,1280]{2,1,0:T(8,128)(2,1)} %all_to_all.20.far_key_ref.far_value_ref.query_ref.near_key_ref.near_value_ref, bf16[16,224,1280]{2,1,0:T(8,128)(2,1)} %all_to_all.20.far_key_ref.far_value_ref.query_ref.near_key_ref.near_value_ref, ...), custom_call_target="tpu_custom_call" | custom-call | tf_op jit(solution)/shard_map/pallas_call | solution.py:140
  305.3 162.2 %all-to-all-done.2.far_key_ref.far_value_ref.query_ref.near_key_ref.near_value_ref = bf16[16,224,1280]{2,1,0:T(8,128)(2,1)} async-done(((bf16[16,224,1280]{2,1,0:T(8,128)(2,1)}), bf16[16,224,1280]{2,1,0:T(8,128)(2,1)}, u32[]{:S(2)}, u32[]{:S(2)}) %all-to-all-start.2) | async-done | bytes 9175072 | tf_op jit(solution)/shard_map/all_to_all | solution.py:262
  467.4 4.9 all-to-all-start.1
  472.3 26.9 %shard_map.69 = (bf16[16,32,1280]{2,1,0:T(8,128)(2,1)}, f32[10,512,1]{2,1,0:T(8,128)}) custom-call(bf16[16,224,1280]{2,1,0:T(8,128)(2,1)} %all-to-all-done.2.far_key_ref.far_value_ref.query_ref.near_key_ref.near_value_ref, bf16[16,224,1280]{2,1,0:T(8,128)(2,1)} %all-to-all-done.2.far_key_ref.far_value_ref.query_ref.near_key_ref.near_value_ref, ...), custom_call_target="tpu_custom_call" | custom-call | tf_op jit(solution)/shard_map/pallas_call | solution.py:140
  499.2 3.7 all-to-all-done.1
  502.9 4.9 all-to-all-start.3
  507.9 0.1 select_reduce_fusion.6
  508.0 2.5 reduce
  510.5 2.5 reduce.1
  513.0 0.1 copy.29
  513.2 1.0 gather_fusion.2
  514.2 0.1 copy.30
  514.4 0.7 reshape.702
  515.1 23.3 %all-to-all-done.3 = bf16[16,32,1280]{2,1,0:T(8,128)(2,1)S(1)} async-done(((bf16[16,32,1280]{2,1,0:T(8,128)(2,1)}), bf16[16,32,1280]{2,1,0:T(8,128)(2,1)S(1)}, u32[]{:S(2)}, u32[]{:S(2)}) %all-to-all-start.3) | async-done | bytes 1310752 | tf_op jit(solution)/shard_map/all_to_all | solution.py:264
  538.3 1.1 copy-done.7
  539.4 1.9 pad_maximum_fusion
  541.3 3.5 gather_fusion.8
  544.8 3.7 broadcast_select_fusion.2
  (73 shorter events, 2.0 us)
Async XLA Ops:
  0.6 18.4 %copy-start = (bf16[512,2560]{1,0:T(8,128)(2,1)S(1)}, bf16[512,2560]{1,0:T(8,128)(2,1)}, u32[]{:S(2)}) copy-start(bf16[512,2560]{1,0:T(8,128)(2,1)} %param.10) | copy-start | bytes 7864324
  19.1 6.6 %copy-start.9 = (s32[128]{0:T(128)S(1)}, s32[128]{0:T(128)}, u32[]{:S(2)}) copy-start(s32[128]{0:T(128)} %param.12) | copy-start | bytes 1540
  29.9 8.3 %copy-start.2 = (bf16[512,2560]{1,0:T(8,128)(2,1)S(1)}, bf16[512,2560]{1,0:T(8,128)(2,1)}, u32[]{:S(2)}) copy-start(bf16[512,2560]{1,0:T(8,128)(2,1)} %param.9) | copy-start | bytes 7864324
  41.8 6.0 %copy-start.3 = (bf16[512,2560]{1,0:T(8,128)(2,1)S(1)}, bf16[512,2560]{1,0:T(8,128)(2,1)}, u32[]{:S(2)}) copy-start(bf16[512,2560]{1,0:T(8,128)(2,1)} %gather_fusion.6) | copy-start | bytes 7864324
  41.8 6.1 %copy-start.4 = (bf16[512,2560]{1,0:T(8,128)(2,1)S(1)}, bf16[512,2560]{1,0:T(8,128)(2,1)}, u32[]{:S(2)}) copy-start(bf16[512,2560]{1,0:T(8,128)(2,1)} %gather_fusion.7) | copy-start | bytes 7864324
  41.8 6.4 %copy-start.5 = (bf16[512,2560]{1,0:T(8,128)(2,1)S(1)}, bf16[512,2560]{1,0:T(8,128)(2,1)}, u32[]{:S(2)}) copy-start(bf16[512,2560]{1,0:T(8,128)(2,1)} %gather_fusion.5) | copy-start | bytes 7864324
  262.3 8.7 %copy-start.8 = (s32[128,23]{0,1:T(8,128)S(1)}, s32[128,23]{0,1:T(8,128)}, u32[]{:S(2)}) copy-start(s32[128,23]{0,1:T(8,128)} %param.13) | copy-start | bytes 35332
  262.3 205.1 %all-to-all-start.2 = ((bf16[16,224,1280]{2,1,0:T(8,128)(2,1)}), bf16[16,224,1280]{2,1,0:T(8,128)(2,1)}, u32[]{:S(2)}, u32[]{:S(2)}) async-start(bf16[16,224,1280]{2,1,0:T(8,128)(2,1)} %get-tuple-element.35), calls=%async_computation.2 | async-start | bytes 18350080 | tf_op jit(solution)/shard_map/all_to_all | solution.py:262
  467.4 35.5 %all-to-all-start.1 = ((bf16[16,32,1280]{2,1,0:T(8,128)(2,1)}), bf16[16,32,1280]{2,1,0:T(8,128)(2,1)S(1)}, u32[]{:S(2)}, u32[]{:S(2)}) async-start(bf16[16,32,1280]{2,1,0:T(8,128)(2,1)} %get-tuple-element.18), calls=%async_computation.1 | async-start | bytes 2621440 | tf_op jit(solution)/shard_map/all_to_all | solution.py:264
  502.9 7.6 %copy-start.6 = (bf16[16,32,1280]{2,1,0:T(8,128)(2,1)}, bf16[16,32,1280]{2,1,0:T(8,128)(2,1)S(1)}, u32[]{:S(2)}) copy-start(bf16[16,32,1280]{2,1,0:T(8,128)(2,1)S(1)} %all-to-all-done.1) | copy-start | bytes 3932164
  502.9 35.4 %all-to-all-start.3 = ((bf16[16,32,1280]{2,1,0:T(8,128)(2,1)}), bf16[16,32,1280]{2,1,0:T(8,128)(2,1)S(1)}, u32[]{:S(2)}, u32[]{:S(2)}) async-start(bf16[16,32,1280]{2,1,0:T(8,128)(2,1)} %get-tuple-element.19), calls=%async_computation.3 | async-start | bytes 2621440 | tf_op jit(solution)/shard_map/all_to_all | solution.py:264
  538.3 1.1 copy-start.7
  544.8 3.7 copy-start.1

commit v6 on v5

--- a/solution.py
+++ b/solution.py
@@ -93,7 +93,7 @@
 
 
 FAR_SLOTS = 4
-HEAD_CHUNKS = 2
+HEAD_CHUNKS = 4
 
 
 def attention_kernel(

time: 549 us -> 585 us (1.066)
  blocking collectives: 205 us -> 319 us
  waiting for transfers between devices: 189 us -> 87.7 us
  starting transfers between devices: 15.7 us -> 25.3 us
    all_to_all x1 -> x3, blocking collectives: 205 us -> 319 us  [shards(): got = lax.all_to_all(sent, 'seq', split_axis=0, concat_axis=0, tiled=True)]
    all_to_all x1, waiting for transfers between devices: 162 us -> 75.8 us  [shards(): got = lax.all_to_all(sent, 'seq', split_axis=0, concat_axis=0, tiled=True)]
    all_to_all x2 -> x4, waiting for transfers between devices: 26.9 us -> 11.8 us  [shards(): lax.all_to_all(mixed, 'seq', split_axis=0, concat_axis=0, tiled=True)]
    all_to_all x2 -> x4, starting transfers between devices: 9.78 us -> 19.8 us  [shards(): lax.all_to_all(mixed, 'seq', split_axis=0, concat_axis=0, tiled=True)]
    pallas_call x2 -> x4, Pallas kernels: 53.8 us -> 59.5 us  [attend(): pl.pallas_call(attention_kernel, grid=(heads,), in_specs=[pl.BlockSpec(fa...]
  transfers between devices with their start and end apart: 3 -> 5, of which waited for: 3 -> 5; matrix products, arithmetic and copies ran while one was open for 3% -> 3% of each run, Pallas kernels for 10% -> 10%
where the time goes in v6:
time: 585 us; the launch traced here: 583 us
  blocking collectives  319 us (55%)
  waiting for transfers between devices  87.7 us (15%)
  local copies, waits for them, and re-layouts  60.2 us (10%)
  Pallas kernels  59.5 us (10%)
  other arithmetic  30.3 us (5%)
  starting transfers between devices  25.3 us (4%)
    all_to_all x3, blocking collectives, shards(): got = lax.all_to_all(sent, 'seq', split_axis=0, concat_axis=0, tiled=True)  319 us
    all_to_all x1, waiting for transfers between devices, shards(): got = lax.all_to_all(sent, 'seq', split_axis=0, concat_axis=0, tiled=True)  75.8 us
    pallas_call x4, Pallas kernels, attend(): pl.pallas_call(attention_kernel, grid=(heads,), in_specs=[pl.BlockSpec(fa...  59.5 us
    all_to_all x4, starting transfers between devices, shards(): lax.all_to_all(mixed, 'seq', split_axis=0, concat_axis=0, tiled=True)  19.8 us
    gather x1, local copies, waits for them, and re-layouts, shards(): jnp.take(value_feats, far_send_rows.reshape(-1), axis=0)  12.5 us
    all_to_all x4, waiting for transfers between devices, shards(): lax.all_to_all(mixed, 'seq', split_axis=0, concat_axis=0, tiled=True)  11.8 us
  transfers between devices with their start and end apart: 5, of which 5 were waited for; matrix products, arithmetic and copies ran while one was open for 3% of the time, Pallas kernels for 10%

profile of v6, /device:TPU:13, one launch (start us, length us, event | category | flops | bytes accessed | tf_op | source)
XLA Modules:
  0.0 583.2 jit_solution(1657521491528356122)
XLA Ops:
  0.7 0.8 iota_compare_fusion.10
  1.5 1.8 select_reduce_fusion
  3.2 0.7 broadcast_compare_fusion
  3.9 0.8 select_reduce_fusion.2
  4.7 0.3 select_reduce_fusion.3
  5.1 0.2 reduce_window_sum.28
  5.2 0.1 select_reduce_fusion.11
  5.8 0.7 eq.369
  6.6 12.5 %gather_fusion.4 = bf16[1024,2560]{1,0:T(8,128)(2,1)} fusion(bf16[512,2560]{1,0:T(8,128)(2,1)} %param.11, s32[1024]{0:T(1024)S(1)} %fusion.18), kind=kCustom, calls=%fused_computation.2.clone | custom fusion | bytes 10489856 | tf_op jit(solution)/shard_map/jit(_take)/gather | solution.py:253
  19.1 6.3 %gather_fusion.3 = bf16[1024,2560]{1,0:T(8,128)(2,1)} fusion(bf16[512,2560]{1,0:T(8,128)(2,1)S(1)} %copy-done, s32[1024]{0:T(1024)S(1)} %fusion.18), kind=kCustom, calls=%fused_computation.clone | custom fusion | bytes 10489856 | tf_op jit(solution)/shard_map/jit(_take)/gather | solution.py:252
  25.4 0.2 convert_reduce_fusion
  25.9 0.1 select_reduce_fusion.13
  26.4 3.5 gather_fusion.6
  29.9 8.3 %gather_fusion.7 = bf16[512,2560]{1,0:T(8,128)(2,1)} fusion(bf16[512,2560]{1,0:T(8,128)(2,1)} %param.11, s32[1024]{0:T(1024)S(1)} %pad_clamp_fusion.3), kind=kCustom, calls=%fused_computation.4.clone | custom fusion | bytes 5244928 | tf_op jit(solution)/shard_map/jit(_take)/gather | solution.py:256
  38.3 3.5 gather_fusion.5
  41.8 6.0 %broadcast_select_fusion = (bf16[1024,2560]{1,0:T(8,128)(2,1)S(1)}, bf16[1024,2560]{1,0:T(8,128)(2,1)S(1)}) fusion(bf16[1024,2560]{1,0:T(8,128)(2,1)} %gather_fusion.4, pred[1024]{0:T(1024)(128)(4,1)S(1)} %compare_and_fusion.2, bf16[1024,2560]{1,0:T(8,128)(2,1)} %gather_fusion.3), kind=kLoop, calls=%fused_computation.9 | loop fusion | flops 5242880 | bytes 20972544 | tf_op jit(solution)/shard_map/jit(_take)/select_n | solution.py:253
  47.8 0.3 copy-done.5
  48.2 1.0 broadcast_select_fusion.3
  49.1 2.3 slice_dynamic-update-slice_fusion.7
  51.4 2.6 slice_dynamic-update-slice_fusion.6
  54.0 1.5 slice_dynamic-update-slice_fusion.19
  55.5 1.5 slice_dynamic-update-slice_fusion.18
  57.0 1.5 slice_dynamic-update-slice_fusion.17
  58.5 107.4 %all_to_all.40.far_key_ref.far_value_ref.query_ref.near_key_ref.near_value_ref = bf16[16,224,640]{2,1,0:T(8,128)(2,1)} all-to-all(bf16[16,224,640]{2,1,0:T(8,128)(2,1)S(1)} %get-tuple-element.46), channel_id=1, replica_groups=mesh['groups'=2,'seq'=16] {'seq'}, dimensions={0} | all-to-all | bytes 9175040 | tf_op jit(solution)/shard_map/all_to_all | solution.py:262
  165.9 106.1 %all_to_all.41.far_key_ref.far_value_ref.query_ref.near_key_ref.near_value_ref = bf16[16,224,640]{2,1,0:T(8,128)(2,1)} all-to-all(bf16[16,224,640]{2,1,0:T(8,128)(2,1)S(1)} %copy-done.7), channel_id=1, replica_groups=mesh['groups'=2,'seq'=16] {'seq'}, dimensions={0} | all-to-all | bytes 9175040 | tf_op jit(solution)/shard_map/all_to_all | solution.py:262
  272.0 105.9 %all_to_all.42.far_key_ref.far_value_ref.query_ref.near_key_ref.near_value_ref = bf16[16,224,640]{2,1,0:T(8,128)(2,1)} all-to-all(bf16[16,224,640]{2,1,0:T(8,128)(2,1)S(1)} %bitcast.29), channel_id=1, replica_groups=mesh['groups'=2,'seq'=16] {'seq'}, dimensions={0} | all-to-all | bytes 9175040 | tf_op jit(solution)/shard_map/all_to_all | solution.py:262
  377.9 5.5 all-to-all-start.6
  383.5 0.2 reduce_window_sum.30
  383.7 0.1 fusion.4
  383.8 0.2 select_reduce_fusion.8
  384.4 0.2 reduce_window_sum.29
  384.5 0.2 select_reduce_fusion.7
  384.9 0.2 select_reduce_fusion.14
  385.9 0.2 select_reduce_fusion.1
  386.2 0.5 select_reduce_fusion.4
  386.7 0.2 compare_reduce_fusion
  386.9 1.9 gather_fusion.1
  388.9 1.8 gather_fusion
  390.7 1.2 select_select_fusion.1.near_bias_ref
  391.9 1.7 select_select_fusion.far_bias_ref
  393.6 14.9 %shard_map.68 = (bf16[16,32,640]{2,1,0:T(8,128)(2,1)}, f32[5,512,1]{2,1,0:T(8,128)}) custom-call(bf16[16,224,640]{2,1,0:T(8,128)(2,1)} %all_to_all.40.far_key_ref.far_value_ref.query_ref.near_key_ref.near_value_ref, bf16[16,224,640]{2,1,0:T(8,128)(2,1)} %all_to_all.40.far_key_ref.far_value_ref.query_ref.near_key_ref.near_value_ref, ...), custom_call_target="tpu_custom_call" | custom-call | tf_op jit(solution)/shard_map/pallas_call | solution.py:140
  408.4 75.8 %all-to-all-done.6.far_key_ref.far_value_ref.query_ref.near_key_ref.near_value_ref = bf16[16,224,640]{2,1,0:T(8,128)(2,1)} async-done(((bf16[16,224,640]{2,1,0:T(8,128)(2,1)}), bf16[16,224,640]{2,1,0:T(8,128)(2,1)}, u32[]{:S(2)}, u32[]{:S(2)}) %all-to-all-start.6) | async-done | bytes 4587552 | tf_op jit(solution)/shard_map/all_to_all | solution.py:262
  484.3 4.9 all-to-all-start.1
  489.2 14.9 %shard_map.69 = (bf16[16,32,640]{2,1,0:T(8,128)(2,1)}, f32[5,512,1]{2,1,0:T(8,128)}) custom-call(bf16[16,224,640]{2,1,0:T(8,128)(2,1)} %all_to_all.41.far_key_ref.far_value_ref.query_ref.near_key_ref.near_value_ref, bf16[16,224,640]{2,1,0:T(8,128)(2,1)} %all_to_all.41.far_key_ref.far_value_ref.query_ref.near_key_ref.near_value_ref, ...), custom_call_target="tpu_custom_call" | custom-call | tf_op jit(solution)/shard_map/pallas_call | solution.py:140
  504.1 1.6 all-to-all-done.1
  505.6 5.0 all-to-all-start.3
  510.6 14.9 %shard_map.70 = (bf16[16,32,640]{2,1,0:T(8,128)(2,1)}, f32[5,512,1]{2,1,0:T(8,128)}) custom-call(bf16[16,224,640]{2,1,0:T(8,128)(2,1)} %all_to_all.42.far_key_ref.far_value_ref.query_ref.near_key_ref.near_value_ref, bf16[16,224,640]{2,1,0:T(8,128)(2,1)} %all_to_all.42.far_key_ref.far_value_ref.query_ref.near_key_ref.near_value_ref, ...), custom_call_target="tpu_custom_call" | custom-call | tf_op jit(solution)/shard_map/pallas_call | solution.py:140
  525.5 1.5 all-to-all-done.3
  527.0 5.0 all-to-all-start.5
  532.0 14.9 %shard_map.71 = (bf16[16,32,640]{2,1,0:T(8,128)(2,1)}, f32[5,512,1]{2,1,0:T(8,128)}) custom-call(bf16[16,224,640]{2,1,0:T(8,128)(2,1)} %all-to-all-done.6.far_key_ref.far_value_ref.query_ref.near_key_ref.near_value_ref, bf16[16,224,640]{2,1,0:T(8,128)(2,1)} %all-to-all-done.6.far_key_ref.far_value_ref.query_ref.near_key_ref.near_value_ref, ...), custom_call_target="tpu_custom_call" | custom-call | tf_op jit(solution)/shard_map/pallas_call | solution.py:140
  546.8 1.5 all-to-all-done.5
  548.4 5.0 all-to-all-start.7
  553.6 1.7 reduce
  555.3 1.7 reduce.1
  557.0 1.7 reduce.2
  558.8 1.7 reduce.3
  560.5 0.1 copy.31
  560.7 1.0 gather_fusion.2
  561.7 0.1 copy.32
  561.9 0.7 reshape.710
  562.6 7.2 %all-to-all-done.7 = bf16[16,32,640]{2,1,0:T(8,128)(2,1)S(1)} async-done(((bf16[16,32,640]{2,1,0:T(8,128)(2,1)}), bf16[16,32,640]{2,1,0:T(8,128)(2,1)S(1)}, u32[]{:S(2)}, u32[]{:S(2)}) %all-to-all-start.7) | async-done | bytes 655392 | tf_op jit(solution)/shard_map/all_to_all | solution.py:264
  569.8 1.6 pad_maximum_fusion
  571.4 8.3 %gather_fusion.8 = bf16[512,2560]{1,0:T(8,128)(2,1)} fusion(bf16[512,2560]{1,0:T(8,128)(2,1)} %pad_maximum_fusion, s32[1024]{0:T(1024)S(1)} %pad_clamp_fusion.1), kind=kCustom, calls=%fused_computation.5.clone | custom fusion | bytes 5244928 | tf_op jit(solution)/shard_map/jit(_take)/gather | solution.py:289
  579.7 3.5 broadcast_select_fusion.2
  (88 shorter events, 3.0 us)
Async XLA Ops:
  0.6 18.4 %copy-start = (bf16[512,2560]{1,0:T(8,128)(2,1)S(1)}, bf16[512,2560]{1,0:T(8,128)(2,1)}, u32[]{:S(2)}) copy-start(bf16[512,2560]{1,0:T(8,128)(2,1)} %param.10) | copy-start | bytes 7864324
  19.1 6.6 %copy-start.9 = (s32[128]{0:T(128)S(1)}, s32[128]{0:T(128)}, u32[]{:S(2)}) copy-start(s32[128]{0:T(128)} %param.12) | copy-start | bytes 1540
  29.9 8.3 %copy-start.2 = (bf16[512,2560]{1,0:T(8,128)(2,1)S(1)}, bf16[512,2560]{1,0:T(8,128)(2,1)}, u32[]{:S(2)}) copy-start(bf16[512,2560]{1,0:T(8,128)(2,1)} %param.9) | copy-start | bytes 7864324
  41.8 6.0 %copy-start.3 = (bf16[512,2560]{1,0:T(8,128)(2,1)S(1)}, bf16[512,2560]{1,0:T(8,128)(2,1)}, u32[]{:S(2)}) copy-start(bf16[512,2560]{1,0:T(8,128)(2,1)} %gather_fusion.6) | copy-start | bytes 7864324
  41.8 6.1 %copy-start.4 = (bf16[512,2560]{1,0:T(8,128)(2,1)S(1)}, bf16[512,2560]{1,0:T(8,128)(2,1)}, u32[]{:S(2)}) copy-start(bf16[512,2560]{1,0:T(8,128)(2,1)} %gather_fusion.7) | copy-start | bytes 7864324
  41.8 6.4 %copy-start.5 = (bf16[512,2560]{1,0:T(8,128)(2,1)S(1)}, bf16[512,2560]{1,0:T(8,128)(2,1)}, u32[]{:S(2)}) copy-start(bf16[512,2560]{1,0:T(8,128)(2,1)} %gather_fusion.5) | copy-start | bytes 7864324
  58.5 107.4 %copy-start.6 = (bf16[16,224,640]{2,1,0:T(8,128)(2,1)}, bf16[16,224,640]{2,1,0:T(8,128)(2,1)S(1)}, u32[]{:S(2)}) copy-start(bf16[16,224,640]{2,1,0:T(8,128)(2,1)S(1)} %get-tuple-element.47) | copy-start | bytes 13762564
  58.5 107.4 %copy-start.7 = (bf16[16,224,640]{2,1,0:T(8,128)(2,1)S(1)}, bf16[16,224,640]{2,1,0:T(8,128)(2,1)}, u32[]{:S(2)}) copy-start(bf16[16,224,640]{2,1,0:T(8,128)(2,1)} %get-tuple-element.49) | copy-start | bytes 13762564
  58.5 213.4 %slice-start = ((s8[4587520]{0:T(1024)(128)(4,1)}), s8[4194304]{0:T(1024)(128)(4,1)S(1)}, s32[]{:S(2)}) async-start(s8[4587520]{0:T(1024)(128)(4,1)} %bitcast.28), calls=%async_computation.8 | async-start | bytes 8388608
  165.9 106.1 %slice-start.1 = ((s8[4587520]{0:T(1024)(128)(4,1)}), s8[393216]{0:T(1024)(128)(4,1)S(1)}, s32[]{:S(2)}) async-start(s8[4587520]{0:T(1024)(128)(4,1)} %bitcast.28), calls=%async_computation.9 | async-start | bytes 786432
  377.9 8.3 %copy-start.8 = (s32[128,23]{0,1:T(8,128)S(1)}, s32[128,23]{0,1:T(8,128)}, u32[]{:S(2)}) copy-start(s32[128,23]{0,1:T(8,128)} %param.13) | copy-start | bytes 35332
  377.9 106.4 %all-to-all-start.6 = ((bf16[16,224,640]{2,1,0:T(8,128)(2,1)}), bf16[16,224,640]{2,1,0:T(8,128)(2,1)}, u32[]{:S(2)}, u32[]{:S(2)}) async-start(bf16[16,224,640]{2,1,0:T(8,128)(2,1)} %copy-done.6), calls=%async_computation.6 | async-start | bytes 9175040 | tf_op jit(solution)/shard_map/all_to_all | solution.py:262
  484.3 21.3 %all-to-all-start.1 = ((bf16[16,32,640]{2,1,0:T(8,128)(2,1)}), bf16[16,32,640]{2,1,0:T(8,128)(2,1)S(1)}, u32[]{:S(2)}, u32[]{:S(2)}) async-start(bf16[16,32,640]{2,1,0:T(8,128)(2,1)} %get-tuple-element.22), calls=%async_computation.1 | async-start | bytes 1310720 | tf_op jit(solution)/shard_map/all_to_all | solution.py:264
  505.6 21.4 %all-to-all-start.3 = ((bf16[16,32,640]{2,1,0:T(8,128)(2,1)}), bf16[16,32,640]{2,1,0:T(8,128)(2,1)S(1)}, u32[]{:S(2)}, u32[]{:S(2)}) async-start(bf16[16,32,640]{2,1,0:T(8,128)(2,1)} %get-tuple-element.23), calls=%async_computation.3 | async-start | bytes 1310720 | tf_op jit(solution)/shard_map/all_to_all | solution.py:264
  527.0 21.4 %all-to-all-start.5 = ((bf16[16,32,640]{2,1,0:T(8,128)(2,1)}), bf16[16,32,640]{2,1,0:T(8,128)(2,1)S(1)}, u32[]{:S(2)}, u32[]{:S(2)}) async-start(bf16[16,32,640]{2,1,0:T(8,128)(2,1)} %get-tuple-element.24), calls=%async_computation.5 | async-start | bytes 1310720 | tf_op jit(solution)/shard_map/all_to_all | solution.py:264
  548.4 21.4 %all-to-all-start.7 = ((bf16[16,32,640]{2,1,0:T(8,128)(2,1)}), bf16[16,32,640]{2,1,0:T(8,128)(2,1)S(1)}, u32[]{:S(2)}, u32[]{:S(2)}) async-start(bf16[16,32,640]{2,1,0:T(8,128)(2,1)} %get-tuple-element.25), calls=%async_computation.7 | async-start | bytes 1310720 | tf_op jit(solution)/shard_map/all_to_all | solution.py:264
  571.4 11.9 %copy-start.1 = (bf16[512,2560]{1,0:T(8,128)(2,1)S(1)}, bf16[512,2560]{1,0:T(8,128)(2,1)}, u32[]{:S(2)}) copy-start(bf16[512,2560]{1,0:T(8,128)(2,1)} %param.10) | copy-start | bytes 7864324

commit v7 on v5

--- a/solution.py
+++ b/solution.py
@@ -247,18 +247,24 @@
     chunk_width = channels // HEAD_CHUNKS
     outputs = []
     logs = []
-    taken = lax.optimization_barrier(
-        (
-            jnp.take(key_feats, far_send_rows.reshape(-1), axis=0).reshape(group_size, -1, channels),
-            jnp.take(value_feats, far_send_rows.reshape(-1), axis=0).reshape(group_size, -1, channels),
-            jnp.take(query_feats, own_send_rows.reshape(-1), axis=0).reshape(group_size, -1, channels),
-            jnp.take(key_feats, own_send_rows.reshape(-1), axis=0).reshape(group_size, -1, channels),
-            jnp.take(value_feats, own_send_rows.reshape(-1), axis=0).reshape(group_size, -1, channels),
-        )
+    sources = (
+        (key_feats, far_send_rows),
+        (value_feats, far_send_rows),
+        (query_feats, own_send_rows),
+        (key_feats, own_send_rows),
+        (value_feats, own_send_rows),
     )
     for chunk in range(HEAD_CHUNKS):
         columns = slice(chunk * chunk_width, (chunk + 1) * chunk_width)
-        sent = jnp.concatenate([part[:, :, columns] for part in taken], axis=1)
+        sent = jnp.concatenate(
+            [
+                jnp.take(source[:, columns], rows.reshape(-1), axis=0).reshape(
+                    group_size, -1, chunk_width
+                )
+                for source, rows in sources
+            ],
+            axis=1,
+        )
         got = lax.all_to_all(sent, "seq", split_axis=0, concat_axis=0, tiled=True)
         mixed, head_logs = attend(got, unit, near_bias, far_bias)
         returned = lax.all_to_all(mixed, "seq", split_axis=0, concat_axis=0, tiled=True)

time: 549 us -> 573 us (1.044)
  blocking collectives: 205 us -> 0 us
  waiting for transfers between devices: 189 us -> 380 us
  local copies, waits for them, and re-layouts: 54.8 us -> 84.9 us
  starting transfers between devices: 15.7 us -> 21.5 us
    all_to_all x1 -> x0, blocking collectives: 205 us -> none  [shards(): got = lax.all_to_all(sent, 'seq', split_axis=0, concat_axis=0, tiled=True)]
    all_to_all x1 -> x2, waiting for transfers between devices: 162 us -> 353 us  [shards(): got = lax.all_to_all(sent, 'seq', split_axis=0, concat_axis=0, tiled=True)]
    gather x5 -> x10, local copies, waits for them, and re-layouts: 34.2 us -> 49.5 us  [shards(): jnp.take(source[:, columns], rows.reshape(-1), axis=0)]
    unnamed x24 -> x40, local copies, waits for them, and re-layouts: 7.92 us -> 17.1 us
    all_to_all x1 -> x2, starting transfers between devices: 5.91 us -> 11.7 us  [shards(): got = lax.all_to_all(sent, 'seq', split_axis=0, concat_axis=0, tiled=True)]
  transfers between devices with their start and end apart: 3 -> 4, of which waited for: 3 -> 4; matrix products, arithmetic and copies ran while one was open for 3% -> 4% of each run, Pallas kernels for 10% -> 9%
where the time goes in v7:
time: 573 us; the launch traced here: 572 us
  waiting for transfers between devices  380 us (66%)
  local copies, waits for them, and re-layouts  84.9 us (15%)
  Pallas kernels  53.8 us (9%)
  other arithmetic  31.5 us (5%)
  starting transfers between devices  21.5 us (4%)
    all_to_all x2, waiting for transfers between devices, shards(): got = lax.all_to_all(sent, 'seq', split_axis=0, concat_axis=0, tiled=True)  353 us
    pallas_call x2, Pallas kernels, attend(): pl.pallas_call(attention_kernel, grid=(heads,), in_specs=[pl.BlockSpec(fa...  53.8 us
    gather x10, local copies, waits for them, and re-layouts, shards(): jnp.take(source[:, columns], rows.reshape(-1), axis=0)  49.5 us
    all_to_all x2, waiting for transfers between devices, shards(): lax.all_to_all(mixed, 'seq', split_axis=0, concat_axis=0, tiled=True)  26.9 us
    unnamed x40, local copies, waits for them, and re-layouts  17.1 us
    all_to_all x2, starting transfers between devices, shards(): got = lax.all_to_all(sent, 'seq', split_axis=0, concat_axis=0, tiled=True)  11.7 us
  transfers between devices with their start and end apart: 4, of which 4 were waited for; matrix products, arithmetic and copies ran while one was open for 4% of the time, Pallas kernels for 9%

profile of v7, /device:TPU:13, one launch (start us, length us, event | category | flops | bytes accessed | tf_op | source)
XLA Modules:
  0.0 572.5 jit_solution(11868087272291141964)
XLA Ops:
  0.7 0.7 iota_compare_fusion.10
  1.3 1.8 select_reduce_fusion
  3.1 0.7 broadcast_compare_fusion
  3.7 0.8 select_reduce_fusion.2
  4.5 0.3 select_reduce_fusion.3
  4.9 0.2 reduce_window_sum.28
  5.6 0.7 eq.355
  6.4 3.1 fusion.46
  9.5 1.3 fusion.45
  10.8 8.1 %gather_fusion.4 = bf16[1024,1280]{1,0:T(8,128)(2,1)} fusion(bf16[512,1280]{1,0:T(8,128)(2,1)} %get-tuple-element.24, s32[1024]{0:T(1024)S(1)} %fusion.18), kind=kCustom, calls=%fused_computation.clone | custom fusion | bytes 5246976 | tf_op jit(solution)/shard_map/jit(_take)/gather | solution.py:261
  18.9 8.1 %gather_fusion.5 = bf16[1024,1280]{1,0:T(8,128)(2,1)} fusion(bf16[512,1280]{1,0:T(8,128)(2,1)} %get-tuple-element.22, s32[1024]{0:T(1024)S(1)} %fusion.18), kind=kCustom, calls=%fused_computation.2.clone | custom fusion | bytes 5246976 | tf_op jit(solution)/shard_map/jit(_take)/gather | solution.py:261
  26.9 0.2 convert_reduce_fusion
  27.9 5.4 gather_fusion.7
  33.3 5.4 gather_fusion.8
  38.8 5.5 gather_fusion.9
  44.2 2.9 gather_fusion.12
  47.1 5.5 gather_fusion.10
  52.6 2.9 gather_fusion.13
  55.5 6.6 %broadcast_select_fusion.3 = (bf16[1024,1280]{1,0:T(8,128)(2,1)}, bf16[1024,1280]{1,0:T(8,128)(2,1)}, bf16[1024,1280]{1,0:T(8,128)(2,1)}, bf16[1024,1280]{1,0:T(8,128)(2,1)S(1)}) fusion(bf16[1024,1280]{1,0:T(8,128)(2,1)} %gather_fusion.5, pred[1024]{0:T(1024)(128)(4,1)S(1)} %compare_and_fusion.2, bf16[1024,1280]{1,0:T(8,128)(2,1)} %gather_fusion.9, ...), kind=kLoop, calls=%fused_computation.18 | loop fusion | flops 5242880 | bytes 20972544 | tf_op jit(solution)/shard_map/jit(_take)/select_n | solution.py:261
  62.1 1.8 constant_dynamic-update-slice_fusion.4
  63.9 0.9 copy-done.13
  64.8 0.2 fusion.44
  65.0 2.9 gather_fusion.6
  67.9 2.9 gather_fusion.11
  70.8 3.6 constant_dynamic-update-slice_fusion.3
  74.6 3.4 broadcast_select_fusion.8
  78.0 1.1 constant_dynamic-update-slice_fusion.2
  79.1 1.2 constant_dynamic-update-slice_fusion.1
  80.3 1.2 constant_dynamic-update-slice_fusion
  81.5 6.8 %all-to-all-start = ((bf16[16,224,1280]{2,1,0:T(8,128)(2,1)}), bf16[16,224,1280]{2,1,0:T(8,128)(2,1)}, u32[]{:S(2)}, u32[]{:S(2)}) async-start(bf16[16,224,1280]{2,1,0:T(8,128)(2,1)} %constant_dynamic-update-slice_fusion), calls=%async_computation | async-start | bytes 18350080 | tf_op jit(solution)/shard_map/all_to_all | solution.py:268
  88.3 1.7 constant_dynamic-update-slice_fusion.9
  90.0 0.9 copy-done
  91.0 1.7 constant_dynamic-update-slice_fusion.8
  92.8 1.2 constant_dynamic-update-slice_fusion.7
  93.9 0.4 copy-done.8
  94.4 1.2 constant_dynamic-update-slice_fusion.6
  95.5 1.2 constant_dynamic-update-slice_fusion.5
  96.7 190.7 %all-to-all-done.far_key_ref.far_value_ref.query_ref.near_key_ref.near_value_ref = bf16[16,224,1280]{2,1,0:T(8,128)(2,1)} async-done(((bf16[16,224,1280]{2,1,0:T(8,128)(2,1)}), bf16[16,224,1280]{2,1,0:T(8,128)(2,1)}, u32[]{:S(2)}, u32[]{:S(2)}) %all-to-all-start) | async-done | bytes 9175072 | tf_op jit(solution)/shard_map/all_to_all | solution.py:268
  287.5 4.9 all-to-all-start.2
  293.4 0.2 reduce_window_sum.29
  293.5 0.2 select_reduce_fusion.5
  293.8 0.2 select_reduce_fusion.14
  294.9 0.2 select_reduce_fusion.1
  295.2 0.5 select_reduce_fusion.4
  295.7 0.2 compare_reduce_fusion
  295.9 1.9 gather_fusion.1
  297.9 1.8 gather_fusion
  299.7 1.2 select_select_fusion.1.near_bias_ref
  300.9 1.6 select_select_fusion.far_bias_ref
  302.5 26.9 %shard_map.68 = (bf16[16,32,1280]{2,1,0:T(8,128)(2,1)}, f32[10,512,1]{2,1,0:T(8,128)}) custom-call(bf16[16,224,1280]{2,1,0:T(8,128)(2,1)} %all-to-all-done.far_key_ref.far_value_ref.query_ref.near_key_ref.near_value_ref, bf16[16,224,1280]{2,1,0:T(8,128)(2,1)} %all-to-all-done.far_key_ref.far_value_ref.query_ref.near_key_ref.near_value_ref, ...), custom_call_target="tpu_custom_call" | custom-call | tf_op jit(solution)/shard_map/pallas_call | solution.py:140
  329.4 162.2 %all-to-all-done.2.far_key_ref.far_value_ref.query_ref.near_key_ref.near_value_ref = bf16[16,224,1280]{2,1,0:T(8,128)(2,1)} async-done(((bf16[16,224,1280]{2,1,0:T(8,128)(2,1)}), bf16[16,224,1280]{2,1,0:T(8,128)(2,1)}, u32[]{:S(2)}, u32[]{:S(2)}) %all-to-all-start.2) | async-done | bytes 9175072 | tf_op jit(solution)/shard_map/all_to_all | solution.py:268
  491.6 4.9 all-to-all-start.1
  496.5 26.9 %shard_map.69 = (bf16[16,32,1280]{2,1,0:T(8,128)(2,1)}, f32[10,512,1]{2,1,0:T(8,128)}) custom-call(bf16[16,224,1280]{2,1,0:T(8,128)(2,1)} %all-to-all-done.2.far_key_ref.far_value_ref.query_ref.near_key_ref.near_value_ref, bf16[16,224,1280]{2,1,0:T(8,128)(2,1)} %all-to-all-done.2.far_key_ref.far_value_ref.query_ref.near_key_ref.near_value_ref, ...), custom_call_target="tpu_custom_call" | custom-call | tf_op jit(solution)/shard_map/pallas_call | solution.py:140
  523.4 3.6 all-to-all-done.1
  527.1 4.9 all-to-all-start.3
  532.2 2.5 reduce
  534.7 2.5 reduce.1
  537.3 1.0 gather_fusion.3
  538.6 0.7 reshape.883
  539.3 23.2 %all-to-all-done.3 = bf16[16,32,1280]{2,1,0:T(8,128)(2,1)S(1)} async-done(((bf16[16,32,1280]{2,1,0:T(8,128)(2,1)}), bf16[16,32,1280]{2,1,0:T(8,128)(2,1)S(1)}, u32[]{:S(2)}, u32[]{:S(2)}) %all-to-all-start.3) | async-done | bytes 1310752 | tf_op jit(solution)/shard_map/all_to_all | solution.py:270
  562.5 1.1 copy-done.11
  563.6 1.9 pad_maximum_fusion
  565.4 3.5 gather_fusion.2
  569.0 3.5 broadcast_select_fusion
  (100 shorter events, 4.3 us)
Async XLA Ops:
  6.4 3.1 copy-start.12
  18.9 8.4 %copy-start.15 = (s32[128]{0:T(128)S(1)}, s32[128]{0:T(128)}, u32[]{:S(2)}) copy-start(s32[128]{0:T(128)} %param.12) | copy-start | bytes 1540
  62.1 2.7 copy-start.13
  67.9 6.5 %copy-start.6 = (bf16[512,1280]{1,0:T(8,128)(2,1)S(1)}, bf16[512,1280]{1,0:T(8,128)(2,1)}, u32[]{:S(2)}) copy-start(bf16[512,1280]{1,0:T(8,128)(2,1)} %gather_fusion.6) | copy-start | bytes 3932164
  70.8 3.6 copy-start.2
  70.8 3.6 copy-start.3
  70.8 3.6 copy-start.4
  70.8 3.8 copy-start.5
  81.5 6.8 %copy-start.1 = (bf16[1024,1280]{1,0:T(8,128)(2,1)S(1)}, bf16[1024,1280]{1,0:T(8,128)(2,1)}, u32[]{:S(2)}) copy-start(bf16[1024,1280]{1,0:T(8,128)(2,1)} %get-tuple-element.33) | copy-start | bytes 7864324
  81.5 206.0 %all-to-all-start = ((bf16[16,224,1280]{2,1,0:T(8,128)(2,1)}), bf16[16,224,1280]{2,1,0:T(8,128)(2,1)}, u32[]{:S(2)}, u32[]{:S(2)}) async-start(bf16[16,224,1280]{2,1,0:T(8,128)(2,1)} %constant_dynamic-update-slice_fusion), calls=%async_computation | async-start | bytes 18350080 | tf_op jit(solution)/shard_map/all_to_all | solution.py:268
  88.3 2.7 copy-start
  91.0 1.8 copy-start.9
  92.6 1.7 copy-start.8
  92.8 2.8 copy-start.7
  96.7 198.5 %copy-start.14 = (s32[128,23]{0,1:T(8,128)S(1)}, s32[128,23]{0,1:T(8,128)}, u32[]{:S(2)}) copy-start(s32[128,23]{0,1:T(8,128)} %param.13) | copy-start | bytes 35332
  287.5 204.1 %all-to-all-start.2 = ((bf16[16,224,1280]{2,1,0:T(8,128)(2,1)}), bf16[16,224,1280]{2,1,0:T(8,128)(2,1)}, u32[]{:S(2)}, u32[]{:S(2)}) async-start(bf16[16,224,1280]{2,1,0:T(8,128)(2,1)} %constant_dynamic-update-slice_fusion.5), calls=%async_computation.2 | async-start | bytes 18350080 | tf_op jit(solution)/shard_map/all_to_all | solution.py:268
  491.6 35.5 %all-to-all-start.1 = ((bf16[16,32,1280]{2,1,0:T(8,128)(2,1)}), bf16[16,32,1280]{2,1,0:T(8,128)(2,1)S(1)}, u32[]{:S(2)}, u32[]{:S(2)}) async-start(bf16[16,32,1280]{2,1,0:T(8,128)(2,1)} %get-tuple-element.8), calls=%async_computation.1 | async-start | bytes 2621440 | tf_op jit(solution)/shard_map/all_to_all | solution.py:270
  527.1 7.6 %copy-start.10 = (bf16[16,32,1280]{2,1,0:T(8,128)(2,1)}, bf16[16,32,1280]{2,1,0:T(8,128)(2,1)S(1)}, u32[]{:S(2)}) copy-start(bf16[16,32,1280]{2,1,0:T(8,128)(2,1)S(1)} %all-to-all-done.1) | copy-start | bytes 3932164
  527.1 35.4 %all-to-all-start.3 = ((bf16[16,32,1280]{2,1,0:T(8,128)(2,1)}), bf16[16,32,1280]{2,1,0:T(8,128)(2,1)S(1)}, u32[]{:S(2)}, u32[]{:S(2)}) async-start(bf16[16,32,1280]{2,1,0:T(8,128)(2,1)} %get-tuple-element.9), calls=%async_computation.3 | async-start | bytes 2621440 | tf_op jit(solution)/shard_map/all_to_all | solution.py:270
  562.5 1.1 copy-start.11

commit v8 on v6

--- a/solution.py
+++ b/solution.py
@@ -93,11 +93,11 @@
 
 
 FAR_SLOTS = 4
-HEAD_CHUNKS = 4
+INTERPRET = False
 
 
 def attention_kernel(
-    far_key_ref, far_value_ref, query_ref, near_key_ref, near_value_ref, near_bias_ref,
+    query_ref, near_key_ref, near_value_ref, far_key_ref, far_value_ref, near_bias_ref,
     far_bias_ref, out_ref, log_ref
 ):
     def flat(ref):
@@ -129,35 +129,38 @@
     log_ref[...] = log_total
 
 
-def attend(got, unit, near_bias, far_bias):
-    group_size, _, channels = got.shape
+def attend(got_query, got_keys, unit, near_bias, far_bias):
+    group_size, clients, _, channels = got_query.shape
+    half = got_keys.shape[0]
     far_rows = FAR_SLOTS * 16
     rows = group_size * unit
     heads = channels // HEAD_DIM
-    base = 2 * far_rows // unit
-    far_spec = (group_size, far_rows, HEAD_DIM)
-    own_spec = (group_size, unit, HEAD_DIM)
+    far_base = 4 * unit // far_rows
+    query_spec = (group_size, None, unit, HEAD_DIM)
+    near_spec = (half, unit, HEAD_DIM)
+    far_spec = (half, far_rows, HEAD_DIM)
     return pl.pallas_call(
         attention_kernel,
-        grid=(heads,),
+        grid=(clients, heads),
         in_specs=[
-            pl.BlockSpec(far_spec, lambda h: (0, 0, h)),
-            pl.BlockSpec(far_spec, lambda h: (0, 1, h)),
-            pl.BlockSpec(own_spec, lambda h: (0, base, h)),
-            pl.BlockSpec(own_spec, lambda h: (0, base + 1, h)),
-            pl.BlockSpec(own_spec, lambda h: (0, base + 2, h)),
-            pl.BlockSpec((rows, rows), lambda h: (0, 0)),
-            pl.BlockSpec((rows, group_size * far_rows), lambda h: (0, 0)),
+            pl.BlockSpec(query_spec, lambda k, h: (0, k, 0, h)),
+            pl.BlockSpec(near_spec, lambda k, h: (0, k, h)),
+            pl.BlockSpec(near_spec, lambda k, h: (0, 2 + k, h)),
+            pl.BlockSpec(far_spec, lambda k, h: (0, far_base + k, h)),
+            pl.BlockSpec(far_spec, lambda k, h: (0, far_base + 2 + k, h)),
+            pl.BlockSpec((None, rows, half * unit), lambda k, h: (k, 0, 0)),
+            pl.BlockSpec((None, rows, half * far_rows), lambda k, h: (k, 0, 0)),
         ],
         out_specs=[
-            pl.BlockSpec(own_spec, lambda h: (0, 0, h)),
-            pl.BlockSpec((None, rows, 1), lambda h: (h, 0, 0)),
+            pl.BlockSpec(query_spec, lambda k, h: (0, k, 0, h)),
+            pl.BlockSpec((None, None, rows, 1), lambda k, h: (k, h, 0, 0)),
         ],
         out_shape=[
-            jax.ShapeDtypeStruct((group_size, unit, channels), jnp.bfloat16),
-            jax.ShapeDtypeStruct((heads, rows, 1), jnp.float32),
+            jax.ShapeDtypeStruct((group_size, clients, unit, channels), jnp.float32),
+            jax.ShapeDtypeStruct((clients, heads, rows, 1), jnp.float32),
         ],
-    )(got, got, got, got, got, near_bias, far_bias)
+        interpret=INTERPRET,
+    )(got_query, got_keys, got_keys, got_keys, got_keys, near_bias, far_bias)
 
 
 def class_of(devices, frame_devs):
@@ -172,23 +175,35 @@
     return picked, jnp.any(hit, axis=-2)
 
 
+def log_add(first, second):
+    top = jnp.maximum(first, second)
+    return top + jnp.log(jnp.exp(first - top) + jnp.exp(second - top))
+
+
 def shards(query_feats, key_feats, value_feats, owner_map, pattern):
     group_size = lax.axis_size("seq")
+    half = group_size // 2
     device = lax.axis_index("seq")
     local_rows, channels = query_feats.shape
+    heads = channels // HEAD_DIM
     strips = local_rows // (4 * WIDTH)
     blocks = WIDTH // 4
     piece_count = strips * blocks
     tile_count = owner_map.shape[0]
+    class_count = tile_count // piece_count
     own_count = tile_count // group_size
     capacity = (piece_count + group_size - 1) // group_size
     unit = capacity * 16
     frame_devs = group_size // FRAMES
     devices = jnp.arange(group_size, dtype=jnp.int32)
+    shifts = jnp.arange(half, dtype=jnp.int32)
     local_iota = jnp.arange(piece_count, dtype=jnp.int32)
     cap_iota = jnp.arange(capacity, dtype=jnp.int32)
     slice_iota = jnp.arange(4, dtype=jnp.int32)
     token_iota = jnp.arange(16, dtype=jnp.int32)
+
+    def partner(ids):
+        return (ids + half) % group_size
 
     def piece_rows(pieces):
         strip = pieces // blocks
@@ -201,70 +216,95 @@
         )
 
     own_rank, class_rank = owner_tables(owner_map, group_size, piece_count)
+    owner_by_class = owner_map.reshape(class_count, piece_count)
+    rank_by_class = class_rank.reshape(class_count, piece_count)
     my_class = class_of(device, frame_devs)
-    my_tiles = my_class * piece_count + local_iota
     my_owner = lax.dynamic_slice_in_dim(owner_map, my_class * piece_count, piece_count)
     my_slot = lax.dynamic_slice_in_dim(class_rank, my_class * piece_count, piece_count)
-    send_hit = (my_owner[None, None, :] == devices[:, None, None]) & (
-        my_slot[None, None, :] == cap_iota[None, :, None]
-    )
-    send_index = jnp.sum(jnp.where(send_hit, local_iota[None, None, :], 0), axis=2)
-    own_send_rows = piece_rows(send_index).reshape(group_size, unit)
     requests = request_table(owner_map, pattern, group_size)
-    wanted = (requests >= 0) & (requests // piece_count == my_class)
-    far_send_piece, _ = ranked_pick(requests % piece_count, wanted, FAR_SLOTS)
-    far_send_rows = piece_rows(far_send_piece).reshape(group_size, FAR_SLOTS * 16)
-    source_class = class_of(devices, frame_devs)
-    class_tiles = source_class[:, None] * piece_count + local_iota[None, :]
-    class_count = tile_count // piece_count
-    mine = pick_rows(owner_map.reshape(class_count, piece_count), source_class) == device
-    near_hit = mine[:, None, :] & (
-        pick_rows(class_rank.reshape(class_count, piece_count), source_class)[:, None, :]
-        == cap_iota[None, :, None]
-    )
-    near_tile = jnp.sum(jnp.where(near_hit, class_tiles[:, None, :], 0), axis=2)
-    near_tile_rows = jnp.broadcast_to(near_tile[:, :, None], (group_size, capacity, 16)).reshape(-1)
-    my_requests = lax.dynamic_index_in_dim(requests, device, axis=0, keepdims=False)
-    far_wanted = (my_requests[None, :] >= 0) & (
-        my_requests[None, :] // piece_count == source_class[:, None]
-    )
-    far_tile, far_valid = ranked_pick(
-        jnp.broadcast_to(my_requests[None, :], (group_size, group_size)), far_wanted, FAR_SLOTS
-    )
-    far_tile = jnp.where(far_valid, far_tile, -1)
-    far_tile_rows = jnp.broadcast_to(
-        far_tile[:, :, None], (group_size, FAR_SLOTS, 16)
-    ).reshape(-1)
+
+    def my_pieces(owners):
+        hit = (my_owner == owners[..., None, None]) & (my_slot == cap_iota[:, None])
+        return jnp.sum(jnp.where(hit, local_iota, 0), axis=-1)
+
+    def far_pieces(clients, source_class):
+        asked = pick_rows(requests, clients)
+        wanted = (asked >= 0) & (asked // piece_count == source_class)
+        return ranked_pick(asked, wanted, FAR_SLOTS)
+
+    clients_of = jnp.stack([devices, partner(devices)], axis=1)
+    query_rows = piece_rows(my_pieces(clients_of)).reshape(-1)
+    half_base = device // half * half
+    key_dests = half_base + (device % half + shifts) % half
+    dest_clients = pick_rows(clients_of, key_dests)
+    near_rows = piece_rows(my_pieces(dest_clients)).reshape(half, -1)
+    far_tiles, _ = far_pieces(dest_clients, my_class)
+    far_rows = piece_rows(far_tiles % piece_count).reshape(half, -1)
+    sent_query = jnp.take(query_feats, query_rows, axis=0).reshape(group_size, -1, channels)
+    payload = jnp.concatenate(
+        [
+            jnp.take(key_feats, near_rows.reshape(-1), axis=0).reshape(half, -1, channels),
+            jnp.take(value_feats, near_rows.reshape(-1), axis=0).reshape(half, -1, channels),
+            jnp.take(key_feats, far_rows.reshape(-1), axis=0).reshape(half, -1, channels),
+            jnp.take(value_feats, far_rows.reshape(-1), axis=0).reshape(half, -1, channels),
+        ],
+        axis=1,
+    )
+    got_query = lax.all_to_all(sent_query, "seq", split_axis=0, concat_axis=0, tiled=True)
+    got_query = got_query.reshape(group_size, 2, unit, channels)
+    received = [payload[0]]
+    for shift in range(1, half):
+        pairs = [(d, d // half * half + (d % half + shift) % half) for d in range(group_size)]
+        received.append(lax.ppermute(payload[shift], "seq", pairs))
+    got_keys = jnp.stack(received, axis=0)
+    key_sources = half_base + (device % half - shifts) % half
+    key_source_class = class_of(key_sources, frame_devs)
+    all_class = class_of(devices, frame_devs)
+    near_biases = []
+    far_biases = []
+    for client in (device, partner(device)):
+        def own_tiles_of(source_class):
+            mine = pick_rows(owner_by_class, source_class) == client
+            ranks = pick_rows(rank_by_class, source_class)
+            hit = mine[:, None, :] & (ranks[:, None, :] == cap_iota[None, :, None])
+            tiles = source_class[:, None, None] * piece_count + local_iota
+            return jnp.sum(jnp.where(hit, tiles, 0), axis=2)
+
+        query_tiles = own_tiles_of(all_class)
+        query_tile_rows = jnp.broadcast_to(
+            query_tiles[:, :, None], (group_size, capacity, 16)
+        ).reshape(-1)
+        near_tiles = own_tiles_of(key_source_class)
+        near_tile_rows = jnp.broadcast_to(near_tiles[:, :, None], (half, capacity, 16)).reshape(-1)
+        client_far, client_valid = far_pieces(
+            jnp.broadcast_to(client, (half,)), key_source_class[:, None]
+        )
+        client_far = jnp.where(client_valid, client_far, -1)
+        far_tile_rows = jnp.broadcast_to(
+            client_far[:, :, None], (half, FAR_SLOTS, 16)
+        ).reshape(-1)
+        own_ids = owned_tiles(owner_map, own_rank, client, own_count)
+        listed = pick_rows(pattern, own_ids)
+        near_ok = jnp.any(listed[:, :, None] == near_tile_rows[None, None, :], axis=1)
+        far_ok = jnp.any(listed[:, :, None] == far_tile_rows[None, None, :], axis=1)
+        query_own = pick(own_rank, query_tile_rows)
+        near_biases.append(
+            jnp.where(jnp.take(near_ok, query_own, axis=0), 0.0, masked_score).astype(jnp.float32)
+        )
+        far_biases.append(
+            jnp.where(jnp.take(far_ok, query_own, axis=0), 0.0, masked_score).astype(jnp.float32)
+        )
+    mixed, head_logs = attend(
+        got_query, got_keys, unit, jnp.stack(near_biases), jnp.stack(far_biases)
+    )
+    head_logs = head_logs[..., 0]
+    sent_logs = head_logs.reshape(2, heads, group_size, unit).transpose(2, 0, 3, 1)
+    returned = lax.all_to_all(mixed, "seq", split_axis=0, concat_axis=0, tiled=True)
+    returned_logs = lax.all_to_all(sent_logs, "seq", split_axis=0, concat_axis=0, tiled=True)
+    partner_pairs = [(d, (d + half) % group_size) for d in range(group_size)]
+    partner_logs = lax.ppermute(head_logs[1], "seq", partner_pairs)
+    total_logs = log_add(head_logs[0], partner_logs)
     own_ids = owned_tiles(owner_map, own_rank, device, own_count)
-    listed = pick_rows(pattern, own_ids)
-    near_ok = jnp.any(listed[:, :, None] == near_tile_rows[None, None, :], axis=1)
-    far_ok = jnp.any(listed[:, :, None] == far_tile_rows[None, None, :], axis=1)
-    query_own = pick(own_rank, near_tile_rows)
-    near_bias = jnp.where(jnp.take(near_ok, query_own, axis=0), 0.0, masked_score)
-    far_bias = jnp.where(jnp.take(far_ok, query_own, axis=0), 0.0, masked_score)
-    near_bias = near_bias.astype(jnp.float32)
-    far_bias = far_bias.astype(jnp.float32)
-    chunk_width = channels // HEAD_CHUNKS
-    outputs = []
-    logs = []
-    taken = lax.optimization_barrier(
-        (
-            jnp.take(key_feats, far_send_rows.reshape(-1), axis=0).reshape(group_size, -1, channels),
-            jnp.take(value_feats, far_send_rows.reshape(-1), axis=0).reshape(group_size, -1, channels),
-            jnp.take(query_feats, own_send_rows.reshape(-1), axis=0).reshape(group_size, -1, channels),
-            jnp.take(key_feats, own_send_rows.reshape(-1), axis=0).reshape(group_size, -1, channels),
-            jnp.take(value_feats, own_send_rows.reshape(-1), axis=0).reshape(group_size, -1, channels),
-        )
-    )
-    for chunk in range(HEAD_CHUNKS):
-        columns = slice(chunk * chunk_width, (chunk + 1) * chunk_width)
-        sent = jnp.concatenate([part[:, :, columns] for part in taken], axis=1)
-        got = lax.all_to_all(sent, "seq", split_axis=0, concat_axis=0, tiled=True)
-        mixed, head_logs = attend(got, unit, near_bias, far_bias)
-        returned = lax.all_to_all(mixed, "seq", split_axis=0, concat_axis=0, tiled=True)
-        outputs.append(returned.reshape(-1, chunk_width))
-        logs.append(head_logs[:, :, 0])
-    head_logs = jnp.concatenate(logs, axis=0)
     own_class = own_ids // piece_count
     own_slot = pick(class_rank, own_ids)
     gather_rows = (
@@ -272,9 +312,8 @@
         + own_slot[:, None]
     )
     log_rows = (gather_rows[:, :, None] * 16 + token_iota).reshape(-1)
-    heads = channels // HEAD_DIM
     log_sums = (
-        jnp.take(head_logs, log_rows, axis=1)
+        jnp.take(total_logs, log_rows, axis=1)
         .reshape(heads, own_count, 64)
         .transpose(1, 0, 2)
         .reshape(1, own_count, heads * 64)
@@ -285,9 +324,24 @@
     column = local_iota_rows % WIDTH
     piece = strip * blocks + column // 4
     token = height * 4 + column % 4
-    back_rows = (pick(my_owner, piece) * capacity + pick(my_slot, piece)) * 16 + token
-    attended = jnp.take(jnp.concatenate(outputs, axis=1), back_rows, axis=0)
-    return (attended, log_sums)
+    row_owner = pick(my_owner, piece)
+    row_slot = pick(my_slot, piece)
+    first_rows = ((row_owner * 2) * capacity + row_slot) * 16 + token
+    second_rows = ((partner(row_owner) * 2 + 1) * capacity + row_slot) * 16 + token
+    flat_out = returned.reshape(-1, channels)
+    flat_logs = returned_logs.reshape(-1, heads)
+    first_logs = jnp.take(flat_logs, first_rows, axis=0)
+    second_logs = jnp.take(flat_logs, second_rows, axis=0)
+    joint = log_add(first_logs, second_logs)
+    first_weight = jnp.exp(first_logs - joint)[:, :, None]
+    second_weight = jnp.exp(second_logs - joint)[:, :, None]
+    first_out = jnp.take(flat_out, first_rows, axis=0)
+    second_out = jnp.take(flat_out, second_rows, axis=0)
+    attended = (
+        first_out.reshape(local_rows, heads, HEAD_DIM) * first_weight
+        + second_out.reshape(local_rows, heads, HEAD_DIM) * second_weight
+    )
+    return (attended.reshape(local_rows, channels).astype(jnp.bfloat16), log_sums)
 
 
 def solution(mesh):

time: 585 us -> 700 us (1.20)
  waiting for transfers between devices: 87.7 us -> 419 us
  blocking collectives: 319 us -> 21.8 us
  local copies, waits for them, and re-layouts: 60.2 us -> 128 us
  other arithmetic: 30.3 us -> 46.5 us
    ppermute x0 -> x8, waiting for transfers between devices: none -> 419 us  [the longest x1 217 us: shards(): partner_logs = lax.ppermute(head_logs[1], 'seq', partner_pairs)]
    all_to_all x3 -> x1, blocking collectives: 319 us -> 21.8 us  [shards(): lax.all_to_all(sent_logs, 'seq', split_axis=0, concat_axis=0, tiled=True)]
    all_to_all x1, waiting for transfers between devices: 75.8 us -> 0.01 us  [shards(): lax.all_to_all(sent_query, 'seq', split_axis=0, concat_axis=0, tiled=True)]
    gather x9 -> x15, local copies, waits for them, and re-layouts: 45.6 us -> 64.4 us  [the longest x1 12.5 us: shards(): jnp.take(value_feats, far_rows.reshape(-1), axis=0)]
    mul x0 -> x4, local copies, waits for them, and re-layouts: none -> 17.9 us  [the longest x2 8.96 us: shards(): first_out.reshape(local_rows, heads, HEAD_DIM) * first_weight]
    all_to_all x4 -> x1, starting transfers between devices: 19.8 us -> 7.41 us  [shards(): lax.all_to_all(mixed, 'seq', split_axis=0, concat_axis=0, tiled=True)]
    all_to_all x4 -> x1, waiting for transfers between devices: 11.8 us -> 0.01 us  [shards(): lax.all_to_all(mixed, 'seq', split_axis=0, concat_axis=0, tiled=True)]
    convert_element_type x0 -> x1, other arithmetic: none -> 9.29 us  [shards(): attended.reshape(local_rows, channels).astype(jnp.bfloat16)]
  transfers between devices with their start and end apart: 5 -> 10, of which waited for: 5 -> 7; matrix products, arithmetic and copies ran while one was open for 3% -> 11% of each run, Pallas kernels for 10% -> 0%
where the time goes in v8:
time: 700 us; the launch traced here: 694 us
  waiting for transfers between devices  419 us (60%)
  local copies, waits for them, and re-layouts  128 us (18%)
  Pallas kernels  56.9 us (8%)
  other arithmetic  46.5 us (7%)
  blocking collectives  21.8 us (3%)
  starting transfers between devices  21 us (3%)
    ppermute x1, waiting for transfers between devices, shards(): partner_logs = lax.ppermute(head_logs[1], 'seq', partner_pairs)  217 us
    ppermute x7, waiting for transfers between devices, shards(): received.append(lax.ppermute(payload[shift], 'seq', pairs))  201 us
    pallas_call x1, Pallas kernels, attend(): pl.pallas_call(attention_kernel, grid=(clients, heads), in_specs=[pl.Bloc...  56.9 us
    all_to_all x1, blocking collectives, shards(): lax.all_to_all(sent_logs, 'seq', split_axis=0, concat_axis=0, tiled=True)  21.8 us
    unnamed x26, local copies, waits for them, and re-layouts  17 us
  transfers between devices with their start and end apart: 10, of which 7 were waited for; matrix products, arithmetic and copies ran while one was open for 11% of the time, Pallas kernels for 0%

profile of v8, /device:TPU:13, one launch (start us, length us, event | category | flops | bytes accessed | tf_op | source)
XLA Modules:
  0.0 694.5 jit_solution(8879808892604965827)
XLA Ops:
  1.1 0.9 iota_compare_fusion.12
  2.0 1.8 select_reduce_fusion
  3.8 0.7 broadcast_compare_fusion.1
  4.5 0.8 select_reduce_fusion.3
  5.3 0.3 select_reduce_fusion.5
  5.8 0.4 reduce_window_sum.39
  6.8 0.7 eq.654
  7.5 6.3 gather_fusion.4
  13.9 12.5 %gather_fusion.5 = bf16[1024,2560]{1,0:T(8,128)(2,1)} fusion(bf16[512,2560]{1,0:T(8,128)(2,1)} %param.19, s32[1024]{0:T(1024)S(1)} %fusion.39), kind=kCustom, calls=%fused_computation.7.clone | custom fusion | bytes 10489856 | tf_op jit(solution)/shard_map/jit(_take)/gather | solution.py:249
  27.5 3.5 gather_fusion.2
  31.0 8.2 %gather_fusion.3 = bf16[512,2560]{1,0:T(8,128)(2,1)} fusion(bf16[512,2560]{1,0:T(8,128)(2,1)} %param.19, s32[1024]{0:T(1024)S(1)} %pad_clamp_fusion.5), kind=kCustom, calls=%fused_computation.8.clone | custom fusion | bytes 5244928 | tf_op jit(solution)/shard_map/jit(_take)/gather | solution.py:247
  39.2 8.5 %broadcast_select_fusion.1 = (bf16[1024,2560]{1,0:T(8,128)(2,1)S(1)}, bf16[1024,2560]{1,0:T(8,128)(2,1)}) fusion(bf16[1024,2560]{1,0:T(8,128)(2,1)} %gather_fusion.4, pred[1024]{0:T(1024)(128)(4,1)S(1)} %compare_and_fusion.1, bf16[1024,2560]{1,0:T(8,128)(2,1)} %gather_fusion.5), kind=kLoop, calls=%fused_computation.22 | loop fusion | flops 5242880 | bytes 20972544 | tf_op jit(solution)/shard_map/jit(_take)/select_n | solution.py:248
  47.8 2.2 broadcast_select_fusion.4
  50.0 5.7 pad_maximum_fusion
  55.7 5.8 slice_bitcast_fusion
  61.5 1.9 collective-permute-start.1
  63.4 0.4 collective-permute-start.2
  63.8 0.9 collective-permute-start.3
  64.8 2.0 collective-permute-start.4
  67.5 6.3 gather_fusion.1
  73.8 5.3 broadcast_select_fusion.2
  79.1 6.1 all-to-all-start
  89.0 0.9 select_reduce_fusion.7
  90.0 0.4 select_reduce_fusion.2
  90.4 1.8 gather_fusion.9
  92.3 1.7 gather_fusion.7
  94.4 1.8 gather_fusion.8
  96.4 1.7 gather_fusion.6
  98.3 1.0 pad_maximum_fusion.2.near_bias_ref
  99.8 1.5 pad_maximum_fusion.1.far_bias_ref
  101.3 16.4 %collective-permute-done = bf16[384,2560]{1,0:T(8,128)(2,1)} collective-permute-done((bf16[384,2560]{1,0:T(8,128)(2,1)}, bf16[384,2560]{1,0:T(8,128)(2,1)}, u32[]{:S(2)}, u32[]{:S(2)}) %collective-permute-start) | collective-permute-done | bytes 1966112 | tf_op jit(solution)/shard_map/ppermute | solution.py:258
  117.7 3.0 bitcast_dynamic-update-slice_fusion.6
  120.7 70.1 %collective-permute-done.1 = bf16[384,2560]{1,0:T(8,128)(2,1)} collective-permute-done((bf16[384,2560]{1,0:T(8,128)(2,1)}, bf16[384,2560]{1,0:T(8,128)(2,1)}, u32[]{:S(2)}, u32[]{:S(2)}) %collective-permute-start.1) | collective-permute-done | bytes 1966112 | tf_op jit(solution)/shard_map/ppermute | solution.py:258
  190.7 3.0 bitcast_dynamic-update-slice_fusion.5
  193.7 22.4 %collective-permute-done.2 = bf16[384,2560]{1,0:T(8,128)(2,1)} collective-permute-done((bf16[384,2560]{1,0:T(8,128)(2,1)}, bf16[384,2560]{1,0:T(8,128)(2,1)}, u32[]{:S(2)}, u32[]{:S(2)}) %collective-permute-start.2) | collective-permute-done | bytes 1966112 | tf_op jit(solution)/shard_map/ppermute | solution.py:258
  216.1 3.0 bitcast_dynamic-update-slice_fusion.4
  219.0 46.2 %collective-permute-done.3 = bf16[384,2560]{1,0:T(8,128)(2,1)} collective-permute-done((bf16[384,2560]{1,0:T(8,128)(2,1)}, bf16[384,2560]{1,0:T(8,128)(2,1)}, u32[]{:S(2)}, u32[]{:S(2)}) %collective-permute-start.3) | collective-permute-done | bytes 1966112 | tf_op jit(solution)/shard_map/ppermute | solution.py:258
  265.2 3.0 bitcast_dynamic-update-slice_fusion.3
  268.3 2.9 bitcast_dynamic-update-slice_fusion.2
  271.2 46.0 %collective-permute-done.5 = bf16[384,2560]{1,0:T(8,128)(2,1)S(1)} collective-permute-done((bf16[384,2560]{1,0:T(8,128)(2,1)S(1)}, bf16[384,2560]{1,0:T(8,128)(2,1)S(1)}, u32[]{:S(2)}, u32[]{:S(2)}) %collective-permute-start.5) | collective-permute-done | bytes 1966112 | tf_op jit(solution)/shard_map/ppermute | solution.py:258
  317.2 1.5 bitcast_dynamic-update-slice_fusion.1
  318.7 0.4 collective-permute-done.6
  319.1 1.4 bitcast_dynamic-update-slice_fusion.near_key_ref.near_value_ref.far_key_ref.far_value_ref
  320.5 56.9 %shard_map.68 = (f32[16,2,32,2560]{3,2,1,0:T(8,128)}, f32[2,20,512,1]{3,2,1,0:T(8,128)}) custom-call(bf16[16,2,32,2560]{3,2,1,0:T(8,128)(2,1)} %bitcast.1.query_ref, bf16[8,384,2560]{2,1,0:T(8,128)(2,1)} %bitcast_dynamic-update-slice_fusion.near_key_ref.near_value_ref.far_key_ref.far_value_ref, ...), custom_call_target="tpu_custom_call" | custom-call | tf_op jit(solution)/shard_map/pallas_call | solution.py:142
  377.4 6.0 copy.115
  383.8 0.3 reshape.1211
  384.1 21.8 %all_to_all.15 = f32[16,1,1280]{2,1,0:T(1,128)S(1)} all-to-all(f32[16,1,1280]{2,1,0:T(1,128)S(1)} %reshape.1211), channel_id=1, replica_groups=mesh['groups'=2,'seq'=16] {'seq'}, dimensions={0} | all-to-all | bytes 163840 | tf_op jit(solution)/shard_map/all_to_all | solution.py:303
  405.9 7.4 %all-to-all-start.1 = ((f32[16,2,32,2560]{3,2,1,0:T(8,128)}), f32[16,2,32,2560]{3,2,1,0:T(8,128)}, u32[]{:S(2)}, u32[]{:S(2)}) async-start(f32[16,2,32,2560]{3,2,1,0:T(8,128)} %get-tuple-element.8), calls=%async_computation.1 | async-start | bytes 20971520 | tf_op jit(solution)/shard_map/all_to_all | solution.py:302
  414.0 6.8 slice_reduce_fusion.1
  420.8 2.2 collective-permute-start.7
  423.0 217.4 %collective-permute-done.7 = f32[20,512]{1,0:T(8,128)S(1)} collective-permute-done((f32[20,512]{1,0:T(8,128)S(1)}, f32[20,512]{1,0:T(8,128)S(1)}, u32[]{:S(2)}, u32[]{:S(2)}) %collective-permute-start.7) | collective-permute-done | bytes 40992 | tf_op jit(solution)/shard_map/ppermute | solution.py:305
  640.6 1.0 gather_fusion
  641.8 0.7 reshape.1057
  642.5 0.5 broadcast.1667
  643.0 0.8 reduce.4
  644.4 1.0 gather_fusion.11
  645.5 1.0 gather_fusion.12
  646.8 3.1 mul.210
  649.8 5.9 copy.120
  655.7 3.0 mul.213
  658.7 5.9 copy.121
  664.6 10.3 %gather_fusion.10 = f32[512,2560]{1,0:T(8,128)} fusion(f32[1024,2560]{1,0:T(8,128)} %bitcast.24, s32[1024]{0:T(1024)S(1)} %get-tuple-element.77), kind=kCustom, calls=%fused_computation.4.clone | custom fusion | bytes 10487808 | tf_op jit(solution)/shard_map/jit(_take)/gather | solution.py:338
  674.9 10.2 %gather_fusion.13 = f32[512,2560]{1,0:T(8,128)} fusion(f32[1024,2560]{1,0:T(8,128)} %bitcast.24, s32[1024]{0:T(1024)S(1)} %get-tuple-element.76), kind=kCustom, calls=%fused_computation.11.clone | custom fusion | bytes 10487808 | tf_op jit(solution)/shard_map/jit(_take)/gather | solution.py:339
  685.2 9.3 %fusion.1 = bf16[512,2560]{1,0:T(8,128)(2,1)} fusion(f32[512,2560]{1,0:T(8,128)} %copy.121, f32[512,2560]{1,0:T(8,128)} %gather_fusion.13, f32[512,2560]{1,0:T(8,128)} %copy.120, f32[512,2560]{1,0:T(8,128)} %gather_fusion.10, pred[512]{0:T(512)(128)(4,1)S(1)} %get-tuple-element.56, pred[512]{0:T(512)(128)(4,1)S(1)} %get-tuple-element.32), kind=kLoop, calls=%fused_computation.17 | loop fusion | flops 7864320 | bytes 23593984 | tf_op jit(solution)/shard_map/convert_element_type | solution.py:344
  (156 shorter events, 10.4 us)
Async XLA Ops:
  0.6 6.9 copy-start
  13.9 12.5 %copy-start.8 = (s32[128]{0:T(128)S(1)}, s32[128]{0:T(128)}, u32[]{:S(2)}) copy-start(s32[128]{0:T(128)} %param.20) | copy-start | bytes 1540
  39.2 8.5 %copy-start.3 = (bf16[512,2560]{1,0:T(8,128)(2,1)S(1)}, bf16[512,2560]{1,0:T(8,128)(2,1)}, u32[]{:S(2)}) copy-start(bf16[512,2560]{1,0:T(8,128)(2,1)} %gather_fusion.2) | copy-start | bytes 7864324
  39.2 8.5 %copy-start.4 = (bf16[512,2560]{1,0:T(8,128)(2,1)S(1)}, bf16[512,2560]{1,0:T(8,128)(2,1)}, u32[]{:S(2)}) copy-start(bf16[512,2560]{1,0:T(8,128)(2,1)} %gather_fusion.3) | copy-start | bytes 7864324
  55.7 11.8 %copy-start.2 = (bf16[512,2560]{1,0:T(8,128)(2,1)S(1)}, bf16[512,2560]{1,0:T(8,128)(2,1)}, u32[]{:S(2)}) copy-start(bf16[512,2560]{1,0:T(8,128)(2,1)} %param.17) | copy-start | bytes 7864324
  61.5 56.2 %collective-permute-start = (bf16[384,2560]{1,0:T(8,128)(2,1)}, bf16[384,2560]{1,0:T(8,128)(2,1)}, u32[]{:S(2)}, u32[]{:S(2)}) collective-permute-start(bf16[384,2560]{1,0:T(8,128)(2,1)} %get-tuple-element.50), channel_id=1, source_target_pairs={{0,1},{1,2},{2,3},{3,4},{4,5},{5,6},{6,7},{7,0},{8,9},{9,10},{10,1... | collective-permute-start | bytes 5898248 | tf_op jit(solution)/shard_map/ppermute | solution.py:258
  61.5 129.2 %collective-permute-start.1 = (bf16[384,2560]{1,0:T(8,128)(2,1)}, bf16[384,2560]{1,0:T(8,128)(2,1)}, u32[]{:S(2)}, u32[]{:S(2)}) collective-permute-start(bf16[384,2560]{1,0:T(8,128)(2,1)} %get-tuple-element.49), channel_id=1, source_target_pairs={{0,2},{1,3},{2,4},{3,5},{4,6},{5,7},{6,0},{7,1},{8,10},{9,11},{10,... | collective-permute-start | bytes 5898248 | tf_op jit(solution)/shard_map/ppermute | solution.py:258
  63.4 152.6 %collective-permute-start.2 = (bf16[384,2560]{1,0:T(8,128)(2,1)}, bf16[384,2560]{1,0:T(8,128)(2,1)}, u32[]{:S(2)}, u32[]{:S(2)}) collective-permute-start(bf16[384,2560]{1,0:T(8,128)(2,1)} %get-tuple-element.48), channel_id=1, source_target_pairs={{0,3},{1,4},{2,5},{3,6},{4,7},{5,0},{6,1},{7,2},{8,11},{9,12},{10,... | collective-permute-start | bytes 5898248 | tf_op jit(solution)/shard_map/ppermute | solution.py:258
  63.8 201.4 %collective-permute-start.3 = (bf16[384,2560]{1,0:T(8,128)(2,1)}, bf16[384,2560]{1,0:T(8,128)(2,1)}, u32[]{:S(2)}, u32[]{:S(2)}) collective-permute-start(bf16[384,2560]{1,0:T(8,128)(2,1)} %get-tuple-element.47), channel_id=1, source_target_pairs={{0,4},{1,5},{2,6},{3,7},{4,0},{5,1},{6,2},{7,3},{8,12},{9,13},{10,... | collective-permute-start | bytes 5898248 | tf_op jit(solution)/shard_map/ppermute | solution.py:258
  64.8 203.5 %collective-permute-start.4 = (bf16[384,2560]{1,0:T(8,128)(2,1)}, bf16[384,2560]{1,0:T(8,128)(2,1)}, u32[]{:S(2)}, u32[]{:S(2)}) collective-permute-start(bf16[384,2560]{1,0:T(8,128)(2,1)} %get-tuple-element.46), channel_id=1, source_target_pairs={{0,5},{1,6},{2,7},{3,0},{4,1},{5,2},{6,3},{7,4},{8,13},{9,14},{10,... | collective-permute-start | bytes 5898248 | tf_op jit(solution)/shard_map/ppermute | solution.py:258
  79.1 9.9 %copy-start.7 = (s32[128,23]{0,1:T(8,128)S(1)}, s32[128,23]{0,1:T(8,128)}, u32[]{:S(2)}) copy-start(s32[128,23]{0,1:T(8,128)} %param.21) | copy-start | bytes 35332
  79.1 241.5 %all-to-all-start = ((bf16[16,64,2560]{2,1,0:T(8,128)(2,1)}), bf16[16,64,2560]{2,1,0:T(8,128)(2,1)}, u32[]{:S(2)}, u32[]{:S(2)}) async-start(bf16[16,64,2560]{2,1,0:T(8,128)(2,1)} %bitcast.61), calls=%async_computation | async-start | bytes 10485760 | tf_op jit(solution)/shard_map/all_to_all | solution.py:253
  98.1 19.6 %copy-start.6 = (bf16[384,2560]{1,0:T(8,128)(2,1)S(1)}, bf16[384,2560]{1,0:T(8,128)(2,1)}, u32[]{:S(2)}) copy-start(bf16[384,2560]{1,0:T(8,128)(2,1)} %get-tuple-element.45) | copy-start | bytes 5898244
  99.3 91.4 %copy-start.5 = (bf16[384,2560]{1,0:T(8,128)(2,1)S(1)}, bf16[384,2560]{1,0:T(8,128)(2,1)}, u32[]{:S(2)}) copy-start(bf16[384,2560]{1,0:T(8,128)(2,1)} %get-tuple-element.44) | copy-start | bytes 5898244
  117.7 199.5 %collective-permute-start.5 = (bf16[384,2560]{1,0:T(8,128)(2,1)S(1)}, bf16[384,2560]{1,0:T(8,128)(2,1)S(1)}, u32[]{:S(2)}, u32[]{:S(2)}) collective-permute-start(bf16[384,2560]{1,0:T(8,128)(2,1)S(1)} %copy-done.6), channel_id=1, source_target_pairs={{0,6},{1,7},{2,0},{3,1},{4,2},{5,3},{6,4},{7,5},{8,14},{9,15},{10,... | collective-permute-start | bytes 5898248 | tf_op jit(solution)/shard_map/ppermute | solution.py:258
  190.7 128.4 %collective-permute-start.6 = (bf16[384,2560]{1,0:T(8,128)(2,1)S(1)}, bf16[384,2560]{1,0:T(8,128)(2,1)S(1)}, u32[]{:S(2)}, u32[]{:S(2)}) collective-permute-start(bf16[384,2560]{1,0:T(8,128)(2,1)S(1)} %copy-done.5), channel_id=1, source_target_pairs={{0,7},{1,0},{2,1},{3,2},{4,3},{5,4},{6,5},{7,6},{8,15},{9,8},{10,9... | collective-permute-start | bytes 5898248 | tf_op jit(solution)/shard_map/ppermute | solution.py:258
  405.9 258.8 %all-to-all-start.1 = ((f32[16,2,32,2560]{3,2,1,0:T(8,128)}), f32[16,2,32,2560]{3,2,1,0:T(8,128)}, u32[]{:S(2)}, u32[]{:S(2)}) async-start(f32[16,2,32,2560]{3,2,1,0:T(8,128)} %get-tuple-element.8), calls=%async_computation.1 | async-start | bytes 20971520 | tf_op jit(solution)/shard_map/all_to_all | solution.py:302
  420.8 219.6 %collective-permute-start.7 = (f32[20,512]{1,0:T(8,128)S(1)}, f32[20,512]{1,0:T(8,128)S(1)}, u32[]{:S(2)}, u32[]{:S(2)}) collective-permute-start(f32[20,512]{1,0:T(8,128)S(1)} %get-tuple-element.13), channel_id=1, source_target_pairs={{0,8},{1,9},{2,10},{3,11},{4,12},{5,13},{6,14},{7,15},{8,0},{9,1},... | collective-permute-start | bytes 122888 | tf_op jit(solution)/shard_map/ppermute | solution.py:305
  685.2 9.3 %copy-start.1 = (bf16[512,2560]{1,0:T(8,128)(2,1)S(1)}, bf16[512,2560]{1,0:T(8,128)(2,1)}, u32[]{:S(2)}) copy-start(bf16[512,2560]{1,0:T(8,128)(2,1)} %param.18) | copy-start | bytes 7864324

commit v9 on v5

--- a/solution.py
+++ b/solution.py
@@ -261,8 +261,7 @@
         sent = jnp.concatenate([part[:, :, columns] for part in taken], axis=1)
         got = lax.all_to_all(sent, "seq", split_axis=0, concat_axis=0, tiled=True)
         mixed, head_logs = attend(got, unit, near_bias, far_bias)
-        returned = lax.all_to_all(mixed, "seq", split_axis=0, concat_axis=0, tiled=True)
-        outputs.append(returned.reshape(-1, chunk_width))
+        outputs.append(mixed)
         logs.append(head_logs[:, :, 0])
     head_logs = jnp.concatenate(logs, axis=0)
     own_class = own_ids // piece_count
@@ -286,7 +285,10 @@
     piece = strip * blocks + column // 4
     token = height * 4 + column % 4
     back_rows = (pick(my_owner, piece) * capacity + pick(my_slot, piece)) * 16 + token
-    attended = jnp.take(jnp.concatenate(outputs, axis=1), back_rows, axis=0)
+    returned = lax.all_to_all(
+        jnp.concatenate(outputs, axis=2), "seq", split_axis=0, concat_axis=0, tiled=True
+    )
+    attended = jnp.take(returned.reshape(-1, channels), back_rows, axis=0)
     return (attended, log_sums)
 
 

time: 549 us -> 569 us (1.036)
  waiting for transfers between devices: 189 us -> 214 us
    all_to_all x2 -> x1, waiting for transfers between devices: 26.9 us -> 51.4 us  [shards(): lax.all_to_all(jnp.concatenate(outputs, axis=2), 'seq', split_axis=0, con...]
  transfers between devices with their start and end apart: 3 -> 2, of which waited for: 3 -> 2; matrix products, arithmetic and copies ran while one was open for 3% -> 3% of each run, Pallas kernels for 10% -> 5%
where the time goes in v9:
time: 569 us; the launch traced here: 568 us
  waiting for transfers between devices  214 us (38%)
  blocking collectives  205 us (36%)
  Pallas kernels  53.8 us (9%)
  local copies, waits for them, and re-layouts  53.7 us (9%)
  other arithmetic  29.8 us (5%)
  starting transfers between devices  10.8 us (2%)
    all_to_all x1, blocking collectives, shards(): got = lax.all_to_all(sent, 'seq', split_axis=0, concat_axis=0, tiled=True)  205 us
    all_to_all x1, waiting for transfers between devices, shards(): got = lax.all_to_all(sent, 'seq', split_axis=0, concat_axis=0, tiled=True)  162 us
    pallas_call x2, Pallas kernels, attend(): pl.pallas_call(attention_kernel, grid=(heads,), in_specs=[pl.BlockSpec(fa...  53.8 us
    all_to_all x1, waiting for transfers between devices, shards(): lax.all_to_all(jnp.concatenate(outputs, axis=2), 'seq', split_axis=0, con...  51.4 us
    gather x1, local copies, waits for them, and re-layouts, shards(): jnp.take(value_feats, far_send_rows.reshape(-1), axis=0)  12.5 us
  transfers between devices with their start and end apart: 2, of which 2 were waited for; matrix products, arithmetic and copies ran while one was open for 3% of the time, Pallas kernels for 5%

profile of v9, /device:TPU:13, one launch (start us, length us, event | category | flops | bytes accessed | tf_op | source)
XLA Modules:
  0.0 568.1 jit_solution(4705256869954497238)
XLA Ops:
  0.7 0.8 iota_compare_fusion.10
  1.5 1.8 select_reduce_fusion
  3.2 0.7 broadcast_compare_fusion
  3.9 0.8 select_reduce_fusion.2
  4.7 0.3 select_reduce_fusion.3
  5.1 0.2 reduce_window_sum.28
  5.2 0.1 select_reduce_fusion.11
  5.6 0.1 add_add_fusion
  5.7 0.1 add.406
  5.8 0.7 eq.369
  6.6 12.5 %gather_fusion.4 = bf16[1024,2560]{1,0:T(8,128)(2,1)} fusion(bf16[512,2560]{1,0:T(8,128)(2,1)} %param.11, s32[1024]{0:T(1024)S(1)} %fusion.18), kind=kCustom, calls=%fused_computation.2.clone | custom fusion | bytes 10489856 | tf_op jit(solution)/shard_map/jit(_take)/gather | solution.py:253
  19.1 6.3 %gather_fusion.3 = bf16[1024,2560]{1,0:T(8,128)(2,1)} fusion(bf16[512,2560]{1,0:T(8,128)(2,1)S(1)} %copy-done, s32[1024]{0:T(1024)S(1)} %fusion.18), kind=kCustom, calls=%fused_computation.clone | custom fusion | bytes 10489856 | tf_op jit(solution)/shard_map/jit(_take)/gather | solution.py:252
  25.4 0.2 convert_reduce_fusion
  25.9 0.1 select_reduce_fusion.13
  26.2 0.1 add_add_fusion.1
  26.3 0.1 add.416
  26.4 3.5 gather_fusion.6
  29.9 8.3 %gather_fusion.7 = bf16[512,2560]{1,0:T(8,128)(2,1)} fusion(bf16[512,2560]{1,0:T(8,128)(2,1)} %param.11, s32[1024]{0:T(1024)S(1)} %pad_clamp_fusion.3), kind=kCustom, calls=%fused_computation.4.clone | custom fusion | bytes 5244928 | tf_op jit(solution)/shard_map/jit(_take)/gather | solution.py:256
  38.3 3.5 gather_fusion.5
  41.8 6.0 %broadcast_select_fusion = (bf16[1024,2560]{1,0:T(8,128)(2,1)S(1)}, bf16[1024,2560]{1,0:T(8,128)(2,1)S(1)}) fusion(bf16[1024,2560]{1,0:T(8,128)(2,1)} %gather_fusion.4, pred[1024]{0:T(1024)(128)(4,1)S(1)} %compare_and_fusion.2, bf16[1024,2560]{1,0:T(8,128)(2,1)} %gather_fusion.3), kind=kLoop, calls=%fused_computation.9 | loop fusion | flops 5242880 | bytes 20972544 | tf_op jit(solution)/shard_map/jit(_take)/select_n | solution.py:253
  47.8 0.3 copy-done.5
  48.2 0.9 broadcast_select_fusion.3
  49.1 2.0 slice_dynamic-update-slice_fusion.3
  51.1 1.9 slice_dynamic-update-slice_fusion.2
  53.0 1.3 slice_dynamic-update-slice_fusion.9
  54.3 1.3 slice_dynamic-update-slice_fusion.8
  55.6 1.3 slice_dynamic-update-slice_fusion.7
  56.9 205.4 %all_to_all.15.far_key_ref.far_value_ref.query_ref.near_key_ref.near_value_ref = bf16[16,224,1280]{2,1,0:T(8,128)(2,1)} all-to-all(bf16[16,224,1280]{2,1,0:T(8,128)(2,1)S(1)} %get-tuple-element.34), channel_id=1, replica_groups=mesh['groups'=2,'seq'=16] {'seq'}, dimensions={0} | all-to-all | bytes 18350080 | tf_op jit(solution)/shard_map/all_to_all | solution.py:262
  262.3 5.9 %all-to-all-start.1 = ((bf16[16,224,1280]{2,1,0:T(8,128)(2,1)}), bf16[16,224,1280]{2,1,0:T(8,128)(2,1)}, u32[]{:S(2)}, u32[]{:S(2)}) async-start(bf16[16,224,1280]{2,1,0:T(8,128)(2,1)} %get-tuple-element.35), calls=%async_computation.1 | async-start | bytes 18350080 | tf_op jit(solution)/shard_map/all_to_all | solution.py:262
  268.3 0.2 reduce_window_sum.30
  268.5 0.1 fusion.4
  268.7 0.2 select_reduce_fusion.8
  269.0 0.1 eq.409
  269.2 0.2 reduce_window_sum.29
  269.4 0.2 select_reduce_fusion.7
  269.6 0.1 select_reduce_fusion.15
  269.7 0.2 select_reduce_fusion.14
  270.0 0.1 add.443
  270.3 0.1 select_reduce_fusion.12
  270.4 0.1 copy.27
  270.6 0.1 eq.384
  270.7 0.2 select_reduce_fusion.1
  271.1 0.5 select_reduce_fusion.4
  271.5 0.2 compare_reduce_fusion
  271.7 1.9 gather_fusion.1
  273.6 0.1 compare_reduce_fusion.1
  273.8 1.8 gather_fusion
  275.5 1.2 select_select_fusion.1.near_bias_ref
  276.7 1.6 select_select_fusion.far_bias_ref
  278.4 26.9 %shard_map.68 = (bf16[16,32,1280]{2,1,0:T(8,128)(2,1)}, f32[10,512,1]{2,1,0:T(8,128)}) custom-call(bf16[16,224,1280]{2,1,0:T(8,128)(2,1)} %all_to_all.15.far_key_ref.far_value_ref.query_ref.near_key_ref.near_value_ref, bf16[16,224,1280]{2,1,0:T(8,128)(2,1)} %all_to_all.15.far_key_ref.far_value_ref.query_ref.near_key_ref.near_value_ref, ...), custom_call_target="tpu_custom_call" | custom-call | tf_op jit(solution)/shard_map/pallas_call | solution.py:140
  305.3 162.2 %all-to-all-done.1.far_key_ref.far_value_ref.query_ref.near_key_ref.near_value_ref = bf16[16,224,1280]{2,1,0:T(8,128)(2,1)} async-done(((bf16[16,224,1280]{2,1,0:T(8,128)(2,1)}), bf16[16,224,1280]{2,1,0:T(8,128)(2,1)}, u32[]{:S(2)}, u32[]{:S(2)}) %all-to-all-start.1) | async-done | bytes 9175072 | tf_op jit(solution)/shard_map/all_to_all | solution.py:262
  467.4 26.9 %shard_map.69 = (bf16[16,32,1280]{2,1,0:T(8,128)(2,1)}, f32[10,512,1]{2,1,0:T(8,128)}) custom-call(bf16[16,224,1280]{2,1,0:T(8,128)(2,1)} %all-to-all-done.1.far_key_ref.far_value_ref.query_ref.near_key_ref.near_value_ref, bf16[16,224,1280]{2,1,0:T(8,128)(2,1)} %all-to-all-done.1.far_key_ref.far_value_ref.query_ref.near_key_ref.near_value_ref, ...), custom_call_target="tpu_custom_call" | custom-call | tf_op jit(solution)/shard_map/pallas_call | solution.py:140
  494.3 3.0 pad_maximum_fusion
  497.3 4.9 all-to-all-start.2
  502.4 0.1 select_reduce_fusion.6
  502.5 2.5 reduce
  505.0 2.5 reduce.1
  507.5 0.1 copy.29
  507.6 1.0 gather_fusion.2
  508.7 0.1 copy.30
  508.9 0.7 reshape.698
  509.6 51.4 %all-to-all-done.2 = bf16[16,32,2560]{2,1,0:T(8,128)(2,1)S(1)} async-done(((bf16[16,32,2560]{2,1,0:T(8,128)(2,1)}), bf16[16,32,2560]{2,1,0:T(8,128)(2,1)S(1)}, u32[]{:S(2)}, u32[]{:S(2)}) %all-to-all-start.2) | async-done | bytes 2621472 | tf_op jit(solution)/shard_map/all_to_all | solution.py:288
  560.9 3.5 gather_fusion.8
  564.4 3.7 broadcast_select_fusion.2
  (69 shorter events, 1.8 us)
Async XLA Ops:
  0.6 18.4 %copy-start = (bf16[512,2560]{1,0:T(8,128)(2,1)S(1)}, bf16[512,2560]{1,0:T(8,128)(2,1)}, u32[]{:S(2)}) copy-start(bf16[512,2560]{1,0:T(8,128)(2,1)} %param.10) | copy-start | bytes 7864324
  19.1 6.6 %copy-start.8 = (s32[128]{0:T(128)S(1)}, s32[128]{0:T(128)}, u32[]{:S(2)}) copy-start(s32[128]{0:T(128)} %param.12) | copy-start | bytes 1540
  29.9 8.3 %copy-start.2 = (bf16[512,2560]{1,0:T(8,128)(2,1)S(1)}, bf16[512,2560]{1,0:T(8,128)(2,1)}, u32[]{:S(2)}) copy-start(bf16[512,2560]{1,0:T(8,128)(2,1)} %param.9) | copy-start | bytes 7864324
  41.8 6.0 %copy-start.3 = (bf16[512,2560]{1,0:T(8,128)(2,1)S(1)}, bf16[512,2560]{1,0:T(8,128)(2,1)}, u32[]{:S(2)}) copy-start(bf16[512,2560]{1,0:T(8,128)(2,1)} %gather_fusion.6) | copy-start | bytes 7864324
  41.8 6.1 %copy-start.4 = (bf16[512,2560]{1,0:T(8,128)(2,1)S(1)}, bf16[512,2560]{1,0:T(8,128)(2,1)}, u32[]{:S(2)}) copy-start(bf16[512,2560]{1,0:T(8,128)(2,1)} %gather_fusion.7) | copy-start | bytes 7864324
  41.8 6.4 %copy-start.5 = (bf16[512,2560]{1,0:T(8,128)(2,1)S(1)}, bf16[512,2560]{1,0:T(8,128)(2,1)}, u32[]{:S(2)}) copy-start(bf16[512,2560]{1,0:T(8,128)(2,1)} %gather_fusion.5) | copy-start | bytes 7864324
  262.3 8.7 %copy-start.7 = (s32[128,23]{0,1:T(8,128)S(1)}, s32[128,23]{0,1:T(8,128)}, u32[]{:S(2)}) copy-start(s32[128,23]{0,1:T(8,128)} %param.13) | copy-start | bytes 35332
  262.3 205.1 %all-to-all-start.1 = ((bf16[16,224,1280]{2,1,0:T(8,128)(2,1)}), bf16[16,224,1280]{2,1,0:T(8,128)(2,1)}, u32[]{:S(2)}, u32[]{:S(2)}) async-start(bf16[16,224,1280]{2,1,0:T(8,128)(2,1)} %get-tuple-element.35), calls=%async_computation.1 | async-start | bytes 18350080 | tf_op jit(solution)/shard_map/all_to_all | solution.py:262
  305.3 189.1 %copy-start.6 = (bf16[16,32,1280]{2,1,0:T(8,128)(2,1)S(1)}, bf16[16,32,1280]{2,1,0:T(8,128)(2,1)}, u32[]{:S(2)}) copy-start(bf16[16,32,1280]{2,1,0:T(8,128)(2,1)} %get-tuple-element.18) | copy-start | bytes 3932164
  497.3 63.6 %all-to-all-start.2 = ((bf16[16,32,2560]{2,1,0:T(8,128)(2,1)}), bf16[16,32,2560]{2,1,0:T(8,128)(2,1)S(1)}, u32[]{:S(2)}, u32[]{:S(2)}) async-start(bf16[16,32,2560]{2,1,0:T(8,128)(2,1)} %pad_maximum_fusion), calls=%async_computation.2 | async-start | bytes 5242880 | tf_op jit(solution)/shard_map/all_to_all | solution.py:288
  564.4 3.7 copy-start.1

commit v10 on v5

--- a/solution.py
+++ b/solution.py
@@ -93,6 +93,7 @@
 
 
 FAR_SLOTS = 4
+INTERPRET = False
 HEAD_CHUNKS = 2
 
 
@@ -157,7 +158,53 @@
             jax.ShapeDtypeStruct((group_size, unit, channels), jnp.bfloat16),
             jax.ShapeDtypeStruct((heads, rows, 1), jnp.float32),
         ],
+        interpret=INTERPRET,
     )(got, got, got, got, got, near_bias, far_bias)
+
+
+def pack_kernel(far_hot_ref, own_hot_ref, query_ref, key_ref, value_ref, out_ref):
+    far_hot = far_hot_ref[...]
+    own_hot = own_hot_ref[...]
+    far_rows = far_hot.shape[0]
+    own_rows = own_hot.shape[0]
+
+    def select(hot, source_ref):
+        return jnp.dot(hot, source_ref[...], preferred_element_type=jnp.float32).astype(
+            out_ref.dtype
+        )
+
+    out_ref[0:far_rows, :] = select(far_hot, key_ref)
+    out_ref[far_rows : 2 * far_rows, :] = select(far_hot, value_ref)
+    base = 2 * far_rows
+    out_ref[base : base + own_rows, :] = select(own_hot, query_ref)
+    out_ref[base + own_rows : base + 2 * own_rows, :] = select(own_hot, key_ref)
+    out_ref[base + 2 * own_rows : base + 3 * own_rows, :] = select(own_hot, value_ref)
+
+
+def pack(far_rows, own_rows, query_feats, key_feats, value_feats, chunks):
+    group_size, far_count = far_rows.shape
+    own_count = own_rows.shape[1]
+    local_rows, channels = query_feats.shape
+    width = channels // chunks
+    row_iota = jnp.arange(local_rows, dtype=jnp.int32)
+    far_hot = (far_rows[:, :, None] == row_iota).astype(jnp.bfloat16)
+    own_hot = (own_rows[:, :, None] == row_iota).astype(jnp.bfloat16)
+    total = 2 * far_count + 3 * own_count
+    source_spec = pl.BlockSpec((local_rows, width), lambda c, j: (0, c))
+    return pl.pallas_call(
+        pack_kernel,
+        grid=(chunks, group_size),
+        in_specs=[
+            pl.BlockSpec((None, far_count, local_rows), lambda c, j: (j, 0, 0)),
+            pl.BlockSpec((None, own_count, local_rows), lambda c, j: (j, 0, 0)),
+            source_spec,
+            source_spec,
+            source_spec,
+        ],
+        out_specs=pl.BlockSpec((None, None, total, width), lambda c, j: (c, j, 0, 0)),
+        out_shape=jax.ShapeDtypeStruct((chunks, group_size, total, width), query_feats.dtype),
+        interpret=INTERPRET,
+    )(far_hot, own_hot, query_feats, key_feats, value_feats)
 
 
 def class_of(devices, frame_devs):
@@ -247,18 +294,9 @@
     chunk_width = channels // HEAD_CHUNKS
     outputs = []
     logs = []
-    taken = lax.optimization_barrier(
-        (
-            jnp.take(key_feats, far_send_rows.reshape(-1), axis=0).reshape(group_size, -1, channels),
-            jnp.take(value_feats, far_send_rows.reshape(-1), axis=0).reshape(group_size, -1, channels),
-            jnp.take(query_feats, own_send_rows.reshape(-1), axis=0).reshape(group_size, -1, channels),
-            jnp.take(key_feats, own_send_rows.reshape(-1), axis=0).reshape(group_size, -1, channels),
-            jnp.take(value_feats, own_send_rows.reshape(-1), axis=0).reshape(group_size, -1, channels),
-        )
-    )
+    packed = pack(far_send_rows, own_send_rows, query_feats, key_feats, value_feats, HEAD_CHUNKS)
     for chunk in range(HEAD_CHUNKS):
-        columns = slice(chunk * chunk_width, (chunk + 1) * chunk_width)
-        sent = jnp.concatenate([part[:, :, columns] for part in taken], axis=1)
+        sent = packed[chunk]
         got = lax.all_to_all(sent, "seq", split_axis=0, concat_axis=0, tiled=True)
         mixed, head_logs = attend(got, unit, near_bias, far_bias)
         returned = lax.all_to_all(mixed, "seq", split_axis=0, concat_axis=0, tiled=True)

time: 549 us -> 559 us (1.018)
  Pallas kernels: 53.8 us -> 98.1 us
  local copies, waits for them, and re-layouts: 54.8 us -> 25.4 us
    pallas_call x0 -> x1, Pallas kernels: none -> 44.4 us  [pack(): pl.pallas_call(pack_kernel, grid=(chunks, group_size), in_specs=[pl.Block...]
    gather x5 -> x0, local copies, waits for them, and re-layouts: 34.2 us -> none  [the longest x1 12.5 us: shards(): jnp.take(value_feats, far_send_rows.reshape(-1), axis=0)]
    squeeze x0 -> x1, local copies, waits for them, and re-layouts: none -> 11.5 us  [shards(): sent = packed[chunk]]
    select_n x3 -> x0, other arithmetic: 6.96 us -> none  [the longest x1 6.03 us: shards(): jnp.take(value_feats, far_send_rows.reshape(-1), axis=0)]
    unnamed x24 -> x8, local copies, waits for them, and re-layouts: 7.92 us -> 1.07 us
where the time goes in v10:
time: 559 us; the launch traced here: 558 us
  blocking collectives  205 us (37%)
  waiting for transfers between devices  189 us (34%)
  Pallas kernels  98.1 us (18%)
  local copies, waits for them, and re-layouts  25.4 us (5%)
  other arithmetic  23.5 us (4%)
  starting transfers between devices  15.7 us (3%)
    all_to_all x1, blocking collectives, shards(): got = lax.all_to_all(sent, 'seq', split_axis=0, concat_axis=0, tiled=True)  205 us
    all_to_all x1, waiting for transfers between devices, shards(): got = lax.all_to_all(sent, 'seq', split_axis=0, concat_axis=0, tiled=True)  163 us
    pallas_call x2, Pallas kernels, attend(): pl.pallas_call(attention_kernel, grid=(heads,), in_specs=[pl.BlockSpec(fa...  53.8 us
    pallas_call x1, Pallas kernels, pack(): pl.pallas_call(pack_kernel, grid=(chunks, group_size), in_specs=[pl.Block...  44.4 us
    all_to_all x2, waiting for transfers between devices, shards(): lax.all_to_all(mixed, 'seq', split_axis=0, concat_axis=0, tiled=True)  26.4 us
    squeeze x1, local copies, waits for them, and re-layouts, shards(): sent = packed[chunk]  11.5 us
  transfers between devices with their start and end apart: 3, of which 3 were waited for; matrix products, arithmetic and copies ran while one was open for 3% of the time, Pallas kernels for 10%

profile of v10, /device:TPU:13, one launch (start us, length us, event | category | flops | bytes accessed | tf_op | source)
XLA Modules:
  0.0 558.1 jit_solution(14265487340107441685)
XLA Ops:
  0.7 0.7 iota_compare_fusion.12
  1.3 0.7 eq.381
  2.1 1.8 select_reduce_fusion
  3.8 0.7 broadcast_compare_fusion
  4.5 0.8 select_reduce_fusion.2
  5.3 0.3 select_reduce_fusion.3
  5.7 0.2 reduce_window_sum.28
  5.8 0.1 select_reduce_fusion.11
  6.2 0.1 add.516
  6.4 0.1 add.523
  6.5 0.1 add.518
  6.6 0.1 add.527
  6.7 1.2 fusion.far_hot_ref
  7.9 0.2 convert_reduce_fusion
  8.1 0.1 reshape.874
  8.2 0.7 dynamic_slice.10
  9.1 0.1 select_reduce_fusion.13
  9.2 0.1 copy.25
  9.4 0.1 add.531
  9.6 0.1 add.538
  9.9 1.0 fusion.1.own_hot_ref
  10.9 44.4 %shard_map.68 = bf16[2,16,224,1280]{3,2,1,0:T(8,128)(2,1)} custom-call(bf16[16,64,512]{2,1,0:T(8,128)(2,1)} %fusion.far_hot_ref, bf16[16,32,512]{2,1,0:T(8,128)(2,1)} %fusion.1.own_hot_ref, bf16[512,2560]{1,0:T(8,128)(2,1)} %query_ref.1, bf16[512,2560]{1,0:T(8,128)(2,1)} %key_ref.1, bf16[512,2560]{1,0:T(8,128)(2,1)} %value_ref.1), custom_call_target="tpu_custom_call" | custom-call | tf_op jit(solution)/shard_map/pallas_call | solution.py:194
  55.2 11.5 %slice_bitcast_fusion.1 = (bf16[16,224,1280]{2,1,0:T(8,128)(2,1)S(1)}, bf16[16,224,1280]{2,1,0:T(8,128)(2,1)}) fusion(bf16[2,16,224,1280]{3,2,1,0:T(8,128)(2,1)} %shard_map.68), kind=kLoop, calls=%fused_computation.5 | loop fusion | bytes 36700160 | tf_op jit(solution)/shard_map/squeeze | solution.py:299
  66.7 205.4 %all_to_all.20.far_key_ref.far_value_ref.query_ref.near_key_ref.near_value_ref = bf16[16,224,1280]{2,1,0:T(8,128)(2,1)} all-to-all(bf16[16,224,1280]{2,1,0:T(8,128)(2,1)S(1)} %get-tuple-element.18), channel_id=1, replica_groups=mesh['groups'=2,'seq'=16] {'seq'}, dimensions={0} | all-to-all | bytes 18350080 | tf_op jit(solution)/shard_map/all_to_all | solution.py:300
  272.1 5.9 %all-to-all-start.2 = ((bf16[16,224,1280]{2,1,0:T(8,128)(2,1)}), bf16[16,224,1280]{2,1,0:T(8,128)(2,1)}, u32[]{:S(2)}, u32[]{:S(2)}) async-start(bf16[16,224,1280]{2,1,0:T(8,128)(2,1)} %get-tuple-element.19), calls=%async_computation.2 | async-start | bytes 18350080 | tf_op jit(solution)/shard_map/all_to_all | solution.py:300
  278.2 0.2 reduce_window_sum.30
  278.3 0.1 fusion.6
  278.5 0.2 select_reduce_fusion.8
  278.8 0.1 eq.444
  278.9 0.1 fusion.3
  279.0 0.2 reduce_window_sum.29
  279.4 0.1 select_reduce_fusion.12
  279.5 0.1 copy.27
  279.6 0.1 eq.419
  279.7 0.2 select_reduce_fusion.5
  279.9 0.2 select_reduce_fusion.1
  280.2 0.1 select_reduce_fusion.15
  280.4 0.5 select_reduce_fusion.4
  280.9 0.2 compare_reduce_fusion
  281.1 1.9 gather_fusion.1
  283.0 0.1 compare_reduce_fusion.1
  283.1 1.8 gather_fusion
  284.9 1.2 select_select_fusion.1.near_bias_ref
  286.1 1.6 select_select_fusion.far_bias_ref
  287.7 26.9 %shard_map.69 = (bf16[16,32,1280]{2,1,0:T(8,128)(2,1)}, f32[10,512,1]{2,1,0:T(8,128)}) custom-call(bf16[16,224,1280]{2,1,0:T(8,128)(2,1)} %all_to_all.20.far_key_ref.far_value_ref.query_ref.near_key_ref.near_value_ref, bf16[16,224,1280]{2,1,0:T(8,128)(2,1)} %all_to_all.20.far_key_ref.far_value_ref.query_ref.near_key_ref.near_value_ref, ...), custom_call_target="tpu_custom_call" | custom-call | tf_op jit(solution)/shard_map/pallas_call | solution.py:141
  314.6 162.6 %all-to-all-done.2.far_key_ref.far_value_ref.query_ref.near_key_ref.near_value_ref = bf16[16,224,1280]{2,1,0:T(8,128)(2,1)} async-done(((bf16[16,224,1280]{2,1,0:T(8,128)(2,1)}), bf16[16,224,1280]{2,1,0:T(8,128)(2,1)}, u32[]{:S(2)}, u32[]{:S(2)}) %all-to-all-start.2) | async-done | bytes 9175072 | tf_op jit(solution)/shard_map/all_to_all | solution.py:300
  477.2 4.9 all-to-all-start.1
  482.1 26.9 %shard_map.70 = (bf16[16,32,1280]{2,1,0:T(8,128)(2,1)}, f32[10,512,1]{2,1,0:T(8,128)}) custom-call(bf16[16,224,1280]{2,1,0:T(8,128)(2,1)} %all-to-all-done.2.far_key_ref.far_value_ref.query_ref.near_key_ref.near_value_ref, bf16[16,224,1280]{2,1,0:T(8,128)(2,1)} %all-to-all-done.2.far_key_ref.far_value_ref.query_ref.near_key_ref.near_value_ref, ...), custom_call_target="tpu_custom_call" | custom-call | tf_op jit(solution)/shard_map/pallas_call | solution.py:141
  509.0 3.7 all-to-all-done.1
  512.7 4.9 all-to-all-start.3
  517.6 0.2 select_reduce_fusion.14
  517.9 0.1 add.568
  518.1 0.1 select_reduce_fusion.7
  518.3 2.5 reduce
  520.8 2.5 reduce.1
  523.3 0.1 copy.29
  523.5 1.0 gather_fusion.3
  524.5 0.1 copy.30
  524.7 0.7 reshape.877
  525.4 22.8 %all-to-all-done.3 = bf16[16,32,1280]{2,1,0:T(8,128)(2,1)S(1)} async-done(((bf16[16,32,1280]{2,1,0:T(8,128)(2,1)}), bf16[16,32,1280]{2,1,0:T(8,128)(2,1)S(1)}, u32[]{:S(2)}, u32[]{:S(2)}) %all-to-all-start.3) | async-done | bytes 1310752 | tf_op jit(solution)/shard_map/all_to_all | solution.py:302
  548.1 1.1 copy-done.1
  549.2 1.9 pad_maximum_fusion
  551.1 3.5 gather_fusion.2
  554.6 3.5 broadcast_select_fusion
  (65 shorter events, 1.9 us)
Async XLA Ops:
  272.1 6.8 %copy-start.3 = (s32[128]{0:T(128)S(1)}, s32[128]{0:T(128)}, u32[]{:S(2)}) copy-start(s32[128]{0:T(128)} %param.8) | copy-start | bytes 1540
  272.1 8.3 %copy-start.2 = (s32[128,23]{0,1:T(8,128)S(1)}, s32[128,23]{0,1:T(8,128)}, u32[]{:S(2)}) copy-start(s32[128,23]{0,1:T(8,128)} %param.9) | copy-start | bytes 35332
  272.1 205.1 %all-to-all-start.2 = ((bf16[16,224,1280]{2,1,0:T(8,128)(2,1)}), bf16[16,224,1280]{2,1,0:T(8,128)(2,1)}, u32[]{:S(2)}, u32[]{:S(2)}) async-start(bf16[16,224,1280]{2,1,0:T(8,128)(2,1)} %get-tuple-element.19), calls=%async_computation.2 | async-start | bytes 18350080 | tf_op jit(solution)/shard_map/all_to_all | solution.py:300
  477.2 35.5 %all-to-all-start.1 = ((bf16[16,32,1280]{2,1,0:T(8,128)(2,1)}), bf16[16,32,1280]{2,1,0:T(8,128)(2,1)S(1)}, u32[]{:S(2)}, u32[]{:S(2)}) async-start(bf16[16,32,1280]{2,1,0:T(8,128)(2,1)} %get-tuple-element.6), calls=%async_computation.1 | async-start | bytes 2621440 | tf_op jit(solution)/shard_map/all_to_all | solution.py:302
  512.7 8.1 %copy-start = (bf16[16,32,1280]{2,1,0:T(8,128)(2,1)}, bf16[16,32,1280]{2,1,0:T(8,128)(2,1)S(1)}, u32[]{:S(2)}) copy-start(bf16[16,32,1280]{2,1,0:T(8,128)(2,1)S(1)} %all-to-all-done.1) | copy-start | bytes 3932164
  512.7 35.4 %all-to-all-start.3 = ((bf16[16,32,1280]{2,1,0:T(8,128)(2,1)}), bf16[16,32,1280]{2,1,0:T(8,128)(2,1)S(1)}, u32[]{:S(2)}, u32[]{:S(2)}) async-start(bf16[16,32,1280]{2,1,0:T(8,128)(2,1)} %get-tuple-element.7), calls=%async_computation.3 | async-start | bytes 2621440 | tf_op jit(solution)/shard_map/all_to_all | solution.py:302
  548.1 1.1 copy-start.1

commit v11 on v10

--- a/solution.py
+++ b/solution.py
@@ -162,23 +162,32 @@
     )(got, got, got, got, got, near_bias, far_bias)
 
 
-def pack_kernel(far_hot_ref, own_hot_ref, query_ref, key_ref, value_ref, out_ref):
+PACK_DESTS = 4
+
+
+def pack_kernel(far_hot_ref, own_hot_ref, query_ref, key_ref, value_ref, *out_refs):
     far_hot = far_hot_ref[...]
     own_hot = own_hot_ref[...]
-    far_rows = far_hot.shape[0]
-    own_rows = own_hot.shape[0]
-
-    def select(hot, source_ref):
-        return jnp.dot(hot, source_ref[...], preferred_element_type=jnp.float32).astype(
-            out_ref.dtype
+    dests, far_rows, local_rows = far_hot.shape
+    own_rows = own_hot.shape[1]
+    far_hot = far_hot.reshape(dests * far_rows, local_rows)
+    own_hot = own_hot.reshape(dests * own_rows, local_rows)
+    base = 2 * far_rows
+    for index, out_ref in enumerate(out_refs):
+        width = out_ref.shape[2]
+        columns = slice(index * width, (index + 1) * width)
+
+        def select(hot, source_ref, rows):
+            picked = jnp.dot(hot, source_ref[:, columns], preferred_element_type=jnp.float32)
+            return picked.astype(out_ref.dtype).reshape(dests, rows, width)
+
+        out_ref[:, 0:far_rows, :] = select(far_hot, key_ref, far_rows)
+        out_ref[:, far_rows:base, :] = select(far_hot, value_ref, far_rows)
+        out_ref[:, base : base + own_rows, :] = select(own_hot, query_ref, own_rows)
+        out_ref[:, base + own_rows : base + 2 * own_rows, :] = select(own_hot, key_ref, own_rows)
+        out_ref[:, base + 2 * own_rows : base + 3 * own_rows, :] = select(
+            own_hot, value_ref, own_rows
         )
-
-    out_ref[0:far_rows, :] = select(far_hot, key_ref)
-    out_ref[far_rows : 2 * far_rows, :] = select(far_hot, value_ref)
-    base = 2 * far_rows
-    out_ref[base : base + own_rows, :] = select(own_hot, query_ref)
-    out_ref[base + own_rows : base + 2 * own_rows, :] = select(own_hot, key_ref)
-    out_ref[base + 2 * own_rows : base + 3 * own_rows, :] = select(own_hot, value_ref)
 
 
 def pack(far_rows, own_rows, query_feats, key_feats, value_feats, chunks):
@@ -186,23 +195,25 @@
     own_count = own_rows.shape[1]
     local_rows, channels = query_feats.shape
     width = channels // chunks
+    dests = PACK_DESTS if group_size % PACK_DESTS == 0 else 1
     row_iota = jnp.arange(local_rows, dtype=jnp.int32)
     far_hot = (far_rows[:, :, None] == row_iota).astype(jnp.bfloat16)
     own_hot = (own_rows[:, :, None] == row_iota).astype(jnp.bfloat16)
     total = 2 * far_count + 3 * own_count
-    source_spec = pl.BlockSpec((local_rows, width), lambda c, j: (0, c))
+    source_spec = pl.BlockSpec((local_rows, channels), lambda j: (0, 0))
+    out_spec = pl.BlockSpec((dests, total, width), lambda j: (j, 0, 0))
     return pl.pallas_call(
         pack_kernel,
-        grid=(chunks, group_size),
+        grid=(group_size // dests,),
         in_specs=[
-            pl.BlockSpec((None, far_count, local_rows), lambda c, j: (j, 0, 0)),
-            pl.BlockSpec((None, own_count, local_rows), lambda c, j: (j, 0, 0)),
+            pl.BlockSpec((dests, far_count, local_rows), lambda j: (j, 0, 0)),
+            pl.BlockSpec((dests, own_count, local_rows), lambda j: (j, 0, 0)),
             source_spec,
             source_spec,
             source_spec,
         ],
-        out_specs=pl.BlockSpec((None, None, total, width), lambda c, j: (c, j, 0, 0)),
-        out_shape=jax.ShapeDtypeStruct((chunks, group_size, total, width), query_feats.dtype),
+        out_specs=[out_spec] * chunks,
+        out_shape=[jax.ShapeDtypeStruct((group_size, total, width), query_feats.dtype)] * chunks,
         interpret=INTERPRET,
     )(far_hot, own_hot, query_feats, key_feats, value_feats)
 

time: 559 us -> 519 us (0.928)
  Pallas kernels: 98.1 us -> 69 us
  local copies, waits for them, and re-layouts: 25.4 us -> 13.9 us
    pallas_call x1, Pallas kernels: 44.4 us -> 15.3 us  [pack(): pl.pallas_call(pack_kernel, grid=(group_size // dests,), in_specs=[pl.Blo...]
    squeeze x1 -> x0, local copies, waits for them, and re-layouts: 11.5 us -> none  [shards(): sent = packed[chunk]]
where the time goes in v11:
time: 519 us; the launch traced here: 518 us
  blocking collectives  206 us (40%)
  waiting for transfers between devices  189 us (36%)
  Pallas kernels  69 us (13%)
  other arithmetic  23.5 us (5%)
  starting transfers between devices  15.7 us (3%)
  local copies, waits for them, and re-layouts  13.9 us (3%)
    all_to_all x1, blocking collectives, shards(): got = lax.all_to_all(sent, 'seq', split_axis=0, concat_axis=0, tiled=True)  206 us
    all_to_all x1, waiting for transfers between devices, shards(): got = lax.all_to_all(sent, 'seq', split_axis=0, concat_axis=0, tiled=True)  163 us
    pallas_call x2, Pallas kernels, attend(): pl.pallas_call(attention_kernel, grid=(heads,), in_specs=[pl.BlockSpec(fa...  53.8 us
    all_to_all x2, waiting for transfers between devices, shards(): lax.all_to_all(mixed, 'seq', split_axis=0, concat_axis=0, tiled=True)  26.4 us
    pallas_call x1, Pallas kernels, pack(): pl.pallas_call(pack_kernel, grid=(group_size // dests,), in_specs=[pl.Blo...  15.3 us
  transfers between devices with their start and end apart: 3, of which 3 were waited for; matrix products, arithmetic and copies ran while one was open for 3% of the time, Pallas kernels for 10%

profile of v11, /device:TPU:13, one launch (start us, length us, event | category | flops | bytes accessed | tf_op | source)
XLA Modules:
  0.0 517.8 jit_solution(15754508481513913651)
XLA Ops:
  0.7 0.7 iota_compare_fusion.12
  1.3 0.7 eq.381
  2.1 1.8 select_reduce_fusion
  3.8 0.7 broadcast_compare_fusion
  4.5 0.8 select_reduce_fusion.2
  5.3 0.3 select_reduce_fusion.3
  5.7 0.2 reduce_window_sum.28
  5.8 0.1 select_reduce_fusion.11
  6.2 0.1 add.516
  6.4 0.1 add.523
  6.5 0.1 add.518
  6.6 0.1 add.527
  6.7 1.2 fusion.far_hot_ref
  7.9 0.2 convert_reduce_fusion
  8.1 0.1 reshape.874
  8.2 0.7 dynamic_slice.10
  9.1 0.1 select_reduce_fusion.13
  9.2 0.1 copy.25
  9.4 0.1 add.531
  9.6 0.1 add.538
  9.7 0.1 add.533
  9.9 1.0 fusion.1.own_hot_ref
  10.9 15.3 %shard_map.68 = (bf16[16,224,1280]{2,1,0:T(8,128)(2,1)}, bf16[16,224,1280]{2,1,0:T(8,128)(2,1)}) custom-call(bf16[16,64,512]{2,1,0:T(8,128)(2,1)} %fusion.far_hot_ref, bf16[16,32,512]{2,1,0:T(8,128)(2,1)} %fusion.1.own_hot_ref, bf16[512,2560]{1,0:T(8,128)(2,1)} %query_ref.1, bf16[512,2560]{1,0:T(8,128)(2,1)} %key_ref.1, bf16[512,2560]{1,0:T(8,128)(2,1)} %value_ref.1), custom_call_target="tpu_custom_call" | custom-call | tf_op jit(solution)/shard_map/pallas_call | solution.py:205
  26.1 205.6 %all_to_all.20.far_key_ref.far_value_ref.query_ref.near_key_ref.near_value_ref = bf16[16,224,1280]{2,1,0:T(8,128)(2,1)} all-to-all(bf16[16,224,1280]{2,1,0:T(8,128)(2,1)} %get-tuple-element.8), channel_id=1, replica_groups=mesh['groups'=2,'seq'=16] {'seq'}, dimensions={0} | all-to-all | bytes 18350080 | tf_op jit(solution)/shard_map/all_to_all | solution.py:311
  231.8 5.9 %all-to-all-start.2 = ((bf16[16,224,1280]{2,1,0:T(8,128)(2,1)}), bf16[16,224,1280]{2,1,0:T(8,128)(2,1)}, u32[]{:S(2)}, u32[]{:S(2)}) async-start(bf16[16,224,1280]{2,1,0:T(8,128)(2,1)} %get-tuple-element.10), calls=%async_computation.2 | async-start | bytes 18350080 | tf_op jit(solution)/shard_map/all_to_all | solution.py:311
  237.8 0.2 reduce_window_sum.30
  238.0 0.1 fusion.6
  238.1 0.2 select_reduce_fusion.8
  238.5 0.1 eq.444
  238.6 0.1 fusion.3
  238.6 0.2 reduce_window_sum.29
  239.0 0.1 select_reduce_fusion.12
  239.1 0.1 copy.27
  239.3 0.1 eq.419
  239.4 0.2 select_reduce_fusion.5
  239.6 0.2 select_reduce_fusion.1
  239.9 0.1 select_reduce_fusion.15
  240.1 0.5 select_reduce_fusion.4
  240.5 0.2 compare_reduce_fusion
  240.7 1.9 gather_fusion.1
  242.6 0.1 compare_reduce_fusion.1
  242.8 1.8 gather_fusion
  244.5 1.2 select_select_fusion.1.near_bias_ref
  245.7 1.6 select_select_fusion.far_bias_ref
  247.4 26.9 %shard_map.69 = (bf16[16,32,1280]{2,1,0:T(8,128)(2,1)}, f32[10,512,1]{2,1,0:T(8,128)}) custom-call(bf16[16,224,1280]{2,1,0:T(8,128)(2,1)} %all_to_all.20.far_key_ref.far_value_ref.query_ref.near_key_ref.near_value_ref, bf16[16,224,1280]{2,1,0:T(8,128)(2,1)} %all_to_all.20.far_key_ref.far_value_ref.query_ref.near_key_ref.near_value_ref, ...), custom_call_target="tpu_custom_call" | custom-call | tf_op jit(solution)/shard_map/pallas_call | solution.py:141
  274.3 162.6 %all-to-all-done.2.far_key_ref.far_value_ref.query_ref.near_key_ref.near_value_ref = bf16[16,224,1280]{2,1,0:T(8,128)(2,1)} async-done(((bf16[16,224,1280]{2,1,0:T(8,128)(2,1)}), bf16[16,224,1280]{2,1,0:T(8,128)(2,1)}, u32[]{:S(2)}, u32[]{:S(2)}) %all-to-all-start.2) | async-done | bytes 9175072 | tf_op jit(solution)/shard_map/all_to_all | solution.py:311
  436.9 4.9 all-to-all-start.1
  441.8 26.9 %shard_map.70 = (bf16[16,32,1280]{2,1,0:T(8,128)(2,1)}, f32[10,512,1]{2,1,0:T(8,128)}) custom-call(bf16[16,224,1280]{2,1,0:T(8,128)(2,1)} %all-to-all-done.2.far_key_ref.far_value_ref.query_ref.near_key_ref.near_value_ref, bf16[16,224,1280]{2,1,0:T(8,128)(2,1)} %all-to-all-done.2.far_key_ref.far_value_ref.query_ref.near_key_ref.near_value_ref, ...), custom_call_target="tpu_custom_call" | custom-call | tf_op jit(solution)/shard_map/pallas_call | solution.py:141
  468.7 3.6 all-to-all-done.1
  472.4 4.9 all-to-all-start.3
  477.2 0.2 select_reduce_fusion.14
  477.6 0.1 add.568
  477.8 0.1 select_reduce_fusion.7
  477.9 2.5 reduce
  480.4 2.5 reduce.1
  482.9 0.1 copy.29
  483.1 1.0 gather_fusion.3
  484.1 0.1 copy.30
  484.3 0.7 reshape.877
  485.0 22.8 %all-to-all-done.3 = bf16[16,32,1280]{2,1,0:T(8,128)(2,1)S(1)} async-done(((bf16[16,32,1280]{2,1,0:T(8,128)(2,1)}), bf16[16,32,1280]{2,1,0:T(8,128)(2,1)S(1)}, u32[]{:S(2)}, u32[]{:S(2)}) %all-to-all-start.3) | async-done | bytes 1310752 | tf_op jit(solution)/shard_map/all_to_all | solution.py:313
  507.8 1.1 copy-done.1
  508.8 1.9 pad_maximum_fusion
  510.7 3.5 gather_fusion.2
  514.2 3.5 broadcast_select_fusion
  (64 shorter events, 1.8 us)
Async XLA Ops:
  231.8 6.8 %copy-start.3 = (s32[128]{0:T(128)S(1)}, s32[128]{0:T(128)}, u32[]{:S(2)}) copy-start(s32[128]{0:T(128)} %param.8) | copy-start | bytes 1540
  231.8 8.3 %copy-start.2 = (s32[128,23]{0,1:T(8,128)S(1)}, s32[128,23]{0,1:T(8,128)}, u32[]{:S(2)}) copy-start(s32[128,23]{0,1:T(8,128)} %param.9) | copy-start | bytes 35332
  231.8 205.1 %all-to-all-start.2 = ((bf16[16,224,1280]{2,1,0:T(8,128)(2,1)}), bf16[16,224,1280]{2,1,0:T(8,128)(2,1)}, u32[]{:S(2)}, u32[]{:S(2)}) async-start(bf16[16,224,1280]{2,1,0:T(8,128)(2,1)} %get-tuple-element.10), calls=%async_computation.2 | async-start | bytes 18350080 | tf_op jit(solution)/shard_map/all_to_all | solution.py:311
  436.9 35.5 %all-to-all-start.1 = ((bf16[16,32,1280]{2,1,0:T(8,128)(2,1)}), bf16[16,32,1280]{2,1,0:T(8,128)(2,1)S(1)}, u32[]{:S(2)}, u32[]{:S(2)}) async-start(bf16[16,32,1280]{2,1,0:T(8,128)(2,1)} %get-tuple-element.9), calls=%async_computation.1 | async-start | bytes 2621440 | tf_op jit(solution)/shard_map/all_to_all | solution.py:313
  472.3 8.1 %copy-start = (bf16[16,32,1280]{2,1,0:T(8,128)(2,1)}, bf16[16,32,1280]{2,1,0:T(8,128)(2,1)S(1)}, u32[]{:S(2)}) copy-start(bf16[16,32,1280]{2,1,0:T(8,128)(2,1)S(1)} %all-to-all-done.1) | copy-start | bytes 3932164
  472.4 35.4 %all-to-all-start.3 = ((bf16[16,32,1280]{2,1,0:T(8,128)(2,1)}), bf16[16,32,1280]{2,1,0:T(8,128)(2,1)S(1)}, u32[]{:S(2)}, u32[]{:S(2)}) async-start(bf16[16,32,1280]{2,1,0:T(8,128)(2,1)} %get-tuple-element.11), calls=%async_computation.3 | async-start | bytes 2621440 | tf_op jit(solution)/shard_map/all_to_all | solution.py:313
  507.8 1.1 copy-start.1

commit v12 on v11

--- a/solution.py
+++ b/solution.py
@@ -95,6 +95,7 @@
 FAR_SLOTS = 4
 INTERPRET = False
 HEAD_CHUNKS = 2
+LAST_SPLITS = 2
 
 
 def attention_kernel(
@@ -130,11 +131,10 @@
     log_ref[...] = log_total
 
 
-def attend(got, unit, near_bias, far_bias):
+def attend(got, unit, near_bias, far_bias, first_head, heads):
     group_size, _, channels = got.shape
     far_rows = FAR_SLOTS * 16
     rows = group_size * unit
-    heads = channels // HEAD_DIM
     base = 2 * far_rows // unit
     far_spec = (group_size, far_rows, HEAD_DIM)
     own_spec = (group_size, unit, HEAD_DIM)
@@ -142,11 +142,11 @@
         attention_kernel,
         grid=(heads,),
         in_specs=[
-            pl.BlockSpec(far_spec, lambda h: (0, 0, h)),
-            pl.BlockSpec(far_spec, lambda h: (0, 1, h)),
-            pl.BlockSpec(own_spec, lambda h: (0, base, h)),
-            pl.BlockSpec(own_spec, lambda h: (0, base + 1, h)),
-            pl.BlockSpec(own_spec, lambda h: (0, base + 2, h)),
+            pl.BlockSpec(far_spec, lambda h: (0, 0, first_head + h)),
+            pl.BlockSpec(far_spec, lambda h: (0, 1, first_head + h)),
+            pl.BlockSpec(own_spec, lambda h: (0, base, first_head + h)),
+            pl.BlockSpec(own_spec, lambda h: (0, base + 1, first_head + h)),
+            pl.BlockSpec(own_spec, lambda h: (0, base + 2, first_head + h)),
             pl.BlockSpec((rows, rows), lambda h: (0, 0)),
             pl.BlockSpec((rows, group_size * far_rows), lambda h: (0, 0)),
         ],
@@ -155,7 +155,7 @@
             pl.BlockSpec((None, rows, 1), lambda h: (h, 0, 0)),
         ],
         out_shape=[
-            jax.ShapeDtypeStruct((group_size, unit, channels), jnp.bfloat16),
+            jax.ShapeDtypeStruct((group_size, unit, heads * HEAD_DIM), jnp.bfloat16),
             jax.ShapeDtypeStruct((heads, rows, 1), jnp.float32),
         ],
         interpret=INTERPRET,
@@ -309,10 +309,16 @@
     for chunk in range(HEAD_CHUNKS):
         sent = packed[chunk]
         got = lax.all_to_all(sent, "seq", split_axis=0, concat_axis=0, tiled=True)
-        mixed, head_logs = attend(got, unit, near_bias, far_bias)
-        returned = lax.all_to_all(mixed, "seq", split_axis=0, concat_axis=0, tiled=True)
-        outputs.append(returned.reshape(-1, chunk_width))
-        logs.append(head_logs[:, :, 0])
+        chunk_heads = chunk_width // HEAD_DIM
+        parts = LAST_SPLITS if chunk == HEAD_CHUNKS - 1 else 1
+        for part in range(parts):
+            part_heads = chunk_heads // parts
+            mixed, head_logs = attend(
+                got, unit, near_bias, far_bias, part * part_heads, part_heads
+            )
+            returned = lax.all_to_all(mixed, "seq", split_axis=0, concat_axis=0, tiled=True)
+            outputs.append(returned.reshape(-1, part_heads * HEAD_DIM))
+            logs.append(head_logs[:, :, 0])
     head_logs = jnp.concatenate(logs, axis=0)
     own_class = own_ids // piece_count
     own_slot = pick(class_rank, own_ids)

time: 519 us -> 537 us (1.035)
  waiting for transfers between devices: 189 us -> 198 us
  starting transfers between devices: 15.7 us -> 21.8 us
    all_to_all x1, waiting for transfers between devices: 163 us -> 175 us  [shards(): got = lax.all_to_all(sent, 'seq', split_axis=0, concat_axis=0, tiled=True)]
    all_to_all x2 -> x3, starting transfers between devices: 9.78 us -> 15.9 us  [shards(): lax.all_to_all(mixed, 'seq', split_axis=0, concat_axis=0, tiled=True)]
    all_to_all x2 -> x3, waiting for transfers between devices: 26.4 us -> 23.4 us  [shards(): lax.all_to_all(mixed, 'seq', split_axis=0, concat_axis=0, tiled=True)]
    pallas_call x2 -> x3, Pallas kernels: 53.8 us -> 56.6 us  [attend(): pl.pallas_call(attention_kernel, grid=(heads,), in_specs=[pl.BlockSpec(fa...]
  transfers between devices with their start and end apart: 3 -> 4, of which waited for: 3 -> 3; matrix products, arithmetic and copies ran while one was open for 3% -> 3% of each run, Pallas kernels for 10% -> 11%
where the time goes in v12:
time: 537 us; the launch traced here: 536 us
  blocking collectives  206 us (38%)
  waiting for transfers between devices  198 us (37%)
  Pallas kernels  71.8 us (13%)
  other arithmetic  24.3 us (5%)
  starting transfers between devices  21.8 us (4%)
  local copies, waits for them, and re-layouts  13.9 us (3%)
    all_to_all x1, blocking collectives, shards(): got = lax.all_to_all(sent, 'seq', split_axis=0, concat_axis=0, tiled=True)  206 us
    all_to_all x1, waiting for transfers between devices, shards(): got = lax.all_to_all(sent, 'seq', split_axis=0, concat_axis=0, tiled=True)  175 us
    pallas_call x3, Pallas kernels, attend(): pl.pallas_call(attention_kernel, grid=(heads,), in_specs=[pl.BlockSpec(fa...  56.6 us
    all_to_all x3, waiting for transfers between devices, shards(): lax.all_to_all(mixed, 'seq', split_axis=0, concat_axis=0, tiled=True)  23.4 us
    all_to_all x3, starting transfers between devices, shards(): lax.all_to_all(mixed, 'seq', split_axis=0, concat_axis=0, tiled=True)  15.9 us
    pallas_call x1, Pallas kernels, pack(): pl.pallas_call(pack_kernel, grid=(group_size // dests,), in_specs=[pl.Blo...  15.3 us
  transfers between devices with their start and end apart: 4, of which 3 were waited for; matrix products, arithmetic and copies ran while one was open for 3% of the time, Pallas kernels for 11%

profile of v12, /device:TPU:13, one launch (start us, length us, event | category | flops | bytes accessed | tf_op | source)
XLA Modules:
  0.0 536.5 jit_solution(17262061753743243492)
XLA Ops:
  0.7 0.7 iota_compare_fusion.12
  1.3 0.7 eq.381
  2.1 1.8 select_reduce_fusion
  3.8 0.7 broadcast_compare_fusion
  4.5 0.8 select_reduce_fusion.2
  5.3 0.3 select_reduce_fusion.3
  5.7 0.2 reduce_window_sum.28
  5.8 0.1 select_reduce_fusion.11
  6.2 0.1 add.516
  6.4 0.1 add.523
  6.7 1.2 fusion.far_hot_ref
  7.9 0.2 convert_reduce_fusion
  8.1 0.1 reshape.877
  8.2 0.7 dynamic_slice.10
  9.1 0.1 select_reduce_fusion.13
  9.2 0.1 copy.26
  9.4 0.1 add.531
  9.6 0.1 add.538
  9.9 1.0 fusion.1.own_hot_ref
  10.9 15.3 %shard_map.68 = (bf16[16,224,1280]{2,1,0:T(8,128)(2,1)}, bf16[16,224,1280]{2,1,0:T(8,128)(2,1)}) custom-call(bf16[16,64,512]{2,1,0:T(8,128)(2,1)} %fusion.far_hot_ref, bf16[16,32,512]{2,1,0:T(8,128)(2,1)} %fusion.1.own_hot_ref, bf16[512,2560]{1,0:T(8,128)(2,1)} %query_ref.1, bf16[512,2560]{1,0:T(8,128)(2,1)} %key_ref.1, bf16[512,2560]{1,0:T(8,128)(2,1)} %value_ref.1), custom_call_target="tpu_custom_call" | custom-call | tf_op jit(solution)/shard_map/pallas_call | solution.py:205
  26.1 205.6 %all_to_all.25.far_key_ref.far_value_ref.query_ref.near_key_ref.near_value_ref = bf16[16,224,1280]{2,1,0:T(8,128)(2,1)} all-to-all(bf16[16,224,1280]{2,1,0:T(8,128)(2,1)} %get-tuple-element.12), channel_id=1, replica_groups=mesh['groups'=2,'seq'=16] {'seq'}, dimensions={0} | all-to-all | bytes 18350080 | tf_op jit(solution)/shard_map/all_to_all | solution.py:311
  231.8 5.9 %all-to-all-start = ((bf16[16,224,1280]{2,1,0:T(8,128)(2,1)}), bf16[16,224,1280]{2,1,0:T(8,128)(2,1)}, u32[]{:S(2)}, u32[]{:S(2)}) async-start(bf16[16,224,1280]{2,1,0:T(8,128)(2,1)} %get-tuple-element.10), calls=%async_computation | async-start | bytes 18350080 | tf_op jit(solution)/shard_map/all_to_all | solution.py:311
  237.8 0.2 reduce_window_sum.30
  238.0 0.1 fusion.6
  238.1 0.2 select_reduce_fusion.8
  238.4 0.1 eq.444
  238.5 0.1 fusion.3
  238.6 0.2 reduce_window_sum.29
  239.0 0.1 select_reduce_fusion.12
  239.1 0.1 copy.28
  239.3 0.1 eq.419
  239.4 0.2 select_reduce_fusion.5
  239.6 0.2 select_reduce_fusion.1
  239.8 0.1 select_reduce_fusion.15
  240.0 0.5 select_reduce_fusion.4
  240.5 0.2 compare_reduce_fusion
  240.7 1.9 gather_fusion.1
  242.6 0.1 compare_reduce_fusion.1
  242.7 1.8 gather_fusion
  244.5 1.2 select_select_fusion.1.near_bias_ref
  245.7 1.7 select_select_fusion.far_bias_ref
  247.4 14.8 %shard_map.70 = (bf16[16,32,640]{2,1,0:T(8,128)(2,1)}, f32[5,512,1]{2,1,0:T(8,128)}) custom-call(bf16[16,224,1280]{2,1,0:T(8,128)(2,1)} %all_to_all.25.far_key_ref.far_value_ref.query_ref.near_key_ref.near_value_ref, bf16[16,224,1280]{2,1,0:T(8,128)(2,1)} %all_to_all.25.far_key_ref.far_value_ref.query_ref.near_key_ref.near_value_ref, ...), custom_call_target="tpu_custom_call" | custom-call | tf_op jit(solution)/shard_map/pallas_call | solution.py:141
  262.2 174.6 %all-to-all-done.far_key_ref.far_value_ref.query_ref.near_key_ref.near_value_ref = bf16[16,224,1280]{2,1,0:T(8,128)(2,1)} async-done(((bf16[16,224,1280]{2,1,0:T(8,128)(2,1)}), bf16[16,224,1280]{2,1,0:T(8,128)(2,1)}, u32[]{:S(2)}, u32[]{:S(2)}) %all-to-all-start) | async-done | bytes 9175072 | tf_op jit(solution)/shard_map/all_to_all | solution.py:311
  436.9 4.9 all-to-all-start.3
  441.8 14.9 %shard_map.71 = (bf16[16,32,640]{2,1,0:T(8,128)(2,1)}, f32[5,512,1]{2,1,0:T(8,128)}) custom-call(bf16[16,224,1280]{2,1,0:T(8,128)(2,1)} %all_to_all.25.far_key_ref.far_value_ref.query_ref.near_key_ref.near_value_ref, bf16[16,224,1280]{2,1,0:T(8,128)(2,1)} %all_to_all.25.far_key_ref.far_value_ref.query_ref.near_key_ref.near_value_ref, ...), custom_call_target="tpu_custom_call" | custom-call | tf_op jit(solution)/shard_map/pallas_call | solution.py:141
  456.6 1.6 all-to-all-done.3
  458.2 5.0 all-to-all-start.4
  463.2 26.9 %shard_map.69 = (bf16[16,32,1280]{2,1,0:T(8,128)(2,1)}, f32[10,512,1]{2,1,0:T(8,128)}) custom-call(bf16[16,224,1280]{2,1,0:T(8,128)(2,1)} %all-to-all-done.far_key_ref.far_value_ref.query_ref.near_key_ref.near_value_ref, bf16[16,224,1280]{2,1,0:T(8,128)(2,1)} %all-to-all-done.far_key_ref.far_value_ref.query_ref.near_key_ref.near_value_ref, ...), custom_call_target="tpu_custom_call" | custom-call | tf_op jit(solution)/shard_map/pallas_call | solution.py:141
  490.1 6.0 %all-to-all-start.1 = ((bf16[16,32,1280]{2,1,0:T(8,128)(2,1)}), bf16[16,32,1280]{2,1,0:T(8,128)(2,1)S(1)}, u32[]{:S(2)}, u32[]{:S(2)}) async-start(bf16[16,32,1280]{2,1,0:T(8,128)(2,1)} %get-tuple-element.11), calls=%async_computation.1 | async-start | bytes 2621440 | tf_op jit(solution)/shard_map/all_to_all | solution.py:319
  496.1 0.2 select_reduce_fusion.14
  496.4 0.1 add.568
  496.6 0.1 select_reduce_fusion.7
  496.8 2.5 reduce
  499.3 1.7 reduce.1
  501.0 1.7 reduce.2
  502.8 0.1 copy.30
  502.9 1.0 gather_fusion.3
  504.0 0.1 copy.31
  504.2 0.7 reshape.881
  504.9 21.8 %all-to-all-done.1 = bf16[16,32,1280]{2,1,0:T(8,128)(2,1)S(1)} async-done(((bf16[16,32,1280]{2,1,0:T(8,128)(2,1)}), bf16[16,32,1280]{2,1,0:T(8,128)(2,1)S(1)}, u32[]{:S(2)}, u32[]{:S(2)}) %all-to-all-start.1) | async-done | bytes 1310752 | tf_op jit(solution)/shard_map/all_to_all | solution.py:319
  526.7 1.1 copy-done
  527.7 1.7 pad_maximum_fusion
  529.4 3.5 gather_fusion.2
  532.9 3.5 broadcast_select_fusion
  (68 shorter events, 2.1 us)
Async XLA Ops:
  231.8 6.8 %copy-start.3 = (s32[128]{0:T(128)S(1)}, s32[128]{0:T(128)}, u32[]{:S(2)}) copy-start(s32[128]{0:T(128)} %param.8) | copy-start | bytes 1540
  231.8 8.3 %copy-start.2 = (s32[128,23]{0,1:T(8,128)S(1)}, s32[128,23]{0,1:T(8,128)}, u32[]{:S(2)}) copy-start(s32[128,23]{0,1:T(8,128)} %param.9) | copy-start | bytes 35332
  231.8 205.1 %all-to-all-start = ((bf16[16,224,1280]{2,1,0:T(8,128)(2,1)}), bf16[16,224,1280]{2,1,0:T(8,128)(2,1)}, u32[]{:S(2)}, u32[]{:S(2)}) async-start(bf16[16,224,1280]{2,1,0:T(8,128)(2,1)} %get-tuple-element.10), calls=%async_computation | async-start | bytes 18350080 | tf_op jit(solution)/shard_map/all_to_all | solution.py:311
  436.9 21.3 %all-to-all-start.3 = ((bf16[16,32,640]{2,1,0:T(8,128)(2,1)}), bf16[16,32,640]{2,1,0:T(8,128)(2,1)S(1)}, u32[]{:S(2)}, u32[]{:S(2)}) async-start(bf16[16,32,640]{2,1,0:T(8,128)(2,1)} %get-tuple-element.13), calls=%async_computation.3 | async-start | bytes 1310720 | tf_op jit(solution)/shard_map/all_to_all | solution.py:319
  458.2 31.8 %all-to-all-start.4 = ((bf16[16,32,640]{2,1,0:T(8,128)(2,1)}), bf16[16,32,640]{2,1,0:T(8,128)(2,1)S(1)}, u32[]{:S(2)}, u32[]{:S(2)}) async-start(bf16[16,32,640]{2,1,0:T(8,128)(2,1)} %get-tuple-element.14), calls=%async_computation.4 | async-start | bytes 1310720 | tf_op jit(solution)/shard_map/all_to_all | solution.py:319
  490.1 9.3 %copy-start.1 = (bf16[16,32,640]{2,1,0:T(8,128)(2,1)}, bf16[16,32,640]{2,1,0:T(8,128)(2,1)S(1)}, u32[]{:S(2)}) copy-start(bf16[16,32,640]{2,1,0:T(8,128)(2,1)S(1)} %all-to-all-done.4) | copy-start | bytes 1966084
  490.1 36.6 %all-to-all-start.1 = ((bf16[16,32,1280]{2,1,0:T(8,128)(2,1)}), bf16[16,32,1280]{2,1,0:T(8,128)(2,1)S(1)}, u32[]{:S(2)}, u32[]{:S(2)}) async-start(bf16[16,32,1280]{2,1,0:T(8,128)(2,1)} %get-tuple-element.11), calls=%async_computation.1 | async-start | bytes 2621440 | tf_op jit(solution)/shard_map/all_to_all | solution.py:319
  526.7 1.1 copy-start

commit v13 on v12

--- a/solution.py
+++ b/solution.py
@@ -310,7 +310,7 @@
         sent = packed[chunk]
         got = lax.all_to_all(sent, "seq", split_axis=0, concat_axis=0, tiled=True)
         chunk_heads = chunk_width // HEAD_DIM
-        parts = LAST_SPLITS if chunk == HEAD_CHUNKS - 1 else 1
+        parts = LAST_SPLITS
         for part in range(parts):
             part_heads = chunk_heads // parts
             mixed, head_logs = attend(

time: 537 us -> 534 us (level)
  waiting for transfers between devices: 198 us -> 188 us
    all_to_all x3 -> x4, waiting for transfers between devices: 23.4 us -> 13.7 us  [shards(): lax.all_to_all(mixed, 'seq', split_axis=0, concat_axis=0, tiled=True)]
    all_to_all x3 -> x4, starting transfers between devices: 15.9 us -> 20.1 us  [shards(): lax.all_to_all(mixed, 'seq', split_axis=0, concat_axis=0, tiled=True)]
    pallas_call x3 -> x4, Pallas kernels: 56.6 us -> 59.6 us  [attend(): pl.pallas_call(attention_kernel, grid=(heads,), in_specs=[pl.BlockSpec(fa...]
  transfers between devices with their start and end apart: 4 -> 5, of which waited for: 3 -> 5; matrix products, arithmetic and copies ran while one was open for 3% -> 3% of each run, Pallas kernels for 11% -> 11%
where the time goes in v13:
time: 534 us; the launch traced here: 532 us
  blocking collectives  206 us (39%)
  waiting for transfers between devices  188 us (35%)
  Pallas kernels  74.8 us (14%)
  starting transfers between devices  26 us (5%)
  other arithmetic  22.6 us (4%)
  local copies, waits for them, and re-layouts  13.7 us (3%)
    all_to_all x1, blocking collectives, shards(): got = lax.all_to_all(sent, 'seq', split_axis=0, concat_axis=0, tiled=True)  206 us
    all_to_all x1, waiting for transfers between devices, shards(): got = lax.all_to_all(sent, 'seq', split_axis=0, concat_axis=0, tiled=True)  175 us
    pallas_call x4, Pallas kernels, attend(): pl.pallas_call(attention_kernel, grid=(heads,), in_specs=[pl.BlockSpec(fa...  59.6 us
    all_to_all x4, starting transfers between devices, shards(): lax.all_to_all(mixed, 'seq', split_axis=0, concat_axis=0, tiled=True)  20.1 us
    pallas_call x1, Pallas kernels, pack(): pl.pallas_call(pack_kernel, grid=(group_size // dests,), in_specs=[pl.Blo...  15.2 us
    all_to_all x4, waiting for transfers between devices, shards(): lax.all_to_all(mixed, 'seq', split_axis=0, concat_axis=0, tiled=True)  13.7 us
  transfers between devices with their start and end apart: 5, of which 5 were waited for; matrix products, arithmetic and copies ran while one was open for 3% of the time, Pallas kernels for 11%

profile of v13, /device:TPU:13, one launch (start us, length us, event | category | flops | bytes accessed | tf_op | source)
XLA Modules:
  0.0 532.1 jit_solution(9694572524852603872)
XLA Ops:
  0.7 0.7 iota_compare_fusion.12
  1.3 0.7 eq.381
  2.1 1.8 select_reduce_fusion
  3.8 0.7 broadcast_compare_fusion
  4.5 0.8 select_reduce_fusion.2
  5.3 0.3 select_reduce_fusion.3
  5.7 0.2 reduce_window_sum.28
  5.8 0.1 select_reduce_fusion.11
  6.2 0.1 add.516
  6.4 0.1 add.523
  6.7 1.2 fusion.far_hot_ref
  7.9 0.2 convert_reduce_fusion
  8.2 0.7 dynamic_slice.10
  9.1 0.1 select_reduce_fusion.13
  9.6 0.1 add.538
  9.9 1.0 fusion.1.own_hot_ref
  10.9 15.2 %shard_map.68 = (bf16[16,224,1280]{2,1,0:T(8,128)(2,1)}, bf16[16,224,1280]{2,1,0:T(8,128)(2,1)}) custom-call(bf16[16,64,512]{2,1,0:T(8,128)(2,1)} %fusion.far_hot_ref, bf16[16,32,512]{2,1,0:T(8,128)(2,1)} %fusion.1.own_hot_ref, bf16[512,2560]{1,0:T(8,128)(2,1)} %query_ref.1, bf16[512,2560]{1,0:T(8,128)(2,1)} %key_ref.1, bf16[512,2560]{1,0:T(8,128)(2,1)} %value_ref.1), custom_call_target="tpu_custom_call" | custom-call | tf_op jit(solution)/shard_map/pallas_call | solution.py:205
  26.1 205.6 %all_to_all.30.far_key_ref.far_value_ref.query_ref.near_key_ref.near_value_ref = bf16[16,224,1280]{2,1,0:T(8,128)(2,1)} all-to-all(bf16[16,224,1280]{2,1,0:T(8,128)(2,1)} %get-tuple-element.12), channel_id=1, replica_groups=mesh['groups'=2,'seq'=16] {'seq'}, dimensions={0} | all-to-all | bytes 18350080 | tf_op jit(solution)/shard_map/all_to_all | solution.py:311
  231.7 5.9 %all-to-all-start.3 = ((bf16[16,224,1280]{2,1,0:T(8,128)(2,1)}), bf16[16,224,1280]{2,1,0:T(8,128)(2,1)}, u32[]{:S(2)}, u32[]{:S(2)}) async-start(bf16[16,224,1280]{2,1,0:T(8,128)(2,1)} %get-tuple-element.15), calls=%async_computation.3 | async-start | bytes 18350080 | tf_op jit(solution)/shard_map/all_to_all | solution.py:311
  237.8 0.2 reduce_window_sum.30
  237.9 0.1 fusion.6
  238.1 0.2 select_reduce_fusion.8
  238.4 0.1 eq.444
  238.6 0.2 reduce_window_sum.29
  239.0 0.1 select_reduce_fusion.12
  239.2 0.1 eq.419
  239.3 0.2 select_reduce_fusion.5
  239.5 0.2 select_reduce_fusion.1
  239.8 0.1 select_reduce_fusion.15
  240.0 0.5 select_reduce_fusion.4
  240.5 0.2 compare_reduce_fusion
  240.7 1.9 gather_fusion.1
  242.6 0.1 compare_reduce_fusion.1
  242.7 1.8 gather_fusion
  244.5 1.2 select_select_fusion.1.near_bias_ref
  245.7 1.7 select_select_fusion.far_bias_ref
  247.4 14.8 %shard_map.69 = (bf16[16,32,640]{2,1,0:T(8,128)(2,1)}, f32[5,512,1]{2,1,0:T(8,128)}) custom-call(bf16[16,224,1280]{2,1,0:T(8,128)(2,1)} %all_to_all.30.far_key_ref.far_value_ref.query_ref.near_key_ref.near_value_ref, bf16[16,224,1280]{2,1,0:T(8,128)(2,1)} %all_to_all.30.far_key_ref.far_value_ref.query_ref.near_key_ref.near_value_ref, ...), custom_call_target="tpu_custom_call" | custom-call | tf_op jit(solution)/shard_map/pallas_call | solution.py:141
  262.2 174.6 %all-to-all-done.3.far_key_ref.far_value_ref.query_ref.near_key_ref.near_value_ref = bf16[16,224,1280]{2,1,0:T(8,128)(2,1)} async-done(((bf16[16,224,1280]{2,1,0:T(8,128)(2,1)}), bf16[16,224,1280]{2,1,0:T(8,128)(2,1)}, u32[]{:S(2)}, u32[]{:S(2)}) %all-to-all-start.3) | async-done | bytes 9175072 | tf_op jit(solution)/shard_map/all_to_all | solution.py:311
  436.8 4.9 all-to-all-start.1
  441.7 14.9 %shard_map.70 = (bf16[16,32,640]{2,1,0:T(8,128)(2,1)}, f32[5,512,1]{2,1,0:T(8,128)}) custom-call(bf16[16,224,1280]{2,1,0:T(8,128)(2,1)} %all_to_all.30.far_key_ref.far_value_ref.query_ref.near_key_ref.near_value_ref, bf16[16,224,1280]{2,1,0:T(8,128)(2,1)} %all_to_all.30.far_key_ref.far_value_ref.query_ref.near_key_ref.near_value_ref, ...), custom_call_target="tpu_custom_call" | custom-call | tf_op jit(solution)/shard_map/pallas_call | solution.py:141
  456.6 1.6 all-to-all-done.1
  458.2 5.0 all-to-all-start.2
  463.1 14.9 %shard_map.71 = (bf16[16,32,640]{2,1,0:T(8,128)(2,1)}, f32[5,512,1]{2,1,0:T(8,128)}) custom-call(bf16[16,224,1280]{2,1,0:T(8,128)(2,1)} %all-to-all-done.3.far_key_ref.far_value_ref.query_ref.near_key_ref.near_value_ref, bf16[16,224,1280]{2,1,0:T(8,128)(2,1)} %all-to-all-done.3.far_key_ref.far_value_ref.query_ref.near_key_ref.near_value_ref, ...), custom_call_target="tpu_custom_call" | custom-call | tf_op jit(solution)/shard_map/pallas_call | solution.py:141
  478.0 1.5 all-to-all-done.2
  479.6 5.0 all-to-all-start.4
  484.5 0.2 select_reduce_fusion.14
  484.9 0.1 add.568
  485.0 0.1 select_reduce_fusion.7
  485.2 15.0 %shard_map.72 = (bf16[16,32,640]{2,1,0:T(8,128)(2,1)}, f32[5,512,1]{2,1,0:T(8,128)}) custom-call(bf16[16,224,1280]{2,1,0:T(8,128)(2,1)} %all-to-all-done.3.far_key_ref.far_value_ref.query_ref.near_key_ref.near_value_ref, bf16[16,224,1280]{2,1,0:T(8,128)(2,1)} %all-to-all-done.3.far_key_ref.far_value_ref.query_ref.near_key_ref.near_value_ref, ...), custom_call_target="tpu_custom_call" | custom-call | tf_op jit(solution)/shard_map/pallas_call | solution.py:141
  500.1 0.8 all-to-all-done.4
  500.9 5.2 all-to-all-start.5
  506.3 0.4 reduce
  506.7 1.8 reduce.1
  508.5 1.7 reduce.2
  510.3 0.4 reduce.3
  510.7 0.1 copy.31
  510.9 1.0 gather_fusion.3
  511.9 0.1 copy.32
  512.1 0.7 reshape.885
  512.8 9.8 %all-to-all-done.5 = bf16[16,32,640]{2,1,0:T(8,128)(2,1)S(1)} async-done(((bf16[16,32,640]{2,1,0:T(8,128)(2,1)}), bf16[16,32,640]{2,1,0:T(8,128)(2,1)S(1)}, u32[]{:S(2)}, u32[]{:S(2)}) %all-to-all-start.5) | async-done | bytes 655392 | tf_op jit(solution)/shard_map/all_to_all | solution.py:319
  522.6 0.8 copy-done.2
  523.5 1.6 pad_maximum_fusion
  525.0 3.5 gather_fusion.2
  528.5 3.5 broadcast_select_fusion
  (78 shorter events, 2.5 us)
Async XLA Ops:
  231.7 6.8 %copy-start.6 = (s32[128]{0:T(128)S(1)}, s32[128]{0:T(128)}, u32[]{:S(2)}) copy-start(s32[128]{0:T(128)} %param.8) | copy-start | bytes 1540
  231.7 8.3 %copy-start.5 = (s32[128,23]{0,1:T(8,128)S(1)}, s32[128,23]{0,1:T(8,128)}, u32[]{:S(2)}) copy-start(s32[128,23]{0,1:T(8,128)} %param.9) | copy-start | bytes 35332
  231.7 205.1 %all-to-all-start.3 = ((bf16[16,224,1280]{2,1,0:T(8,128)(2,1)}), bf16[16,224,1280]{2,1,0:T(8,128)(2,1)}, u32[]{:S(2)}, u32[]{:S(2)}) async-start(bf16[16,224,1280]{2,1,0:T(8,128)(2,1)} %get-tuple-element.15), calls=%async_computation.3 | async-start | bytes 18350080 | tf_op jit(solution)/shard_map/all_to_all | solution.py:311
  436.8 21.3 %all-to-all-start.1 = ((bf16[16,32,640]{2,1,0:T(8,128)(2,1)}), bf16[16,32,640]{2,1,0:T(8,128)(2,1)S(1)}, u32[]{:S(2)}, u32[]{:S(2)}) async-start(bf16[16,32,640]{2,1,0:T(8,128)(2,1)} %get-tuple-element.13), calls=%async_computation.1 | async-start | bytes 1310720 | tf_op jit(solution)/shard_map/all_to_all | solution.py:319
  458.2 21.4 %all-to-all-start.2 = ((bf16[16,32,640]{2,1,0:T(8,128)(2,1)}), bf16[16,32,640]{2,1,0:T(8,128)(2,1)S(1)}, u32[]{:S(2)}, u32[]{:S(2)}) async-start(bf16[16,32,640]{2,1,0:T(8,128)(2,1)} %get-tuple-element.14), calls=%async_computation.2 | async-start | bytes 1310720 | tf_op jit(solution)/shard_map/all_to_all | solution.py:319
  479.6 20.6 %copy-start = (bf16[16,32,640]{2,1,0:T(8,128)(2,1)}, bf16[16,32,640]{2,1,0:T(8,128)(2,1)S(1)}, u32[]{:S(2)}) copy-start(bf16[16,32,640]{2,1,0:T(8,128)(2,1)S(1)} %all-to-all-done.2) | copy-start | bytes 1966084
  479.6 21.4 %all-to-all-start.4 = ((bf16[16,32,640]{2,1,0:T(8,128)(2,1)}), bf16[16,32,640]{2,1,0:T(8,128)(2,1)S(1)}, u32[]{:S(2)}, u32[]{:S(2)}) async-start(bf16[16,32,640]{2,1,0:T(8,128)(2,1)} %get-tuple-element.16), calls=%async_computation.4 | async-start | bytes 1310720 | tf_op jit(solution)/shard_map/all_to_all | solution.py:319
  485.2 21.1 %copy-start.3 = (f32[5,512,1]{2,1,0:T(8,128)S(1)}, f32[5,512,1]{2,1,0:T(8,128)}, u32[]{:S(2)}) copy-start(f32[5,512,1]{2,1,0:T(8,128)} %get-tuple-element.18) | copy-start | bytes 30724
  500.9 9.3 %copy-start.1 = (bf16[16,32,640]{2,1,0:T(8,128)(2,1)}, bf16[16,32,640]{2,1,0:T(8,128)(2,1)S(1)}, u32[]{:S(2)}) copy-start(bf16[16,32,640]{2,1,0:T(8,128)(2,1)S(1)} %all-to-all-done.4) | copy-start | bytes 1966084
  500.9 21.7 %all-to-all-start.5 = ((bf16[16,32,640]{2,1,0:T(8,128)(2,1)}), bf16[16,32,640]{2,1,0:T(8,128)(2,1)S(1)}, u32[]{:S(2)}, u32[]{:S(2)}) async-start(bf16[16,32,640]{2,1,0:T(8,128)(2,1)} %get-tuple-element.17), calls=%async_computation.5 | async-start | bytes 1310720 | tf_op jit(solution)/shard_map/all_to_all | solution.py:319
  506.7 3.6 copy-start.4
  522.6 0.8 copy-start.2

commit v14 on v11

--- a/solution.py
+++ b/solution.py
@@ -298,8 +298,8 @@
     near_ok = jnp.any(listed[:, :, None] == near_tile_rows[None, None, :], axis=1)
     far_ok = jnp.any(listed[:, :, None] == far_tile_rows[None, None, :], axis=1)
     query_own = pick(own_rank, near_tile_rows)
-    near_bias = jnp.where(jnp.take(near_ok, query_own, axis=0), 0.0, masked_score)
-    far_bias = jnp.where(jnp.take(far_ok, query_own, axis=0), 0.0, masked_score)
+    near_bias = jnp.where(jnp.take(near_ok, query_own, axis=0, mode="clip"), 0.0, masked_score)
+    far_bias = jnp.where(jnp.take(far_ok, query_own, axis=0, mode="clip"), 0.0, masked_score)
     near_bias = near_bias.astype(jnp.float32)
     far_bias = far_bias.astype(jnp.float32)
     chunk_width = channels // HEAD_CHUNKS
@@ -323,7 +323,7 @@
     log_rows = (gather_rows[:, :, None] * 16 + token_iota).reshape(-1)
     heads = channels // HEAD_DIM
     log_sums = (
-        jnp.take(head_logs, log_rows, axis=1)
+        jnp.take(head_logs, log_rows, axis=1, mode="clip")
         .reshape(heads, own_count, 64)
         .transpose(1, 0, 2)
         .reshape(1, own_count, heads * 64)
@@ -335,7 +335,7 @@
     piece = strip * blocks + column // 4
     token = height * 4 + column % 4
     back_rows = (pick(my_owner, piece) * capacity + pick(my_slot, piece)) * 16 + token
-    attended = jnp.take(jnp.concatenate(outputs, axis=1), back_rows, axis=0)
+    attended = jnp.take(jnp.concatenate(outputs, axis=1), back_rows, axis=0, mode="clip")
     return (attended, log_sums)
 
 

time: 519 us -> 515 us (level)
  no operation moved by 1% of the time
where the time goes in v14:
time: 515 us; the launch traced here: 514 us
  blocking collectives  206 us (40%)
  waiting for transfers between devices  189 us (37%)
  Pallas kernels  69 us (13%)
  other arithmetic  19.8 us (4%)
  starting transfers between devices  15.7 us (3%)
  local copies, waits for them, and re-layouts  13.9 us (3%)
    all_to_all x1, blocking collectives, shards(): got = lax.all_to_all(sent, 'seq', split_axis=0, concat_axis=0, tiled=True)  206 us
    all_to_all x1, waiting for transfers between devices, shards(): got = lax.all_to_all(sent, 'seq', split_axis=0, concat_axis=0, tiled=True)  163 us
    pallas_call x2, Pallas kernels, attend(): pl.pallas_call(attention_kernel, grid=(heads,), in_specs=[pl.BlockSpec(fa...  53.8 us
    all_to_all x2, waiting for transfers between devices, shards(): lax.all_to_all(mixed, 'seq', split_axis=0, concat_axis=0, tiled=True)  26.6 us
    pallas_call x1, Pallas kernels, pack(): pl.pallas_call(pack_kernel, grid=(group_size // dests,), in_specs=[pl.Blo...  15.3 us
  transfers between devices with their start and end apart: 3, of which 3 were waited for; matrix products, arithmetic and copies ran while one was open for 3% of the time, Pallas kernels for 10%

profile of v14, /device:TPU:13, one launch (start us, length us, event | category | flops | bytes accessed | tf_op | source)
XLA Modules:
  0.0 514.2 jit_solution(10209754795393803666)
XLA Ops:
  0.7 0.7 iota_compare_fusion.12
  1.3 0.7 eq.398
  2.1 1.8 select_reduce_fusion
  3.8 0.7 broadcast_compare_fusion
  4.5 0.8 select_reduce_fusion.2
  5.3 0.3 select_reduce_fusion.3
  5.7 0.2 reduce_window_sum.28
  5.8 0.1 select_reduce_fusion.11
  6.2 0.1 add.413
  6.4 0.1 add.420
  6.5 0.1 add.415
  6.6 0.1 add.424
  6.7 1.2 fusion.far_hot_ref
  7.9 0.2 convert_reduce_fusion
  8.1 0.1 reshape.820
  8.2 0.7 dynamic_slice.10
  9.1 0.1 select_reduce_fusion.13
  9.2 0.1 copy.25
  9.4 0.1 add.429
  9.6 0.1 add.436
  9.7 0.1 add.431
  9.8 0.1 add.439
  9.9 1.0 fusion.1.own_hot_ref
  10.9 15.3 %shard_map.68 = (bf16[16,224,1280]{2,1,0:T(8,128)(2,1)}, bf16[16,224,1280]{2,1,0:T(8,128)(2,1)}) custom-call(bf16[16,64,512]{2,1,0:T(8,128)(2,1)} %fusion.far_hot_ref, bf16[16,32,512]{2,1,0:T(8,128)(2,1)} %fusion.1.own_hot_ref, bf16[512,2560]{1,0:T(8,128)(2,1)} %query_ref.1, bf16[512,2560]{1,0:T(8,128)(2,1)} %key_ref.1, bf16[512,2560]{1,0:T(8,128)(2,1)} %value_ref.1), custom_call_target="tpu_custom_call" | custom-call | tf_op jit(solution)/shard_map/pallas_call | solution.py:205
  26.1 205.6 %all_to_all.20.far_key_ref.far_value_ref.query_ref.near_key_ref.near_value_ref = bf16[16,224,1280]{2,1,0:T(8,128)(2,1)} all-to-all(bf16[16,224,1280]{2,1,0:T(8,128)(2,1)} %get-tuple-element.8), channel_id=1, replica_groups=mesh['groups'=2,'seq'=16] {'seq'}, dimensions={0} | all-to-all | bytes 18350080 | tf_op jit(solution)/shard_map/all_to_all | solution.py:311
  231.8 5.9 %all-to-all-start.2 = ((bf16[16,224,1280]{2,1,0:T(8,128)(2,1)}), bf16[16,224,1280]{2,1,0:T(8,128)(2,1)}, u32[]{:S(2)}, u32[]{:S(2)}) async-start(bf16[16,224,1280]{2,1,0:T(8,128)(2,1)} %get-tuple-element.10), calls=%async_computation.2 | async-start | bytes 18350080 | tf_op jit(solution)/shard_map/all_to_all | solution.py:311
  237.8 0.2 reduce_window_sum.30
  238.0 0.1 fusion.6
  238.1 0.2 select_reduce_fusion.8
  238.5 0.1 eq.441
  238.6 0.1 fusion.3
  238.6 0.2 reduce_window_sum.29
  239.0 0.1 select_reduce_fusion.12
  239.1 0.1 copy.27
  239.3 0.1 eq.427
  239.4 0.2 select_reduce_fusion.7
  239.6 0.2 select_reduce_fusion.1
  239.8 0.1 select_reduce_fusion.15
  240.0 0.5 select_reduce_fusion.4
  240.5 0.2 compare_reduce_fusion
  240.7 1.9 gather_fusion.1
  242.6 0.1 compare_reduce_fusion.1
  242.7 1.8 gather_fusion
  244.5 1.1 broadcast_select_fusion.1.near_bias_ref
  245.7 1.6 broadcast_select_fusion.far_bias_ref
  247.3 26.9 %shard_map.69 = (bf16[16,32,1280]{2,1,0:T(8,128)(2,1)}, f32[10,512,1]{2,1,0:T(8,128)}) custom-call(bf16[16,224,1280]{2,1,0:T(8,128)(2,1)} %all_to_all.20.far_key_ref.far_value_ref.query_ref.near_key_ref.near_value_ref, bf16[16,224,1280]{2,1,0:T(8,128)(2,1)} %all_to_all.20.far_key_ref.far_value_ref.query_ref.near_key_ref.near_value_ref, ...), custom_call_target="tpu_custom_call" | custom-call | tf_op jit(solution)/shard_map/pallas_call | solution.py:141
  274.1 162.8 %all-to-all-done.2.far_key_ref.far_value_ref.query_ref.near_key_ref.near_value_ref = bf16[16,224,1280]{2,1,0:T(8,128)(2,1)} async-done(((bf16[16,224,1280]{2,1,0:T(8,128)(2,1)}), bf16[16,224,1280]{2,1,0:T(8,128)(2,1)}, u32[]{:S(2)}, u32[]{:S(2)}) %all-to-all-start.2) | async-done | bytes 9175072 | tf_op jit(solution)/shard_map/all_to_all | solution.py:311
  436.9 4.9 all-to-all-start.1
  441.8 26.9 %shard_map.70 = (bf16[16,32,1280]{2,1,0:T(8,128)(2,1)}, f32[10,512,1]{2,1,0:T(8,128)}) custom-call(bf16[16,224,1280]{2,1,0:T(8,128)(2,1)} %all-to-all-done.2.far_key_ref.far_value_ref.query_ref.near_key_ref.near_value_ref, bf16[16,224,1280]{2,1,0:T(8,128)(2,1)} %all-to-all-done.2.far_key_ref.far_value_ref.query_ref.near_key_ref.near_value_ref, ...), custom_call_target="tpu_custom_call" | custom-call | tf_op jit(solution)/shard_map/pallas_call | solution.py:141
  468.7 3.6 all-to-all-done.1
  472.4 4.9 all-to-all-start.3
  477.2 0.2 select_reduce_fusion.14
  477.6 0.1 reshape.851
  477.7 0.1 select_reduce_fusion.6
  477.8 2.5 reduce
  480.3 2.5 reduce.1
  482.8 0.1 copy.29
  483.0 1.0 gather_fusion.3
  484.0 0.1 copy.30
  484.2 0.7 reshape.824
  484.9 22.9 %all-to-all-done.3 = bf16[16,32,1280]{2,1,0:T(8,128)(2,1)S(1)} async-done(((bf16[16,32,1280]{2,1,0:T(8,128)(2,1)}), bf16[16,32,1280]{2,1,0:T(8,128)(2,1)S(1)}, u32[]{:S(2)}, u32[]{:S(2)}) %all-to-all-start.3) | async-done | bytes 1310752 | tf_op jit(solution)/shard_map/all_to_all | solution.py:313
  507.8 1.1 copy-done.1
  508.8 1.9 pad_maximum_fusion
  510.7 3.5 gather_fusion.2
  (57 shorter events, 1.6 us)
Async XLA Ops:
  231.8 6.8 %copy-start.3 = (s32[128]{0:T(128)S(1)}, s32[128]{0:T(128)}, u32[]{:S(2)}) copy-start(s32[128]{0:T(128)} %param.8) | copy-start | bytes 1540
  231.8 8.3 %copy-start.2 = (s32[128,23]{0,1:T(8,128)S(1)}, s32[128,23]{0,1:T(8,128)}, u32[]{:S(2)}) copy-start(s32[128,23]{0,1:T(8,128)} %param.9) | copy-start | bytes 35332
  231.8 205.1 %all-to-all-start.2 = ((bf16[16,224,1280]{2,1,0:T(8,128)(2,1)}), bf16[16,224,1280]{2,1,0:T(8,128)(2,1)}, u32[]{:S(2)}, u32[]{:S(2)}) async-start(bf16[16,224,1280]{2,1,0:T(8,128)(2,1)} %get-tuple-element.10), calls=%async_computation.2 | async-start | bytes 18350080 | tf_op jit(solution)/shard_map/all_to_all | solution.py:311
  436.9 35.5 %all-to-all-start.1 = ((bf16[16,32,1280]{2,1,0:T(8,128)(2,1)}), bf16[16,32,1280]{2,1,0:T(8,128)(2,1)S(1)}, u32[]{:S(2)}, u32[]{:S(2)}) async-start(bf16[16,32,1280]{2,1,0:T(8,128)(2,1)} %get-tuple-element.9), calls=%async_computation.1 | async-start | bytes 2621440 | tf_op jit(solution)/shard_map/all_to_all | solution.py:313
  472.3 8.0 %copy-start = (bf16[16,32,1280]{2,1,0:T(8,128)(2,1)}, bf16[16,32,1280]{2,1,0:T(8,128)(2,1)S(1)}, u32[]{:S(2)}) copy-start(bf16[16,32,1280]{2,1,0:T(8,128)(2,1)S(1)} %all-to-all-done.1) | copy-start | bytes 3932164
  472.4 35.4 %all-to-all-start.3 = ((bf16[16,32,1280]{2,1,0:T(8,128)(2,1)}), bf16[16,32,1280]{2,1,0:T(8,128)(2,1)S(1)}, u32[]{:S(2)}, u32[]{:S(2)}) async-start(bf16[16,32,1280]{2,1,0:T(8,128)(2,1)} %get-tuple-element.11), calls=%async_computation.3 | async-start | bytes 2621440 | tf_op jit(solution)/shard_map/all_to_all | solution.py:313
  507.8 1.1 copy-start.1

commit v15 on v14

--- a/solution.py
+++ b/solution.py
@@ -335,7 +335,9 @@
     piece = strip * blocks + column // 4
     token = height * 4 + column % 4
     back_rows = (pick(my_owner, piece) * capacity + pick(my_slot, piece)) * 16 + token
-    attended = jnp.take(jnp.concatenate(outputs, axis=1), back_rows, axis=0, mode="clip")
+    attended = jnp.concatenate(
+        [jnp.take(part, back_rows, axis=0, mode="clip") for part in outputs], axis=1
+    )
     return (attended, log_sums)
 
 

time: 515 us -> 514 us (level)
  transfers between devices with their start and end apart: 3 -> 3, of which waited for: 3 -> 3; matrix products, arithmetic and copies ran while one was open for 3% -> 4% of each run, Pallas kernels for 10% -> 10%
where the time goes in v15:
time: 514 us
  blocking collectives  206 us (40%)
  waiting for transfers between devices  186 us (36%)
  Pallas kernels  69 us (13%)
  other arithmetic  20.9 us (4%)
  starting transfers between devices  15.7 us (3%)
  local copies, waits for them, and re-layouts  15.1 us (3%)
    all_to_all x1, blocking collectives, shards(): got = lax.all_to_all(sent, 'seq', split_axis=0, concat_axis=0, tiled=True)  206 us
    all_to_all x1, waiting for transfers between devices, shards(): got = lax.all_to_all(sent, 'seq', split_axis=0, concat_axis=0, tiled=True)  163 us
    pallas_call x2, Pallas kernels, attend(): pl.pallas_call(attention_kernel, grid=(heads,), in_specs=[pl.BlockSpec(fa...  53.8 us
    all_to_all x2, waiting for transfers between devices, shards(): lax.all_to_all(mixed, 'seq', split_axis=0, concat_axis=0, tiled=True)  23.7 us
    pallas_call x1, Pallas kernels, pack(): pl.pallas_call(pack_kernel, grid=(group_size // dests,), in_specs=[pl.Blo...  15.3 us
  transfers between devices with their start and end apart: 3, of which 3 were waited for; matrix products, arithmetic and copies ran while one was open for 4% of the time, Pallas kernels for 10%

profile of v15, /device:TPU:13, one launch (start us, length us, event | category | flops | bytes accessed | tf_op | source)
XLA Modules:
  0.0 513.7 jit_solution(14358011748594632303)
XLA Ops:
  0.7 0.7 iota_compare_fusion.12
  1.3 0.7 eq.398
  2.1 1.8 select_reduce_fusion
  3.8 0.7 broadcast_compare_fusion
  4.5 0.8 select_reduce_fusion.2
  5.3 0.3 select_reduce_fusion.3
  5.7 0.2 reduce_window_sum.28
  5.8 0.1 select_reduce_fusion.11
  6.2 0.1 add.413
  6.4 0.1 add.420
  6.5 0.1 add.415
  6.6 0.1 add.424
  6.7 1.2 fusion.far_hot_ref
  7.9 0.2 convert_reduce_fusion
  8.1 0.1 reshape.820
  8.2 0.7 dynamic_slice.10
  9.1 0.1 select_reduce_fusion.13
  9.2 0.1 copy.25
  9.4 0.1 add.429
  9.6 0.1 add.436
  9.7 0.1 add.431
  9.8 0.1 add.439
  9.9 1.0 fusion.1.own_hot_ref
  10.9 15.3 %shard_map.68 = (bf16[16,224,1280]{2,1,0:T(8,128)(2,1)}, bf16[16,224,1280]{2,1,0:T(8,128)(2,1)}) custom-call(bf16[16,64,512]{2,1,0:T(8,128)(2,1)} %fusion.far_hot_ref, bf16[16,32,512]{2,1,0:T(8,128)(2,1)} %fusion.1.own_hot_ref, bf16[512,2560]{1,0:T(8,128)(2,1)} %query_ref.1, bf16[512,2560]{1,0:T(8,128)(2,1)} %key_ref.1, bf16[512,2560]{1,0:T(8,128)(2,1)} %value_ref.1), custom_call_target="tpu_custom_call" | custom-call | tf_op jit(solution)/shard_map/pallas_call | solution.py:205
  26.1 205.6 %all_to_all.20.far_key_ref.far_value_ref.query_ref.near_key_ref.near_value_ref = bf16[16,224,1280]{2,1,0:T(8,128)(2,1)} all-to-all(bf16[16,224,1280]{2,1,0:T(8,128)(2,1)} %get-tuple-element.8), channel_id=1, replica_groups=mesh['groups'=2,'seq'=16] {'seq'}, dimensions={0} | all-to-all | bytes 18350080 | tf_op jit(solution)/shard_map/all_to_all | solution.py:311
  231.8 5.9 %all-to-all-start.2 = ((bf16[16,224,1280]{2,1,0:T(8,128)(2,1)}), bf16[16,224,1280]{2,1,0:T(8,128)(2,1)}, u32[]{:S(2)}, u32[]{:S(2)}) async-start(bf16[16,224,1280]{2,1,0:T(8,128)(2,1)} %get-tuple-element.10), calls=%async_computation.2 | async-start | bytes 18350080 | tf_op jit(solution)/shard_map/all_to_all | solution.py:311
  237.8 0.2 reduce_window_sum.30
  238.0 0.1 fusion.6
  238.1 0.2 select_reduce_fusion.8
  238.5 0.1 eq.441
  238.6 0.1 fusion.3
  238.6 0.2 reduce_window_sum.29
  239.0 0.1 select_reduce_fusion.12
  239.1 0.1 copy.27
  239.3 0.1 eq.427
  239.4 0.2 select_reduce_fusion.7
  239.6 0.2 select_reduce_fusion.1
  239.8 0.1 select_reduce_fusion.15
  240.0 0.5 select_reduce_fusion.4
  240.5 0.2 compare_reduce_fusion
  240.7 1.9 gather_fusion.1
  242.6 0.1 compare_reduce_fusion.1
  242.7 1.8 gather_fusion
  244.5 1.1 broadcast_select_fusion.1.near_bias_ref
  245.7 1.6 broadcast_select_fusion.far_bias_ref
  247.3 26.9 %shard_map.69 = (bf16[16,32,1280]{2,1,0:T(8,128)(2,1)}, f32[10,512,1]{2,1,0:T(8,128)}) custom-call(bf16[16,224,1280]{2,1,0:T(8,128)(2,1)} %all_to_all.20.far_key_ref.far_value_ref.query_ref.near_key_ref.near_value_ref, bf16[16,224,1280]{2,1,0:T(8,128)(2,1)} %all_to_all.20.far_key_ref.far_value_ref.query_ref.near_key_ref.near_value_ref, ...), custom_call_target="tpu_custom_call" | custom-call | tf_op jit(solution)/shard_map/pallas_call | solution.py:141
  274.1 162.8 %all-to-all-done.2.far_key_ref.far_value_ref.query_ref.near_key_ref.near_value_ref = bf16[16,224,1280]{2,1,0:T(8,128)(2,1)} async-done(((bf16[16,224,1280]{2,1,0:T(8,128)(2,1)}), bf16[16,224,1280]{2,1,0:T(8,128)(2,1)}, u32[]{:S(2)}, u32[]{:S(2)}) %all-to-all-start.2) | async-done | bytes 9175072 | tf_op jit(solution)/shard_map/all_to_all | solution.py:311
  436.9 4.9 all-to-all-start.1
  441.8 26.9 %shard_map.70 = (bf16[16,32,1280]{2,1,0:T(8,128)(2,1)}, f32[10,512,1]{2,1,0:T(8,128)}) custom-call(bf16[16,224,1280]{2,1,0:T(8,128)(2,1)} %all-to-all-done.2.far_key_ref.far_value_ref.query_ref.near_key_ref.near_value_ref, bf16[16,224,1280]{2,1,0:T(8,128)(2,1)} %all-to-all-done.2.far_key_ref.far_value_ref.query_ref.near_key_ref.near_value_ref, ...), custom_call_target="tpu_custom_call" | custom-call | tf_op jit(solution)/shard_map/pallas_call | solution.py:141
  468.7 3.6 all-to-all-done.1
  472.3 4.9 all-to-all-start.3
  477.2 0.2 select_reduce_fusion.14
  477.6 0.1 reshape.859
  477.7 0.1 select_reduce_fusion.6
  477.8 2.5 reduce
  480.3 2.5 reduce.1
  482.8 0.1 copy.29
  483.0 1.0 gather_fusion.4
  484.0 0.1 copy.30
  484.2 0.7 reshape.824
  484.9 2.9 gather_fusion.2
  487.7 20.0 %all-to-all-done.3 = bf16[16,32,1280]{2,1,0:T(8,128)(2,1)S(1)} async-done(((bf16[16,32,1280]{2,1,0:T(8,128)(2,1)}), bf16[16,32,1280]{2,1,0:T(8,128)(2,1)S(1)}, u32[]{:S(2)}, u32[]{:S(2)}) %all-to-all-start.3) | async-done | bytes 1310752 | tf_op jit(solution)/shard_map/all_to_all | solution.py:313
  507.8 2.9 gather_fusion.3
  510.7 3.0 pad_maximum_fusion
  (56 shorter events, 1.6 us)
Async XLA Ops:
  231.8 6.8 %copy-start.2 = (s32[128]{0:T(128)S(1)}, s32[128]{0:T(128)}, u32[]{:S(2)}) copy-start(s32[128]{0:T(128)} %param.8) | copy-start | bytes 1540
  231.8 8.3 %copy-start.1 = (s32[128,23]{0,1:T(8,128)S(1)}, s32[128,23]{0,1:T(8,128)}, u32[]{:S(2)}) copy-start(s32[128,23]{0,1:T(8,128)} %param.9) | copy-start | bytes 35332
  231.8 205.1 %all-to-all-start.2 = ((bf16[16,224,1280]{2,1,0:T(8,128)(2,1)}), bf16[16,224,1280]{2,1,0:T(8,128)(2,1)}, u32[]{:S(2)}, u32[]{:S(2)}) async-start(bf16[16,224,1280]{2,1,0:T(8,128)(2,1)} %get-tuple-element.10), calls=%async_computation.2 | async-start | bytes 18350080 | tf_op jit(solution)/shard_map/all_to_all | solution.py:311
  436.9 35.5 %all-to-all-start.1 = ((bf16[16,32,1280]{2,1,0:T(8,128)(2,1)}), bf16[16,32,1280]{2,1,0:T(8,128)(2,1)S(1)}, u32[]{:S(2)}, u32[]{:S(2)}) async-start(bf16[16,32,1280]{2,1,0:T(8,128)(2,1)} %get-tuple-element.9), calls=%async_computation.1 | async-start | bytes 2621440 | tf_op jit(solution)/shard_map/all_to_all | solution.py:313
  472.3 35.4 %all-to-all-start.3 = ((bf16[16,32,1280]{2,1,0:T(8,128)(2,1)}), bf16[16,32,1280]{2,1,0:T(8,128)(2,1)S(1)}, u32[]{:S(2)}, u32[]{:S(2)}) async-start(bf16[16,32,1280]{2,1,0:T(8,128)(2,1)} %get-tuple-element.11), calls=%async_computation.3 | async-start | bytes 2621440 | tf_op jit(solution)/shard_map/all_to_all | solution.py:313
  507.8 2.9 copy-start

commit v16 on v15

--- a/solution.py
+++ b/solution.py
@@ -97,37 +97,54 @@
 HEAD_CHUNKS = 2
 
 
+HEADS_PER_STEP = 2
+
+
 def attention_kernel(
     far_key_ref, far_value_ref, query_ref, near_key_ref, near_value_ref, near_bias_ref,
     far_bias_ref, out_ref, log_ref
 ):
-    def flat(ref):
-        block = ref[...]
+    def flat(ref, columns):
+        block = ref[:, :, columns]
         return block.reshape(block.shape[0] * block.shape[1], block.shape[2])
 
-    query = flat(query_ref)
     dims = (((1,), (1,)), ((), ()))
     scale = HEAD_DIM ** (-0.5)
-    near_scores = lax.dot_general(
-        query, flat(near_key_ref), dims, preferred_element_type=jnp.float32
-    ) * scale + near_bias_ref[...]
-    far_scores = lax.dot_general(
-        query, flat(far_key_ref), dims, preferred_element_type=jnp.float32
-    ) * scale + far_bias_ref[...]
-    row_max = jnp.maximum(
-        jnp.max(near_scores, axis=1, keepdims=True), jnp.max(far_scores, axis=1, keepdims=True)
-    )
-    near_exp = jnp.exp(near_scores - row_max)
-    far_exp = jnp.exp(far_scores - row_max)
-    total = jnp.sum(near_exp, axis=1, keepdims=True) + jnp.sum(far_exp, axis=1, keepdims=True)
-    log_total = row_max + jnp.log(total)
-    inverse = 1.0 / total
-    near_weights = (near_exp * inverse).astype(jnp.bfloat16)
-    far_weights = (far_exp * inverse).astype(jnp.bfloat16)
-    mixed = jnp.dot(near_weights, flat(near_value_ref), preferred_element_type=jnp.float32)
-    mixed = mixed + jnp.dot(far_weights, flat(far_value_ref), preferred_element_type=jnp.float32)
-    out_ref[...] = mixed.astype(out_ref.dtype).reshape(out_ref.shape)
-    log_ref[...] = log_total
+    near_bias = near_bias_ref[...]
+    far_bias = far_bias_ref[...]
+    for step_head in range(log_ref.shape[0]):
+        columns = slice(step_head * HEAD_DIM, (step_head + 1) * HEAD_DIM)
+        query = flat(query_ref, columns)
+        near_scores = lax.dot_general(
+            query, flat(near_key_ref, columns), dims, preferred_element_type=jnp.float32
+        ) * scale + near_bias
+        far_scores = lax.dot_general(
+            query, flat(far_key_ref, columns), dims, preferred_element_type=jnp.float32
+        ) * scale + far_bias
+        row_max = jnp.maximum(
+            jnp.max(near_scores, axis=1, keepdims=True),
+            jnp.max(far_scores, axis=1, keepdims=True),
+        )
+        near_exp = jnp.exp(near_scores - row_max)
+        far_exp = jnp.exp(far_scores - row_max)
+        total = jnp.sum(near_exp, axis=1, keepdims=True) + jnp.sum(
+            far_exp, axis=1, keepdims=True
+        )
+        log_total = row_max + jnp.log(total)
+        inverse = 1.0 / total
+        near_weights = (near_exp * inverse).astype(jnp.bfloat16)
+        far_weights = (far_exp * inverse).astype(jnp.bfloat16)
+        mixed = jnp.dot(
+            near_weights, flat(near_value_ref, columns), preferred_element_type=jnp.float32
+        )
+        mixed = mixed + jnp.dot(
+            far_weights, flat(far_value_ref, columns), preferred_element_type=jnp.float32
+        )
+        out_shape = out_ref.shape
+        out_ref[:, :, columns] = mixed.astype(out_ref.dtype).reshape(
+            out_shape[0], out_shape[1], HEAD_DIM
+        )
+        log_ref[step_head] = log_total
 
 
 def attend(got, unit, near_bias, far_bias):
@@ -135,12 +152,14 @@
     far_rows = FAR_SLOTS * 16
     rows = group_size * unit
     heads = channels // HEAD_DIM
+    per_step = HEADS_PER_STEP if heads % HEADS_PER_STEP == 0 else 1
+    width = per_step * HEAD_DIM
     base = 2 * far_rows // unit
-    far_spec = (group_size, far_rows, HEAD_DIM)
-    own_spec = (group_size, unit, HEAD_DIM)
+    far_spec = (group_size, far_rows, width)
+    own_spec = (group_size, unit, width)
     return pl.pallas_call(
         attention_kernel,
-        grid=(heads,),
+        grid=(heads // per_step,),
         in_specs=[
             pl.BlockSpec(far_spec, lambda h: (0, 0, h)),
             pl.BlockSpec(far_spec, lambda h: (0, 1, h)),
@@ -152,7 +171,7 @@
         ],
         out_specs=[
             pl.BlockSpec(own_spec, lambda h: (0, 0, h)),
-            pl.BlockSpec((None, rows, 1), lambda h: (h, 0, 0)),
+            pl.BlockSpec((per_step, rows, 1), lambda h: (h, 0, 0)),
         ],
         out_shape=[
             jax.ShapeDtypeStruct((group_size, unit, channels), jnp.bfloat16),

time: 514 us -> 514 us (level)
  waiting for transfers between devices: 186 us -> 197 us
  Pallas kernels: 69 us -> 58.9 us
    pallas_call x2, Pallas kernels: 53.8 us -> 43.6 us  [attend(): pl.pallas_call(attention_kernel, grid=(heads // per_step,), in_specs=[pl....]
  transfers between devices with their start and end apart: 3 -> 3, of which waited for: 3 -> 3; matrix products, arithmetic and copies ran while one was open for 4% -> 4% of each run, Pallas kernels for 10% -> 8%
where the time goes in v16:
time: 514 us
  blocking collectives  206 us (40%)
  waiting for transfers between devices  197 us (38%)
  Pallas kernels  58.9 us (11%)
  other arithmetic  20.9 us (4%)
  starting transfers between devices  15.7 us (3%)
  local copies, waits for them, and re-layouts  15.1 us (3%)
    all_to_all x1, blocking collectives, shards(): got = lax.all_to_all(sent, 'seq', split_axis=0, concat_axis=0, tiled=True)  206 us
    all_to_all x1, waiting for transfers between devices, shards(): got = lax.all_to_all(sent, 'seq', split_axis=0, concat_axis=0, tiled=True)  168 us
    pallas_call x2, Pallas kernels, attend(): pl.pallas_call(attention_kernel, grid=(heads // per_step,), in_specs=[pl....  43.6 us
    all_to_all x2, waiting for transfers between devices, shards(): lax.all_to_all(mixed, 'seq', split_axis=0, concat_axis=0, tiled=True)  28.8 us
    pallas_call x1, Pallas kernels, pack(): pl.pallas_call(pack_kernel, grid=(group_size // dests,), in_specs=[pl.Blo...  15.3 us
  transfers between devices with their start and end apart: 3, of which 3 were waited for; matrix products, arithmetic and copies ran while one was open for 4% of the time, Pallas kernels for 8%

profile of v16, /device:TPU:13, one launch (start us, length us, event | category | flops | bytes accessed | tf_op | source)
XLA Modules:
  0.0 513.7 jit_solution(13235933520190602583)
XLA Ops:
  0.7 0.7 iota_compare_fusion.12
  1.3 0.7 eq.398
  2.1 1.8 select_reduce_fusion
  3.8 0.7 broadcast_compare_fusion
  4.5 0.8 select_reduce_fusion.2
  5.3 0.3 select_reduce_fusion.3
  5.7 0.2 reduce_window_sum.28
  5.8 0.1 select_reduce_fusion.11
  6.2 0.1 add.413
  6.4 0.1 add.420
  6.5 0.1 add.415
  6.6 0.1 add.424
  6.7 1.2 fusion.far_hot_ref
  7.9 0.2 convert_reduce_fusion
  8.1 0.1 reshape.820
  8.2 0.7 dynamic_slice.10
  9.1 0.1 select_reduce_fusion.13
  9.2 0.1 copy.25
  9.4 0.1 add.429
  9.6 0.1 add.436
  9.7 0.1 add.431
  9.8 0.1 add.439
  9.9 1.0 fusion.1.own_hot_ref
  10.9 15.3 %shard_map.68 = (bf16[16,224,1280]{2,1,0:T(8,128)(2,1)}, bf16[16,224,1280]{2,1,0:T(8,128)(2,1)}) custom-call(bf16[16,64,512]{2,1,0:T(8,128)(2,1)} %fusion.far_hot_ref, bf16[16,32,512]{2,1,0:T(8,128)(2,1)} %fusion.1.own_hot_ref, bf16[512,2560]{1,0:T(8,128)(2,1)} %query_ref.1, bf16[512,2560]{1,0:T(8,128)(2,1)} %key_ref.1, bf16[512,2560]{1,0:T(8,128)(2,1)} %value_ref.1), custom_call_target="tpu_custom_call" | custom-call | tf_op jit(solution)/shard_map/pallas_call | solution.py:224
  26.1 205.6 %all_to_all.20.far_key_ref.far_value_ref.query_ref.near_key_ref.near_value_ref = bf16[16,224,1280]{2,1,0:T(8,128)(2,1)} all-to-all(bf16[16,224,1280]{2,1,0:T(8,128)(2,1)} %get-tuple-element.8), channel_id=1, replica_groups=mesh['groups'=2,'seq'=16] {'seq'}, dimensions={0} | all-to-all | bytes 18350080 | tf_op jit(solution)/shard_map/all_to_all | solution.py:330
  231.8 5.9 %all-to-all-start.2 = ((bf16[16,224,1280]{2,1,0:T(8,128)(2,1)}), bf16[16,224,1280]{2,1,0:T(8,128)(2,1)}, u32[]{:S(2)}, u32[]{:S(2)}) async-start(bf16[16,224,1280]{2,1,0:T(8,128)(2,1)} %get-tuple-element.10), calls=%async_computation.2 | async-start | bytes 18350080 | tf_op jit(solution)/shard_map/all_to_all | solution.py:330
  237.8 0.2 reduce_window_sum.30
  238.0 0.1 fusion.6
  238.1 0.2 select_reduce_fusion.8
  238.5 0.1 eq.441
  238.6 0.1 fusion.3
  238.6 0.2 reduce_window_sum.29
  239.0 0.1 select_reduce_fusion.12
  239.1 0.1 copy.27
  239.3 0.1 eq.427
  239.4 0.2 select_reduce_fusion.7
  239.6 0.2 select_reduce_fusion.1
  239.8 0.1 select_reduce_fusion.15
  240.0 0.5 select_reduce_fusion.4
  240.5 0.2 compare_reduce_fusion
  240.7 1.9 gather_fusion.1
  242.6 0.1 compare_reduce_fusion.1
  242.7 1.8 gather_fusion
  244.5 1.1 broadcast_select_fusion.1.near_bias_ref
  245.7 1.6 broadcast_select_fusion.far_bias_ref
  247.3 21.8 %shard_map.69 = (bf16[16,32,1280]{2,1,0:T(8,128)(2,1)}, f32[10,512,1]{2,1,0:T(8,128)}) custom-call(bf16[16,224,1280]{2,1,0:T(8,128)(2,1)} %all_to_all.20.far_key_ref.far_value_ref.query_ref.near_key_ref.near_value_ref, bf16[16,224,1280]{2,1,0:T(8,128)(2,1)} %all_to_all.20.far_key_ref.far_value_ref.query_ref.near_key_ref.near_value_ref, ...), custom_call_target="tpu_custom_call" | custom-call | tf_op jit(solution)/shard_map/pallas_call | solution.py:160
  269.0 167.8 %all-to-all-done.2.far_key_ref.far_value_ref.query_ref.near_key_ref.near_value_ref = bf16[16,224,1280]{2,1,0:T(8,128)(2,1)} async-done(((bf16[16,224,1280]{2,1,0:T(8,128)(2,1)}), bf16[16,224,1280]{2,1,0:T(8,128)(2,1)}, u32[]{:S(2)}, u32[]{:S(2)}) %all-to-all-start.2) | async-done | bytes 9175072 | tf_op jit(solution)/shard_map/all_to_all | solution.py:330
  436.9 4.9 all-to-all-start.1
  441.8 21.8 %shard_map.70 = (bf16[16,32,1280]{2,1,0:T(8,128)(2,1)}, f32[10,512,1]{2,1,0:T(8,128)}) custom-call(bf16[16,224,1280]{2,1,0:T(8,128)(2,1)} %all-to-all-done.2.far_key_ref.far_value_ref.query_ref.near_key_ref.near_value_ref, bf16[16,224,1280]{2,1,0:T(8,128)(2,1)} %all-to-all-done.2.far_key_ref.far_value_ref.query_ref.near_key_ref.near_value_ref, ...), custom_call_target="tpu_custom_call" | custom-call | tf_op jit(solution)/shard_map/pallas_call | solution.py:160
  463.6 8.7 %all-to-all-done.1 = bf16[16,32,1280]{2,1,0:T(8,128)(2,1)S(1)} async-done(((bf16[16,32,1280]{2,1,0:T(8,128)(2,1)}), bf16[16,32,1280]{2,1,0:T(8,128)(2,1)S(1)}, u32[]{:S(2)}, u32[]{:S(2)}) %all-to-all-start.1) | async-done | bytes 1310752 | tf_op jit(solution)/shard_map/all_to_all | solution.py:332
  472.3 4.9 all-to-all-start.3
  477.2 0.2 select_reduce_fusion.14
  477.6 0.1 reshape.859
  477.7 0.1 select_reduce_fusion.6
  477.8 2.5 reduce
  480.3 2.5 reduce.1
  482.8 0.1 copy.29
  483.0 1.0 gather_fusion.4
  484.0 0.1 copy.30
  484.2 0.7 reshape.824
  484.9 2.9 gather_fusion.2
  487.7 20.0 %all-to-all-done.3 = bf16[16,32,1280]{2,1,0:T(8,128)(2,1)S(1)} async-done(((bf16[16,32,1280]{2,1,0:T(8,128)(2,1)}), bf16[16,32,1280]{2,1,0:T(8,128)(2,1)S(1)}, u32[]{:S(2)}, u32[]{:S(2)}) %all-to-all-start.3) | async-done | bytes 1310752 | tf_op jit(solution)/shard_map/all_to_all | solution.py:332
  507.8 2.9 gather_fusion.3
  510.7 3.0 pad_maximum_fusion
  (56 shorter events, 1.6 us)
Async XLA Ops:
  231.8 6.8 %copy-start.2 = (s32[128]{0:T(128)S(1)}, s32[128]{0:T(128)}, u32[]{:S(2)}) copy-start(s32[128]{0:T(128)} %param.8) | copy-start | bytes 1540
  231.8 8.3 %copy-start.1 = (s32[128,23]{0,1:T(8,128)S(1)}, s32[128,23]{0,1:T(8,128)}, u32[]{:S(2)}) copy-start(s32[128,23]{0,1:T(8,128)} %param.9) | copy-start | bytes 35332
  231.8 205.1 %all-to-all-start.2 = ((bf16[16,224,1280]{2,1,0:T(8,128)(2,1)}), bf16[16,224,1280]{2,1,0:T(8,128)(2,1)}, u32[]{:S(2)}, u32[]{:S(2)}) async-start(bf16[16,224,1280]{2,1,0:T(8,128)(2,1)} %get-tuple-element.10), calls=%async_computation.2 | async-start | bytes 18350080 | tf_op jit(solution)/shard_map/all_to_all | solution.py:330
  436.9 35.5 %all-to-all-start.1 = ((bf16[16,32,1280]{2,1,0:T(8,128)(2,1)}), bf16[16,32,1280]{2,1,0:T(8,128)(2,1)S(1)}, u32[]{:S(2)}, u32[]{:S(2)}) async-start(bf16[16,32,1280]{2,1,0:T(8,128)(2,1)} %get-tuple-element.9), calls=%async_computation.1 | async-start | bytes 2621440 | tf_op jit(solution)/shard_map/all_to_all | solution.py:332
  472.3 35.4 %all-to-all-start.3 = ((bf16[16,32,1280]{2,1,0:T(8,128)(2,1)}), bf16[16,32,1280]{2,1,0:T(8,128)(2,1)S(1)}, u32[]{:S(2)}, u32[]{:S(2)}) async-start(bf16[16,32,1280]{2,1,0:T(8,128)(2,1)} %get-tuple-element.11), calls=%async_computation.3 | async-start | bytes 2621440 | tf_op jit(solution)/shard_map/all_to_all | solution.py:332
  507.8 2.9 copy-start

commit v17 on v16

--- a/solution.py
+++ b/solution.py
@@ -184,13 +184,17 @@
 PACK_DESTS = 4
 
 
-def pack_kernel(far_hot_ref, own_hot_ref, query_ref, key_ref, value_ref, *out_refs):
-    far_hot = far_hot_ref[...]
-    own_hot = own_hot_ref[...]
-    dests, far_rows, local_rows = far_hot.shape
-    own_rows = own_hot.shape[1]
-    far_hot = far_hot.reshape(dests * far_rows, local_rows)
-    own_hot = own_hot.reshape(dests * own_rows, local_rows)
+def pack_kernel(far_index_ref, own_index_ref, query_ref, key_ref, value_ref, *out_refs):
+    dests = out_refs[0].shape[0]
+    local_rows = query_ref.shape[0]
+
+    def one_hot(index_ref):
+        count = index_ref.shape[0]
+        iota = lax.broadcasted_iota(jnp.int32, (count, local_rows), 1)
+        return jnp.where(index_ref[...] == iota, 1.0, 0.0).astype(jnp.bfloat16), count // dests
+
+    far_hot, far_rows = one_hot(far_index_ref)
+    own_hot, own_rows = one_hot(own_index_ref)
     base = 2 * far_rows
     for index, out_ref in enumerate(out_refs):
         width = out_ref.shape[2]
@@ -215,9 +219,6 @@
     local_rows, channels = query_feats.shape
     width = channels // chunks
     dests = PACK_DESTS if group_size % PACK_DESTS == 0 else 1
-    row_iota = jnp.arange(local_rows, dtype=jnp.int32)
-    far_hot = (far_rows[:, :, None] == row_iota).astype(jnp.bfloat16)
-    own_hot = (own_rows[:, :, None] == row_iota).astype(jnp.bfloat16)
     total = 2 * far_count + 3 * own_count
     source_spec = pl.BlockSpec((local_rows, channels), lambda j: (0, 0))
     out_spec = pl.BlockSpec((dests, total, width), lambda j: (j, 0, 0))
@@ -225,8 +226,8 @@
         pack_kernel,
         grid=(group_size // dests,),
         in_specs=[
-            pl.BlockSpec((dests, far_count, local_rows), lambda j: (j, 0, 0)),
-            pl.BlockSpec((dests, own_count, local_rows), lambda j: (j, 0, 0)),
+            pl.BlockSpec((dests * far_count, 1), lambda j: (j, 0)),
+            pl.BlockSpec((dests * own_count, 1), lambda j: (j, 0)),
             source_spec,
             source_spec,
             source_spec,
@@ -234,7 +235,7 @@
         out_specs=[out_spec] * chunks,
         out_shape=[jax.ShapeDtypeStruct((group_size, total, width), query_feats.dtype)] * chunks,
         interpret=INTERPRET,
-    )(far_hot, own_hot, query_feats, key_feats, value_feats)
+    )(far_rows.reshape(-1, 1), own_rows.reshape(-1, 1), query_feats, key_feats, value_feats)
 
 
 def class_of(devices, frame_devs):

time: 514 us -> 513 us (level)
  transfers between devices with their start and end apart: 3 -> 3, of which waited for: 3 -> 3; matrix products, arithmetic and copies ran while one was open for 4% -> 4% of each run, Pallas kernels for 8% -> 9%
where the time goes in v17:
time: 513 us
  blocking collectives  206 us (40%)
  waiting for transfers between devices  197 us (38%)
  Pallas kernels  59 us (12%)
  other arithmetic  18.8 us (4%)
  local copies, waits for them, and re-layouts  16 us (3%)
  starting transfers between devices  15.7 us (3%)
    all_to_all x1, blocking collectives, shards(): got = lax.all_to_all(sent, 'seq', split_axis=0, concat_axis=0, tiled=True)  206 us
    all_to_all x1, waiting for transfers between devices, shards(): got = lax.all_to_all(sent, 'seq', split_axis=0, concat_axis=0, tiled=True)  168 us
    pallas_call x2, Pallas kernels, attend(): pl.pallas_call(attention_kernel, grid=(heads // per_step,), in_specs=[pl....  43.6 us
    all_to_all x2, waiting for transfers between devices, shards(): lax.all_to_all(mixed, 'seq', split_axis=0, concat_axis=0, tiled=True)  28.8 us
    pallas_call x1, Pallas kernels, pack(): pl.pallas_call(pack_kernel, grid=(group_size // dests,), in_specs=[pl.Blo...  15.4 us
  transfers between devices with their start and end apart: 3, of which 3 were waited for; matrix products, arithmetic and copies ran while one was open for 4% of the time, Pallas kernels for 9%

profile of v17, /device:TPU:13, one launch (start us, length us, event | category | flops | bytes accessed | tf_op | source)
XLA Modules:
  0.0 512.7 jit_solution(2537766147561701634)
XLA Ops:
  0.7 0.7 eq.369
  1.4 0.7 iota_compare_fusion.10
  2.1 0.2 convert_reduce_fusion
  2.3 0.1 reshape.858
  2.4 0.7 dynamic_slice.10
  3.2 0.1 select_reduce_fusion.13
  3.3 0.1 copy.29
  3.4 0.1 copy.30
  3.5 0.1 add_add_fusion.1
  3.6 0.9 add.458.own_index_ref
  4.5 1.8 select_reduce_fusion
  6.3 0.7 broadcast_compare_fusion
  6.9 0.8 select_reduce_fusion.2
  7.7 0.3 select_reduce_fusion.3
  8.1 0.2 reduce_window_sum.28
  8.2 0.1 select_reduce_fusion.11
  8.4 0.1 copy.27
  8.5 0.1 copy.28
  8.6 0.1 add_add_fusion
  8.7 1.1 add.457.far_index_ref
  9.8 15.4 %shard_map.68 = (bf16[16,224,1280]{2,1,0:T(8,128)(2,1)}, bf16[16,224,1280]{2,1,0:T(8,128)(2,1)}) custom-call(s32[1024,1]{1,0:T(8,128)} %add.457.far_index_ref, s32[512,1]{1,0:T(8,128)} %add.458.own_index_ref, bf16[512,2560]{1,0:T(8,128)(2,1)} %query_ref.1, bf16[512,2560]{1,0:T(8,128)(2,1)} %key_ref.1, bf16[512,2560]{1,0:T(8,128)(2,1)} %value_ref.1), custom_call_target="tpu_custom_call" | custom-call | tf_op jit(solution)/shard_map/pallas_call | solution.py:225
  25.2 205.6 %all_to_all.20.far_key_ref.far_value_ref.query_ref.near_key_ref.near_value_ref = bf16[16,224,1280]{2,1,0:T(8,128)(2,1)} all-to-all(bf16[16,224,1280]{2,1,0:T(8,128)(2,1)} %get-tuple-element.8), channel_id=1, replica_groups=mesh['groups'=2,'seq'=16] {'seq'}, dimensions={0} | all-to-all | bytes 18350080 | tf_op jit(solution)/shard_map/all_to_all | solution.py:331
  230.8 5.9 %all-to-all-start.2 = ((bf16[16,224,1280]{2,1,0:T(8,128)(2,1)}), bf16[16,224,1280]{2,1,0:T(8,128)(2,1)}, u32[]{:S(2)}, u32[]{:S(2)}) async-start(bf16[16,224,1280]{2,1,0:T(8,128)(2,1)} %get-tuple-element.10), calls=%async_computation.2 | async-start | bytes 18350080 | tf_op jit(solution)/shard_map/all_to_all | solution.py:331
  236.8 0.1 compare_and_fusion
  236.8 0.2 reduce_window_sum.30
  237.0 0.1 fusion.4
  237.2 0.2 select_reduce_fusion.8
  237.3 0.1 copy.34
  237.5 0.1 eq.409
  237.6 0.1 fusion.1
  237.7 0.2 reduce_window_sum.29
  237.9 0.1 select_reduce_fusion.10
  238.0 0.1 select_reduce_fusion.12
  238.1 0.1 copy.33
  238.3 0.1 eq.395
  238.4 0.2 select_reduce_fusion.7
  238.6 0.2 select_reduce_fusion.1
  238.9 0.1 select_reduce_fusion.15
  239.1 0.5 select_reduce_fusion.4
  239.6 0.2 compare_reduce_fusion
  239.7 1.9 gather_fusion.1
  241.6 0.1 compare_reduce_fusion.1
  241.8 1.8 gather_fusion
  243.5 1.1 broadcast_select_fusion.1.near_bias_ref
  244.7 1.6 broadcast_select_fusion.far_bias_ref
  246.3 21.8 %shard_map.69 = (bf16[16,32,1280]{2,1,0:T(8,128)(2,1)}, f32[10,512,1]{2,1,0:T(8,128)}) custom-call(bf16[16,224,1280]{2,1,0:T(8,128)(2,1)} %all_to_all.20.far_key_ref.far_value_ref.query_ref.near_key_ref.near_value_ref, bf16[16,224,1280]{2,1,0:T(8,128)(2,1)} %all_to_all.20.far_key_ref.far_value_ref.query_ref.near_key_ref.near_value_ref, ...), custom_call_target="tpu_custom_call" | custom-call | tf_op jit(solution)/shard_map/pallas_call | solution.py:160
  268.1 167.8 %all-to-all-done.2.far_key_ref.far_value_ref.query_ref.near_key_ref.near_value_ref = bf16[16,224,1280]{2,1,0:T(8,128)(2,1)} async-done(((bf16[16,224,1280]{2,1,0:T(8,128)(2,1)}), bf16[16,224,1280]{2,1,0:T(8,128)(2,1)}, u32[]{:S(2)}, u32[]{:S(2)}) %all-to-all-start.2) | async-done | bytes 9175072 | tf_op jit(solution)/shard_map/all_to_all | solution.py:331
  435.9 4.9 all-to-all-start.1
  440.8 21.8 %shard_map.70 = (bf16[16,32,1280]{2,1,0:T(8,128)(2,1)}, f32[10,512,1]{2,1,0:T(8,128)}) custom-call(bf16[16,224,1280]{2,1,0:T(8,128)(2,1)} %all-to-all-done.2.far_key_ref.far_value_ref.query_ref.near_key_ref.near_value_ref, bf16[16,224,1280]{2,1,0:T(8,128)(2,1)} %all-to-all-done.2.far_key_ref.far_value_ref.query_ref.near_key_ref.near_value_ref, ...), custom_call_target="tpu_custom_call" | custom-call | tf_op jit(solution)/shard_map/pallas_call | solution.py:160
  462.6 8.7 %all-to-all-done.1 = bf16[16,32,1280]{2,1,0:T(8,128)(2,1)S(1)} async-done(((bf16[16,32,1280]{2,1,0:T(8,128)(2,1)}), bf16[16,32,1280]{2,1,0:T(8,128)(2,1)S(1)}, u32[]{:S(2)}, u32[]{:S(2)}) %all-to-all-start.1) | async-done | bytes 1310752 | tf_op jit(solution)/shard_map/all_to_all | solution.py:333
  471.4 4.9 all-to-all-start.3
  476.2 0.2 select_reduce_fusion.14
  476.6 0.1 reshape.897
  476.7 0.1 select_reduce_fusion.6
  476.9 2.5 reduce
  479.3 2.5 reduce.1
  481.9 0.1 copy.35
  482.0 1.0 gather_fusion.4
  483.0 0.1 copy.36
  483.2 0.7 reshape.862
  483.9 2.9 gather_fusion.2
  486.8 20.0 %all-to-all-done.3 = bf16[16,32,1280]{2,1,0:T(8,128)(2,1)S(1)} async-done(((bf16[16,32,1280]{2,1,0:T(8,128)(2,1)}), bf16[16,32,1280]{2,1,0:T(8,128)(2,1)S(1)}, u32[]{:S(2)}, u32[]{:S(2)}) %all-to-all-start.3) | async-done | bytes 1310752 | tf_op jit(solution)/shard_map/all_to_all | solution.py:333
  506.8 2.9 gather_fusion.3
  509.7 3.0 pad_maximum_fusion
  (39 shorter events, 0.8 us)
Async XLA Ops:
  230.8 6.8 %copy-start.2 = (s32[128]{0:T(128)S(1)}, s32[128]{0:T(128)}, u32[]{:S(2)}) copy-start(s32[128]{0:T(128)} %param.8) | copy-start | bytes 1540
  230.8 8.3 %copy-start.1 = (s32[128,23]{0,1:T(8,128)S(1)}, s32[128,23]{0,1:T(8,128)}, u32[]{:S(2)}) copy-start(s32[128,23]{0,1:T(8,128)} %param.9) | copy-start | bytes 35332
  230.8 205.1 %all-to-all-start.2 = ((bf16[16,224,1280]{2,1,0:T(8,128)(2,1)}), bf16[16,224,1280]{2,1,0:T(8,128)(2,1)}, u32[]{:S(2)}, u32[]{:S(2)}) async-start(bf16[16,224,1280]{2,1,0:T(8,128)(2,1)} %get-tuple-element.10), calls=%async_computation.2 | async-start | bytes 18350080 | tf_op jit(solution)/shard_map/all_to_all | solution.py:331
  435.9 35.5 %all-to-all-start.1 = ((bf16[16,32,1280]{2,1,0:T(8,128)(2,1)}), bf16[16,32,1280]{2,1,0:T(8,128)(2,1)S(1)}, u32[]{:S(2)}, u32[]{:S(2)}) async-start(bf16[16,32,1280]{2,1,0:T(8,128)(2,1)} %get-tuple-element.9), calls=%async_computation.1 | async-start | bytes 2621440 | tf_op jit(solution)/shard_map/all_to_all | solution.py:333
  471.4 35.4 %all-to-all-start.3 = ((bf16[16,32,1280]{2,1,0:T(8,128)(2,1)}), bf16[16,32,1280]{2,1,0:T(8,128)(2,1)S(1)}, u32[]{:S(2)}, u32[]{:S(2)}) async-start(bf16[16,32,1280]{2,1,0:T(8,128)(2,1)} %get-tuple-element.11), calls=%async_computation.3 | async-start | bytes 2621440 | tf_op jit(solution)/shard_map/all_to_all | solution.py:333
  506.8 2.9 copy-start

commit v18 on v17

--- a/solution.py
+++ b/solution.py
@@ -238,6 +238,32 @@
     )(far_rows.reshape(-1, 1), own_rows.reshape(-1, 1), query_feats, key_feats, value_feats)
 
 
+def unpack_kernel(index_ref, part_ref, prior_ref, out_ref):
+    del prior_ref
+    count, rows = index_ref.shape[0], part_ref.shape[0]
+    iota = lax.broadcasted_iota(jnp.int32, (count, rows), 1)
+    hot = jnp.where(index_ref[...] == iota, 1.0, 0.0).astype(jnp.bfloat16)
+    picked = jnp.dot(hot, part_ref[...], preferred_element_type=jnp.float32)
+    out_ref[...] = picked.astype(out_ref.dtype)
+
+
+def unpack(index, part, prior, column_block):
+    rows, width = part.shape
+    return pl.pallas_call(
+        unpack_kernel,
+        grid=(1,),
+        in_specs=[
+            pl.BlockSpec((rows, 1), lambda i: (0, 0)),
+            pl.BlockSpec((rows, width), lambda i: (0, 0)),
+            pl.BlockSpec((rows, width), lambda i: (0, column_block)),
+        ],
+        out_specs=pl.BlockSpec((rows, width), lambda i: (0, column_block)),
+        out_shape=jax.ShapeDtypeStruct(prior.shape, prior.dtype),
+        input_output_aliases={2: 0},
+        interpret=INTERPRET,
+    )(index.reshape(-1, 1), part, prior)
+
+
 def class_of(devices, frame_devs):
     return devices // frame_devs // 4 * frame_devs + devices % frame_devs
 
@@ -355,9 +381,9 @@
     piece = strip * blocks + column // 4
     token = height * 4 + column % 4
     back_rows = (pick(my_owner, piece) * capacity + pick(my_slot, piece)) * 16 + token
-    attended = jnp.concatenate(
-        [jnp.take(part, back_rows, axis=0, mode="clip") for part in outputs], axis=1
-    )
+    attended = jnp.zeros((local_rows, channels), jnp.bfloat16)
+    for chunk, part in enumerate(outputs):
+        attended = unpack(back_rows, part, attended, chunk)
     return (attended, log_sums)
 
 

time: 513 us -> 512 us (level)
  Pallas kernels: 59 us -> 66.5 us
    pallas_call x0 -> x2, Pallas kernels: none -> 7.47 us  [unpack(): pl.pallas_call(unpack_kernel, grid=(1,), in_specs=[pl.BlockSpec((rows, 1)...]
    gather x2 -> x0, local copies, waits for them, and re-layouts: 5.74 us -> none  [shards(): jnp.take(part, back_rows, axis=0, mode='clip')]
where the time goes in v18:
time: 512 us
  blocking collectives  206 us (40%)
  waiting for transfers between devices  193 us (38%)
  Pallas kernels  66.5 us (13%)
  other arithmetic  16.6 us (3%)
  starting transfers between devices  15.7 us (3%)
  local copies, waits for them, and re-layouts  13.2 us (3%)
    all_to_all x1, blocking collectives, shards(): got = lax.all_to_all(sent, 'seq', split_axis=0, concat_axis=0, tiled=True)  206 us
    all_to_all x1, waiting for transfers between devices, shards(): got = lax.all_to_all(sent, 'seq', split_axis=0, concat_axis=0, tiled=True)  168 us
    pallas_call x2, Pallas kernels, attend(): pl.pallas_call(attention_kernel, grid=(heads // per_step,), in_specs=[pl....  43.6 us
    all_to_all x2, waiting for transfers between devices, shards(): lax.all_to_all(mixed, 'seq', split_axis=0, concat_axis=0, tiled=True)  25.3 us
    pallas_call x1, Pallas kernels, pack(): pl.pallas_call(pack_kernel, grid=(group_size // dests,), in_specs=[pl.Blo...  15.4 us
  transfers between devices with their start and end apart: 3, of which 3 were waited for; matrix products, arithmetic and copies ran while one was open for 4% of the time, Pallas kernels for 9%

profile of v18, /device:TPU:13, one launch (start us, length us, event | category | flops | bytes accessed | tf_op | source)
XLA Modules:
  0.0 511.6 jit_solution(15555929861626853716)
XLA Ops:
  0.6 0.7 iota_compare_fusion.10
  1.3 0.7 eq.355
  2.1 1.8 select_reduce_fusion
  3.8 0.7 broadcast_compare_fusion
  4.5 0.8 select_reduce_fusion.2
  5.3 0.3 select_reduce_fusion.3
  5.7 0.2 reduce_window_sum.28
  5.8 0.1 select_reduce_fusion.11
  6.0 0.1 copy.32
  6.1 0.1 copy.33
  6.2 0.1 add_add_fusion
  6.3 1.1 add.457.far_index_ref
  7.4 0.2 convert_reduce_fusion
  7.6 0.1 reshape.860
  7.7 0.7 dynamic_slice.10
  8.5 0.1 select_reduce_fusion.13
  8.7 0.1 copy.34
  8.8 0.1 add_add_fusion.1
  8.9 0.9 add.458.own_index_ref
  9.8 15.4 %shard_map.68 = (bf16[16,224,1280]{2,1,0:T(8,128)(2,1)}, bf16[16,224,1280]{2,1,0:T(8,128)(2,1)}) custom-call(s32[1024,1]{1,0:T(8,128)} %add.457.far_index_ref, s32[512,1]{1,0:T(8,128)} %add.458.own_index_ref, bf16[512,2560]{1,0:T(8,128)(2,1)} %query_ref.1, bf16[512,2560]{1,0:T(8,128)(2,1)} %key_ref.1, bf16[512,2560]{1,0:T(8,128)(2,1)} %value_ref.1), custom_call_target="tpu_custom_call" | custom-call | tf_op jit(solution)/shard_map/pallas_call | solution.py:225
  25.2 205.6 %all_to_all.20.far_key_ref.far_value_ref.query_ref.near_key_ref.near_value_ref = bf16[16,224,1280]{2,1,0:T(8,128)(2,1)} all-to-all(bf16[16,224,1280]{2,1,0:T(8,128)(2,1)} %get-tuple-element.10), channel_id=1, replica_groups=mesh['groups'=2,'seq'=16] {'seq'}, dimensions={0} | all-to-all | bytes 18350080 | tf_op jit(solution)/shard_map/all_to_all | solution.py:357
  230.8 5.9 %all-to-all-start = ((bf16[16,224,1280]{2,1,0:T(8,128)(2,1)}), bf16[16,224,1280]{2,1,0:T(8,128)(2,1)}, u32[]{:S(2)}, u32[]{:S(2)}) async-start(bf16[16,224,1280]{2,1,0:T(8,128)(2,1)} %get-tuple-element.8), calls=%async_computation | async-start | bytes 18350080 | tf_op jit(solution)/shard_map/all_to_all | solution.py:357
  236.9 0.2 reduce_window_sum.30
  237.0 0.1 fusion.17
  237.2 0.2 select_reduce_fusion.8
  237.3 0.1 copy.39
  237.5 0.1 eq.412
  237.6 0.1 fusion.14
  237.7 0.2 reduce_window_sum.29
  238.1 0.1 select_reduce_fusion.12
  238.2 0.1 copy.38
  238.3 0.1 eq.398
  238.4 0.2 select_reduce_fusion.5
  238.6 0.2 select_reduce_fusion.1
  238.9 0.1 select_reduce_fusion.15
  239.1 0.5 select_reduce_fusion.4
  239.6 0.2 compare_reduce_fusion
  239.8 1.9 gather_fusion.1
  241.7 0.1 compare_reduce_fusion.1
  241.8 1.8 gather_fusion
  243.6 1.1 broadcast_select_fusion.1.near_bias_ref
  244.7 1.6 broadcast_select_fusion.far_bias_ref
  246.3 21.8 %shard_map.70 = (bf16[16,32,1280]{2,1,0:T(8,128)(2,1)}, f32[10,512,1]{2,1,0:T(8,128)}) custom-call(bf16[16,224,1280]{2,1,0:T(8,128)(2,1)} %all_to_all.20.far_key_ref.far_value_ref.query_ref.near_key_ref.near_value_ref, bf16[16,224,1280]{2,1,0:T(8,128)(2,1)} %all_to_all.20.far_key_ref.far_value_ref.query_ref.near_key_ref.near_value_ref, ...), custom_call_target="tpu_custom_call" | custom-call | tf_op jit(solution)/shard_map/pallas_call | solution.py:160
  268.1 167.8 %all-to-all-done.far_key_ref.far_value_ref.query_ref.near_key_ref.near_value_ref = bf16[16,224,1280]{2,1,0:T(8,128)(2,1)} async-done(((bf16[16,224,1280]{2,1,0:T(8,128)(2,1)}), bf16[16,224,1280]{2,1,0:T(8,128)(2,1)}, u32[]{:S(2)}, u32[]{:S(2)}) %all-to-all-start) | async-done | bytes 9175072 | tf_op jit(solution)/shard_map/all_to_all | solution.py:357
  435.9 4.9 all-to-all-start.3
  440.8 21.8 %shard_map.69 = (bf16[16,32,1280]{2,1,0:T(8,128)(2,1)}, f32[10,512,1]{2,1,0:T(8,128)}) custom-call(bf16[16,224,1280]{2,1,0:T(8,128)(2,1)} %all-to-all-done.far_key_ref.far_value_ref.query_ref.near_key_ref.near_value_ref, bf16[16,224,1280]{2,1,0:T(8,128)(2,1)} %all-to-all-done.far_key_ref.far_value_ref.query_ref.near_key_ref.near_value_ref, ...), custom_call_target="tpu_custom_call" | custom-call | tf_op jit(solution)/shard_map/pallas_call | solution.py:160
  462.7 8.7 %all-to-all-done.3 = bf16[16,32,1280]{2,1,0:T(8,128)(2,1)S(1)} async-done(((bf16[16,32,1280]{2,1,0:T(8,128)(2,1)}), bf16[16,32,1280]{2,1,0:T(8,128)(2,1)S(1)}, u32[]{:S(2)}, u32[]{:S(2)}) %all-to-all-start.3) | async-done | bytes 1310752 | tf_op jit(solution)/shard_map/all_to_all | solution.py:359
  471.4 4.9 all-to-all-start.1
  476.3 0.2 select_reduce_fusion.14
  476.6 0.1 reshape.883
  476.7 0.1 select_reduce_fusion.7
  476.8 0.1 copy.31
  477.0 0.8 fusion.3.index_ref
  477.8 2.5 reduce
  480.3 2.5 reduce.1
  482.8 0.1 copy.40
  482.9 1.0 gather_fusion.2
  484.0 0.1 copy.41
  484.1 0.7 reshape.864
  484.8 1.7 broadcast_in_dim.309.prior_ref
  486.5 3.7 shard_map.71.prior_ref
  490.2 16.6 %all-to-all-done.1 = bf16[16,32,1280]{2,1,0:T(8,128)(2,1)S(1)} async-done(((bf16[16,32,1280]{2,1,0:T(8,128)(2,1)}), bf16[16,32,1280]{2,1,0:T(8,128)(2,1)S(1)}, u32[]{:S(2)}, u32[]{:S(2)}) %all-to-all-start.1) | async-done | bytes 1310752 | tf_op jit(solution)/shard_map/all_to_all | solution.py:359
  506.8 1.1 copy-done.1
  507.9 3.7 shard_map.72
  (41 shorter events, 1.0 us)
Async XLA Ops:
  230.8 6.8 %copy-start.3 = (s32[128]{0:T(128)S(1)}, s32[128]{0:T(128)}, u32[]{:S(2)}) copy-start(s32[128]{0:T(128)} %param.8) | copy-start | bytes 1540
  230.8 8.3 %copy-start.2 = (s32[128,23]{0,1:T(8,128)S(1)}, s32[128,23]{0,1:T(8,128)}, u32[]{:S(2)}) copy-start(s32[128,23]{0,1:T(8,128)} %param.9) | copy-start | bytes 35332
  230.8 205.1 %all-to-all-start = ((bf16[16,224,1280]{2,1,0:T(8,128)(2,1)}), bf16[16,224,1280]{2,1,0:T(8,128)(2,1)}, u32[]{:S(2)}, u32[]{:S(2)}) async-start(bf16[16,224,1280]{2,1,0:T(8,128)(2,1)} %get-tuple-element.8), calls=%async_computation | async-start | bytes 18350080 | tf_op jit(solution)/shard_map/all_to_all | solution.py:357
  435.9 35.5 %all-to-all-start.3 = ((bf16[16,32,1280]{2,1,0:T(8,128)(2,1)}), bf16[16,32,1280]{2,1,0:T(8,128)(2,1)S(1)}, u32[]{:S(2)}, u32[]{:S(2)}) async-start(bf16[16,32,1280]{2,1,0:T(8,128)(2,1)} %get-tuple-element.11), calls=%async_computation.3 | async-start | bytes 2621440 | tf_op jit(solution)/shard_map/all_to_all | solution.py:359
  471.4 8.9 %copy-start = (bf16[16,32,1280]{2,1,0:T(8,128)(2,1)}, bf16[16,32,1280]{2,1,0:T(8,128)(2,1)S(1)}, u32[]{:S(2)}) copy-start(bf16[16,32,1280]{2,1,0:T(8,128)(2,1)S(1)} %all-to-all-done.3) | copy-start | bytes 3932164
  471.4 35.4 %all-to-all-start.1 = ((bf16[16,32,1280]{2,1,0:T(8,128)(2,1)}), bf16[16,32,1280]{2,1,0:T(8,128)(2,1)S(1)}, u32[]{:S(2)}, u32[]{:S(2)}) async-start(bf16[16,32,1280]{2,1,0:T(8,128)(2,1)} %get-tuple-element.9), calls=%async_computation.1 | async-start | bytes 2621440 | tf_op jit(solution)/shard_map/all_to_all | solution.py:359
  506.8 1.1 copy-start.1

commit v19 on v18

--- a/solution.py
+++ b/solution.py
@@ -181,7 +181,7 @@
     )(got, got, got, got, got, near_bias, far_bias)
 
 
-PACK_DESTS = 4
+PACK_DESTS = 8
 
 
 def pack_kernel(far_index_ref, own_index_ref, query_ref, key_ref, value_ref, *out_refs):

time: 512 us -> 513 us (level)
  no operation moved by 1% of the time
where the time goes in v19:
time: 513 us; the launch traced here: 512 us
  blocking collectives  206 us (40%)
  waiting for transfers between devices  193 us (38%)
  Pallas kernels  66.7 us (13%)
  other arithmetic  16.6 us (3%)
  starting transfers between devices  15.7 us (3%)
  local copies, waits for them, and re-layouts  13.2 us (3%)
    all_to_all x1, blocking collectives, shards(): got = lax.all_to_all(sent, 'seq', split_axis=0, concat_axis=0, tiled=True)  206 us
    all_to_all x1, waiting for transfers between devices, shards(): got = lax.all_to_all(sent, 'seq', split_axis=0, concat_axis=0, tiled=True)  168 us
    pallas_call x2, Pallas kernels, attend(): pl.pallas_call(attention_kernel, grid=(heads // per_step,), in_specs=[pl....  43.6 us
    all_to_all x2, waiting for transfers between devices, shards(): lax.all_to_all(mixed, 'seq', split_axis=0, concat_axis=0, tiled=True)  25.4 us
    pallas_call x1, Pallas kernels, pack(): pl.pallas_call(pack_kernel, grid=(group_size // dests,), in_specs=[pl.Blo...  15.7 us
  transfers between devices with their start and end apart: 3, of which 3 were waited for; matrix products, arithmetic and copies ran while one was open for 4% of the time, Pallas kernels for 9%

profile of v19, /device:TPU:13, one launch (start us, length us, event | category | flops | bytes accessed | tf_op | source)
XLA Modules:
  0.0 511.9 jit_solution(5147636125451018420)
XLA Ops:
  0.6 0.7 iota_compare_fusion.10
  1.3 0.7 eq.355
  2.1 1.8 select_reduce_fusion
  3.8 0.7 broadcast_compare_fusion
  4.5 0.8 select_reduce_fusion.2
  5.3 0.3 select_reduce_fusion.3
  5.7 0.2 reduce_window_sum.28
  5.8 0.1 select_reduce_fusion.11
  6.0 0.1 copy.32
  6.1 0.1 copy.33
  6.2 0.1 add_add_fusion
  6.3 1.1 add.457.far_index_ref
  7.4 0.2 convert_reduce_fusion
  7.6 0.1 reshape.860
  7.7 0.7 dynamic_slice.10
  8.5 0.1 select_reduce_fusion.13
  8.7 0.1 copy.34
  8.8 0.1 add_add_fusion.1
  8.9 0.9 add.458.own_index_ref
  9.8 15.7 %shard_map.68 = (bf16[16,224,1280]{2,1,0:T(8,128)(2,1)}, bf16[16,224,1280]{2,1,0:T(8,128)(2,1)}) custom-call(s32[1024,1]{1,0:T(8,128)} %add.457.far_index_ref, s32[512,1]{1,0:T(8,128)} %add.458.own_index_ref, bf16[512,2560]{1,0:T(8,128)(2,1)} %query_ref.1, bf16[512,2560]{1,0:T(8,128)(2,1)} %key_ref.1, bf16[512,2560]{1,0:T(8,128)(2,1)} %value_ref.1), custom_call_target="tpu_custom_call" | custom-call | tf_op jit(solution)/shard_map/pallas_call | solution.py:225
  25.5 205.6 %all_to_all.20.far_key_ref.far_value_ref.query_ref.near_key_ref.near_value_ref = bf16[16,224,1280]{2,1,0:T(8,128)(2,1)} all-to-all(bf16[16,224,1280]{2,1,0:T(8,128)(2,1)} %get-tuple-element.10), channel_id=1, replica_groups=mesh['groups'=2,'seq'=16] {'seq'}, dimensions={0} | all-to-all | bytes 18350080 | tf_op jit(solution)/shard_map/all_to_all | solution.py:357
  231.1 5.9 %all-to-all-start = ((bf16[16,224,1280]{2,1,0:T(8,128)(2,1)}), bf16[16,224,1280]{2,1,0:T(8,128)(2,1)}, u32[]{:S(2)}, u32[]{:S(2)}) async-start(bf16[16,224,1280]{2,1,0:T(8,128)(2,1)} %get-tuple-element.8), calls=%async_computation | async-start | bytes 18350080 | tf_op jit(solution)/shard_map/all_to_all | solution.py:357
  237.2 0.2 reduce_window_sum.30
  237.3 0.1 fusion.17
  237.5 0.2 select_reduce_fusion.8
  237.6 0.1 copy.39
  237.8 0.1 eq.412
  237.9 0.1 fusion.14
  238.0 0.2 reduce_window_sum.29
  238.4 0.1 select_reduce_fusion.12
  238.5 0.1 copy.38
  238.6 0.1 eq.398
  238.7 0.2 select_reduce_fusion.5
  238.9 0.2 select_reduce_fusion.1
  239.2 0.1 select_reduce_fusion.15
  239.4 0.5 select_reduce_fusion.4
  239.9 0.2 compare_reduce_fusion
  240.1 1.9 gather_fusion.1
  242.0 0.1 compare_reduce_fusion.1
  242.1 1.8 gather_fusion
  243.9 1.1 broadcast_select_fusion.1.near_bias_ref
  245.0 1.6 broadcast_select_fusion.far_bias_ref
  246.6 21.8 %shard_map.70 = (bf16[16,32,1280]{2,1,0:T(8,128)(2,1)}, f32[10,512,1]{2,1,0:T(8,128)}) custom-call(bf16[16,224,1280]{2,1,0:T(8,128)(2,1)} %all_to_all.20.far_key_ref.far_value_ref.query_ref.near_key_ref.near_value_ref, bf16[16,224,1280]{2,1,0:T(8,128)(2,1)} %all_to_all.20.far_key_ref.far_value_ref.query_ref.near_key_ref.near_value_ref, ...), custom_call_target="tpu_custom_call" | custom-call | tf_op jit(solution)/shard_map/pallas_call | solution.py:160
  268.4 167.8 %all-to-all-done.far_key_ref.far_value_ref.query_ref.near_key_ref.near_value_ref = bf16[16,224,1280]{2,1,0:T(8,128)(2,1)} async-done(((bf16[16,224,1280]{2,1,0:T(8,128)(2,1)}), bf16[16,224,1280]{2,1,0:T(8,128)(2,1)}, u32[]{:S(2)}, u32[]{:S(2)}) %all-to-all-start) | async-done | bytes 9175072 | tf_op jit(solution)/shard_map/all_to_all | solution.py:357
  436.2 4.9 all-to-all-start.3
  441.1 21.8 %shard_map.69 = (bf16[16,32,1280]{2,1,0:T(8,128)(2,1)}, f32[10,512,1]{2,1,0:T(8,128)}) custom-call(bf16[16,224,1280]{2,1,0:T(8,128)(2,1)} %all-to-all-done.far_key_ref.far_value_ref.query_ref.near_key_ref.near_value_ref, bf16[16,224,1280]{2,1,0:T(8,128)(2,1)} %all-to-all-done.far_key_ref.far_value_ref.query_ref.near_key_ref.near_value_ref, ...), custom_call_target="tpu_custom_call" | custom-call | tf_op jit(solution)/shard_map/pallas_call | solution.py:160
  463.0 8.7 %all-to-all-done.3 = bf16[16,32,1280]{2,1,0:T(8,128)(2,1)S(1)} async-done(((bf16[16,32,1280]{2,1,0:T(8,128)(2,1)}), bf16[16,32,1280]{2,1,0:T(8,128)(2,1)S(1)}, u32[]{:S(2)}, u32[]{:S(2)}) %all-to-all-start.3) | async-done | bytes 1310752 | tf_op jit(solution)/shard_map/all_to_all | solution.py:359
  471.7 4.9 all-to-all-start.1
  476.6 0.2 select_reduce_fusion.14
  476.9 0.1 reshape.883
  477.0 0.1 select_reduce_fusion.7
  477.1 0.1 copy.31
  477.3 0.8 fusion.3.index_ref
  478.1 2.5 reduce
  480.6 2.5 reduce.1
  483.1 0.1 copy.40
  483.2 1.0 gather_fusion.2
  484.3 0.1 copy.41
  484.4 0.7 reshape.864
  485.1 1.7 broadcast_in_dim.309.prior_ref
  486.8 3.7 shard_map.71.prior_ref
  490.5 16.6 %all-to-all-done.1 = bf16[16,32,1280]{2,1,0:T(8,128)(2,1)S(1)} async-done(((bf16[16,32,1280]{2,1,0:T(8,128)(2,1)}), bf16[16,32,1280]{2,1,0:T(8,128)(2,1)S(1)}, u32[]{:S(2)}, u32[]{:S(2)}) %all-to-all-start.1) | async-done | bytes 1310752 | tf_op jit(solution)/shard_map/all_to_all | solution.py:359
  507.1 1.1 copy-done.1
  508.2 3.7 shard_map.72
  (41 shorter events, 1.0 us)
Async XLA Ops:
  231.1 6.8 %copy-start.3 = (s32[128]{0:T(128)S(1)}, s32[128]{0:T(128)}, u32[]{:S(2)}) copy-start(s32[128]{0:T(128)} %param.8) | copy-start | bytes 1540
  231.1 8.3 %copy-start.2 = (s32[128,23]{0,1:T(8,128)S(1)}, s32[128,23]{0,1:T(8,128)}, u32[]{:S(2)}) copy-start(s32[128,23]{0,1:T(8,128)} %param.9) | copy-start | bytes 35332
  231.1 205.1 %all-to-all-start = ((bf16[16,224,1280]{2,1,0:T(8,128)(2,1)}), bf16[16,224,1280]{2,1,0:T(8,128)(2,1)}, u32[]{:S(2)}, u32[]{:S(2)}) async-start(bf16[16,224,1280]{2,1,0:T(8,128)(2,1)} %get-tuple-element.8), calls=%async_computation | async-start | bytes 18350080 | tf_op jit(solution)/shard_map/all_to_all | solution.py:357
  436.2 35.5 %all-to-all-start.3 = ((bf16[16,32,1280]{2,1,0:T(8,128)(2,1)}), bf16[16,32,1280]{2,1,0:T(8,128)(2,1)S(1)}, u32[]{:S(2)}, u32[]{:S(2)}) async-start(bf16[16,32,1280]{2,1,0:T(8,128)(2,1)} %get-tuple-element.11), calls=%async_computation.3 | async-start | bytes 2621440 | tf_op jit(solution)/shard_map/all_to_all | solution.py:359
  471.7 8.9 %copy-start = (bf16[16,32,1280]{2,1,0:T(8,128)(2,1)}, bf16[16,32,1280]{2,1,0:T(8,128)(2,1)S(1)}, u32[]{:S(2)}) copy-start(bf16[16,32,1280]{2,1,0:T(8,128)(2,1)S(1)} %all-to-all-done.3) | copy-start | bytes 3932164
  471.7 35.4 %all-to-all-start.1 = ((bf16[16,32,1280]{2,1,0:T(8,128)(2,1)}), bf16[16,32,1280]{2,1,0:T(8,128)(2,1)S(1)}, u32[]{:S(2)}, u32[]{:S(2)}) async-start(bf16[16,32,1280]{2,1,0:T(8,128)(2,1)} %get-tuple-element.9), calls=%async_computation.1 | async-start | bytes 2621440 | tf_op jit(solution)/shard_map/all_to_all | solution.py:359
  507.1 1.1 copy-start.1

commit v20 on v19

--- a/solution.py
+++ b/solution.py
@@ -181,7 +181,7 @@
     )(got, got, got, got, got, near_bias, far_bias)
 
 
-PACK_DESTS = 8
+PACK_DESTS = 2
 
 
 def pack_kernel(far_index_ref, own_index_ref, query_ref, key_ref, value_ref, *out_refs):

time: 513 us -> 520 us (1.014)
  Pallas kernels: 66.7 us -> 73.7 us
    pallas_call x1, Pallas kernels: 15.7 us -> 22.6 us  [pack(): pl.pallas_call(pack_kernel, grid=(group_size // dests,), in_specs=[pl.Blo...]
where the time goes in v20:
time: 520 us; the launch traced here: 519 us
  blocking collectives  206 us (40%)
  waiting for transfers between devices  193 us (37%)
  Pallas kernels  73.7 us (14%)
  other arithmetic  16.6 us (3%)
  starting transfers between devices  15.7 us (3%)
  local copies, waits for them, and re-layouts  13.2 us (3%)
    all_to_all x1, blocking collectives, shards(): got = lax.all_to_all(sent, 'seq', split_axis=0, concat_axis=0, tiled=True)  206 us
    all_to_all x1, waiting for transfers between devices, shards(): got = lax.all_to_all(sent, 'seq', split_axis=0, concat_axis=0, tiled=True)  168 us
    pallas_call x2, Pallas kernels, attend(): pl.pallas_call(attention_kernel, grid=(heads // per_step,), in_specs=[pl....  43.6 us
    all_to_all x2, waiting for transfers between devices, shards(): lax.all_to_all(mixed, 'seq', split_axis=0, concat_axis=0, tiled=True)  25.3 us
    pallas_call x1, Pallas kernels, pack(): pl.pallas_call(pack_kernel, grid=(group_size // dests,), in_specs=[pl.Blo...  22.6 us
  transfers between devices with their start and end apart: 3, of which 3 were waited for; matrix products, arithmetic and copies ran while one was open for 4% of the time, Pallas kernels for 9%

profile of v20, /device:TPU:13, one launch (start us, length us, event | category | flops | bytes accessed | tf_op | source)
XLA Modules:
  0.0 518.9 jit_solution(14255270007959441459)
XLA Ops:
  0.6 0.7 iota_compare_fusion.10
  1.3 0.7 eq.355
  2.1 1.8 select_reduce_fusion
  3.8 0.7 broadcast_compare_fusion
  4.5 0.8 select_reduce_fusion.2
  5.3 0.3 select_reduce_fusion.3
  5.7 0.2 reduce_window_sum.28
  5.8 0.1 select_reduce_fusion.11
  6.0 0.1 copy.32
  6.1 0.1 copy.33
  6.2 0.1 add_add_fusion
  6.3 1.1 add.457.far_index_ref
  7.4 0.2 convert_reduce_fusion
  7.6 0.1 reshape.860
  7.7 0.7 dynamic_slice.10
  8.5 0.1 select_reduce_fusion.13
  8.7 0.1 copy.34
  8.8 0.1 add_add_fusion.1
  8.9 0.9 add.458.own_index_ref
  9.8 22.6 %shard_map.68 = (bf16[16,224,1280]{2,1,0:T(8,128)(2,1)}, bf16[16,224,1280]{2,1,0:T(8,128)(2,1)}) custom-call(s32[1024,1]{1,0:T(8,128)} %add.457.far_index_ref, s32[512,1]{1,0:T(8,128)} %add.458.own_index_ref, bf16[512,2560]{1,0:T(8,128)(2,1)} %query_ref.1, bf16[512,2560]{1,0:T(8,128)(2,1)} %key_ref.1, bf16[512,2560]{1,0:T(8,128)(2,1)} %value_ref.1), custom_call_target="tpu_custom_call" | custom-call | tf_op jit(solution)/shard_map/pallas_call | solution.py:225
  32.4 205.6 %all_to_all.20.far_key_ref.far_value_ref.query_ref.near_key_ref.near_value_ref = bf16[16,224,1280]{2,1,0:T(8,128)(2,1)} all-to-all(bf16[16,224,1280]{2,1,0:T(8,128)(2,1)} %get-tuple-element.10), channel_id=1, replica_groups=mesh['groups'=2,'seq'=16] {'seq'}, dimensions={0} | all-to-all | bytes 18350080 | tf_op jit(solution)/shard_map/all_to_all | solution.py:357
  238.1 5.9 %all-to-all-start = ((bf16[16,224,1280]{2,1,0:T(8,128)(2,1)}), bf16[16,224,1280]{2,1,0:T(8,128)(2,1)}, u32[]{:S(2)}, u32[]{:S(2)}) async-start(bf16[16,224,1280]{2,1,0:T(8,128)(2,1)} %get-tuple-element.8), calls=%async_computation | async-start | bytes 18350080 | tf_op jit(solution)/shard_map/all_to_all | solution.py:357
  244.1 0.2 reduce_window_sum.30
  244.3 0.1 fusion.17
  244.4 0.2 select_reduce_fusion.8
  244.6 0.1 copy.39
  244.7 0.1 eq.412
  244.8 0.1 fusion.14
  244.9 0.2 reduce_window_sum.29
  245.3 0.1 select_reduce_fusion.12
  245.4 0.1 copy.38
  245.6 0.1 eq.398
  245.7 0.2 select_reduce_fusion.5
  245.9 0.2 select_reduce_fusion.1
  246.1 0.1 select_reduce_fusion.15
  246.3 0.5 select_reduce_fusion.4
  246.8 0.2 compare_reduce_fusion
  247.0 1.9 gather_fusion.1
  248.9 0.1 compare_reduce_fusion.1
  249.0 1.8 gather_fusion
  250.8 1.1 broadcast_select_fusion.1.near_bias_ref
  251.9 1.6 broadcast_select_fusion.far_bias_ref
  253.5 21.8 %shard_map.70 = (bf16[16,32,1280]{2,1,0:T(8,128)(2,1)}, f32[10,512,1]{2,1,0:T(8,128)}) custom-call(bf16[16,224,1280]{2,1,0:T(8,128)(2,1)} %all_to_all.20.far_key_ref.far_value_ref.query_ref.near_key_ref.near_value_ref, bf16[16,224,1280]{2,1,0:T(8,128)(2,1)} %all_to_all.20.far_key_ref.far_value_ref.query_ref.near_key_ref.near_value_ref, ...), custom_call_target="tpu_custom_call" | custom-call | tf_op jit(solution)/shard_map/pallas_call | solution.py:160
  275.3 167.8 %all-to-all-done.far_key_ref.far_value_ref.query_ref.near_key_ref.near_value_ref = bf16[16,224,1280]{2,1,0:T(8,128)(2,1)} async-done(((bf16[16,224,1280]{2,1,0:T(8,128)(2,1)}), bf16[16,224,1280]{2,1,0:T(8,128)(2,1)}, u32[]{:S(2)}, u32[]{:S(2)}) %all-to-all-start) | async-done | bytes 9175072 | tf_op jit(solution)/shard_map/all_to_all | solution.py:357
  443.2 4.9 all-to-all-start.3
  448.1 21.8 %shard_map.69 = (bf16[16,32,1280]{2,1,0:T(8,128)(2,1)}, f32[10,512,1]{2,1,0:T(8,128)}) custom-call(bf16[16,224,1280]{2,1,0:T(8,128)(2,1)} %all-to-all-done.far_key_ref.far_value_ref.query_ref.near_key_ref.near_value_ref, bf16[16,224,1280]{2,1,0:T(8,128)(2,1)} %all-to-all-done.far_key_ref.far_value_ref.query_ref.near_key_ref.near_value_ref, ...), custom_call_target="tpu_custom_call" | custom-call | tf_op jit(solution)/shard_map/pallas_call | solution.py:160
  469.9 8.7 %all-to-all-done.3 = bf16[16,32,1280]{2,1,0:T(8,128)(2,1)S(1)} async-done(((bf16[16,32,1280]{2,1,0:T(8,128)(2,1)}), bf16[16,32,1280]{2,1,0:T(8,128)(2,1)S(1)}, u32[]{:S(2)}, u32[]{:S(2)}) %all-to-all-start.3) | async-done | bytes 1310752 | tf_op jit(solution)/shard_map/all_to_all | solution.py:359
  478.6 4.9 all-to-all-start.1
  483.5 0.2 select_reduce_fusion.14
  483.9 0.1 reshape.883
  484.0 0.1 select_reduce_fusion.7
  484.1 0.1 copy.31
  484.2 0.8 fusion.3.index_ref
  485.0 2.5 reduce
  487.5 2.5 reduce.1
  490.0 0.1 copy.40
  490.2 1.0 gather_fusion.2
  491.2 0.1 copy.41
  491.4 0.7 reshape.864
  492.1 1.7 broadcast_in_dim.309.prior_ref
  493.7 3.7 shard_map.71.prior_ref
  497.5 16.6 %all-to-all-done.1 = bf16[16,32,1280]{2,1,0:T(8,128)(2,1)S(1)} async-done(((bf16[16,32,1280]{2,1,0:T(8,128)(2,1)}), bf16[16,32,1280]{2,1,0:T(8,128)(2,1)S(1)}, u32[]{:S(2)}, u32[]{:S(2)}) %all-to-all-start.1) | async-done | bytes 1310752 | tf_op jit(solution)/shard_map/all_to_all | solution.py:359
  514.1 1.1 copy-done.1
  515.1 3.7 shard_map.72
  (41 shorter events, 1.0 us)
Async XLA Ops:
  238.0 6.8 %copy-start.3 = (s32[128]{0:T(128)S(1)}, s32[128]{0:T(128)}, u32[]{:S(2)}) copy-start(s32[128]{0:T(128)} %param.8) | copy-start | bytes 1540
  238.1 8.3 %copy-start.2 = (s32[128,23]{0,1:T(8,128)S(1)}, s32[128,23]{0,1:T(8,128)}, u32[]{:S(2)}) copy-start(s32[128,23]{0,1:T(8,128)} %param.9) | copy-start | bytes 35332
  238.1 205.1 %all-to-all-start = ((bf16[16,224,1280]{2,1,0:T(8,128)(2,1)}), bf16[16,224,1280]{2,1,0:T(8,128)(2,1)}, u32[]{:S(2)}, u32[]{:S(2)}) async-start(bf16[16,224,1280]{2,1,0:T(8,128)(2,1)} %get-tuple-element.8), calls=%async_computation | async-start | bytes 18350080 | tf_op jit(solution)/shard_map/all_to_all | solution.py:357
  443.2 35.5 %all-to-all-start.3 = ((bf16[16,32,1280]{2,1,0:T(8,128)(2,1)}), bf16[16,32,1280]{2,1,0:T(8,128)(2,1)S(1)}, u32[]{:S(2)}, u32[]{:S(2)}) async-start(bf16[16,32,1280]{2,1,0:T(8,128)(2,1)} %get-tuple-element.11), calls=%async_computation.3 | async-start | bytes 2621440 | tf_op jit(solution)/shard_map/all_to_all | solution.py:359
  478.6 8.9 %copy-start = (bf16[16,32,1280]{2,1,0:T(8,128)(2,1)}, bf16[16,32,1280]{2,1,0:T(8,128)(2,1)S(1)}, u32[]{:S(2)}) copy-start(bf16[16,32,1280]{2,1,0:T(8,128)(2,1)S(1)} %all-to-all-done.3) | copy-start | bytes 3932164
  478.6 35.4 %all-to-all-start.1 = ((bf16[16,32,1280]{2,1,0:T(8,128)(2,1)}), bf16[16,32,1280]{2,1,0:T(8,128)(2,1)S(1)}, u32[]{:S(2)}, u32[]{:S(2)}) async-start(bf16[16,32,1280]{2,1,0:T(8,128)(2,1)} %get-tuple-element.9), calls=%async_computation.1 | async-start | bytes 2621440 | tf_op jit(solution)/shard_map/all_to_all | solution.py:359
  514.1 1.1 copy-start.1
